TPU v7x, 1024 devices: a whole 4x4x32 slice. The times are simulated.
1024 devices in a mesh: ctx: 64 (over x, y, z_hi, core), fsdp: 16 (over z_lo).
Axes of the slice: x: 4, y: 4, z: 32 (z_hi: 2, z_lo: 16; z = z_hi * 16 + z_lo), core: 2. Of those that a mesh axis runs over, the one named last changes fastest.
Arguments:
- hidden: bfloat16 [2, 16, 4096, 3584], P(None, 'fsdp', 'ctx'), may hold values from -6 to 6
- queries: bfloat16 [2, 16, 4096, 1792], P(None, 'fsdp', 'ctx'), may hold values from -180 to 180
- kv_panel: bfloat16 [2, 3584, 256], P(None, 'fsdp'), may hold values from -0.09375 to 0.09375
- layout: int32 [16, 64], P('fsdp'), may hold values from 0 to 63, each once within a row
Outputs:
- attended: bfloat16 [2, 16, 4096, 1792], P(None, 'fsdp', 'ctx')
Inputs may be any that keep to these rules, and one draw needn't show every extreme that they name: `layout`: each row names every block number of a sequence once.
All inputs are finite; a program needn't handle non-finite values.
Results may differ from a plain program's by a relative error of at most 0.02.
The roundings to bfloat16 on the way count: a program that leaves them out, or rounds other values in their place, can miss the bound.
Values may be sent and summed in bfloat16 or wider, within the bound.
No kernel may reach another device: no remote copies, remote signals or barrier semaphores. Data moves between devices by JAX's collectives and lax.ppermute only.
A program may use at most 32 MiB of HBM per device.

v0:
```python
import math

import jax
import jax.numpy as jnp
from jax import lax
from jax.sharding import Mesh
from jax.sharding import PartitionSpec as P

NEGATIVE = -1e30
CTX = ("x", "y", "zh", "core")


def rotate_keys(vectors_in, positions, head_dim):
    half_dim = head_dim // 2
    inverse = 1000000.0 ** (-(jnp.arange(half_dim, dtype=jnp.float32) * 2.0 / head_dim))
    angles = positions.astype(jnp.float32)[..., None] * inverse
    cosine = jnp.cos(angles)
    sine_part = jnp.sin(angles)
    first_half = vectors_in[..., :half_dim]
    second_half = vectors_in[..., half_dim:]
    return jnp.concatenate(
        [
            first_half * cosine - second_half * sine_part,
            second_half * cosine + first_half * sine_part,
        ],
        axis=-1,
    )


def absorb(fold_carry, query_rows, key_part, value_part, allowed, score_scale):
    running, denominator, numerator = fold_carry
    scores = (
        jnp.einsum("tpd,ud->ptu", query_rows, key_part, preferred_element_type=jnp.float32)
        * score_scale
    )
    allowed_all = allowed[None]
    scores = jnp.where(allowed_all, scores, NEGATIVE)
    highest = jnp.maximum(running, jnp.max(scores, axis=-1))
    factor = jnp.exp(running - highest)
    weights = jnp.where(allowed_all, jnp.exp(scores - highest[..., None]), 0.0)
    denominator = denominator * factor + jnp.sum(weights, axis=-1)
    numerator = numerator * factor[..., None] + jnp.einsum(
        "ptu,ud->ptd",
        weights.astype(jnp.bfloat16),
        value_part,
        preferred_element_type=jnp.float32,
    )
    return (highest, denominator, numerator)


def absorb_tiled(fold_carry, query_rows, key_part, value_part, allowed, score_scale):
    key_count = key_part.shape[0]
    tile_width = math.gcd(key_count, 512)

    def one_tile(tile_index, inner):
        tile_start = tile_index * tile_width
        return absorb(
            inner,
            query_rows,
            lax.dynamic_slice_in_dim(key_part, tile_start, tile_width, 0),
            lax.dynamic_slice_in_dim(value_part, tile_start, tile_width, 0),
            lax.dynamic_slice_in_dim(allowed, tile_start, tile_width, 1),
            score_scale,
        )

    return lax.fori_loop(0, key_count // tile_width, one_tile, fold_carry)


def empty_state(blocks, group_size, rows_all, head_dim):
    return (
        jnp.full((blocks, group_size, rows_all), NEGATIVE, jnp.float32),
        jnp.zeros((blocks, group_size, rows_all), jnp.float32),
        jnp.zeros((blocks, group_size, rows_all, head_dim), jnp.float32),
    )


def absorb_chunk(fold_carry, query_rows, chunk, key_blocks, row_limit, score_scale):
    head_dim = query_rows.shape[-1]
    block_len = chunk.shape[-2]
    chunk = chunk.reshape(-1, 2 * head_dim)
    key_block = jnp.repeat(key_blocks.reshape(-1), block_len)
    allowed = key_block[None, None, :] < row_limit[:, :, None]
    return jax.vmap(absorb, in_axes=(0, 0, None, None, 0, None))(
        fold_carry, query_rows, chunk[:, :head_dim], chunk[:, head_dim:], allowed, score_scale
    )


def merge(first, second):
    high_a, den_a, num_a = first
    high_b, den_b, num_b = second
    highest = jnp.maximum(high_a, high_b)
    factor_a = jnp.exp(high_a - highest)
    factor_b = jnp.exp(high_b - highest)
    return (
        highest,
        den_a * factor_a + den_b * factor_b,
        num_a * factor_a[..., None] + num_b * factor_b[..., None],
    )


def swap(value, axis):
    return lax.ppermute(value, axis, [(0, 1), (1, 0)])


def ring4(value, axis):
    size = 4
    forward = [(i, (i + 1) % size) for i in range(size)]
    backward = [(i, (i - 1) % size) for i in range(size)]
    from_left = lax.ppermute(value, axis, forward)
    from_right = lax.ppermute(value, axis, backward)
    from_left2 = lax.ppermute(from_left, axis, forward)
    return jnp.stack([value, from_left, from_left2, from_right])


RING_SHIFT = (0, -1, -2, 1)


def local(hidden, queries, kv_panel, layout):
    block_len = hidden.shape[2]
    model_width = hidden.shape[3]
    heads_kv = kv_panel.shape[0]
    chunk_rows = kv_panel.shape[1]
    head_dim = kv_panel.shape[2] // 2
    group_size = queries.shape[3] // (heads_kv * head_dim)
    group_width = group_size * head_dim
    score_scale = head_dim ** (-0.5)
    n_chunks = model_width // chunk_rows
    x = lax.axis_index("x")
    y = lax.axis_index("y")
    zh = lax.axis_index("zh")
    core = lax.axis_index("core")
    fsdp = lax.axis_index("fsdp")
    ctx = ((x * 4 + y) * 2 + zh) * 2 + core
    block_table = layout[0]

    z_size = 2 * n_chunks
    forward = [(z, (z + 1) % z_size) for z in range(z_size)]
    backward = [(z, (z - 1) % z_size) for z in range(z_size)]
    mine = lax.dynamic_index_in_dim(kv_panel, core, 0, keepdims=False)
    panel = jnp.zeros((n_chunks,) + mine.shape, mine.dtype)
    panel = lax.dynamic_update_index_in_dim(panel, mine, fsdp, 0)
    going_up = mine
    going_down = mine
    for step in range(1, n_chunks // 2 + 1):
        going_up = lax.ppermute(going_up, ("zh", "fsdp"), forward)
        panel = lax.dynamic_update_index_in_dim(panel, going_up, (fsdp - step) % n_chunks, 0)
        if step < n_chunks // 2:
            going_down = lax.ppermute(going_down, ("zh", "fsdp"), backward)
            panel = lax.dynamic_update_index_in_dim(
                panel, going_down, (fsdp + step) % n_chunks, 0
            )
    panel = panel.reshape(model_width, 2 * head_dim)

    own_rows = hidden.reshape(2, block_len, model_width)
    token_rows = jnp.stack([own_rows, swap(own_rows, "core")])
    own_queries = queries.reshape(2, block_len, heads_kv, group_width)
    query_mine = lax.dynamic_index_in_dim(own_queries, core, 2, keepdims=False)
    query_other = lax.dynamic_index_in_dim(own_queries, 1 - core, 2, keepdims=False)
    query_blocks = jnp.stack([query_mine, swap(query_other, "core")])
    ctx_blocks = jnp.stack([ctx, ctx + 1 - 2 * core])
    own_blocks = block_table[ctx_blocks]

    projected = jnp.einsum(
        "bctd,de->bcte", token_rows, panel, preferred_element_type=jnp.float32
    )
    positions = own_blocks[:, None] * block_len + jnp.arange(block_len, dtype=jnp.int32)
    key_rows = rotate_keys(projected[..., :head_dim], positions[:, None, :], head_dim).astype(
        jnp.bfloat16
    )
    value_rows = projected[..., head_dim:].astype(jnp.bfloat16)

    clean = jnp.concatenate([key_rows[:, 0], value_rows[:, 0]], axis=-1)
    rows_all = 2 * block_len
    query_rows = query_blocks.reshape(2, rows_all, group_size, head_dim)
    row_limit = own_blocks[:, None] + jnp.concatenate(
        [jnp.ones((block_len,), jnp.int32), jnp.zeros((block_len,), jnp.int32)]
    )[None, :]
    shifts = jnp.array(RING_SHIFT, jnp.int32)
    src_x = (x + shifts) % 4
    src_y = (y + shifts) % 4
    src_zh = (zh + jnp.arange(2)) % 2
    src_core = (core + jnp.arange(2)) % 2
    src = (
        (src_x[None, None, :, None] * 4 + src_y[None, :, None, None]) * 2
        + src_zh[:, None, None, None]
    ) * 2 + src_core
    every_block = block_table[src.reshape(-1)].reshape(2, 4, 4, 2)

    def chain(rows, side):
        blocks = every_block[side]
        fold_carry = empty_state(2, group_size, rows_all, head_dim)
        fold_carry = absorb_chunk(
            fold_carry, query_rows, rows, blocks[0, 0], row_limit, score_scale
        )
        along_x = ring4(rows, "x")
        fold_carry = absorb_chunk(
            fold_carry, query_rows, along_x[1::2], blocks[0, 1::2], row_limit, score_scale
        )
        fold_carry = absorb_chunk(
            fold_carry, query_rows, along_x[2], blocks[0, 2], row_limit, score_scale
        )
        along_y = ring4(along_x, "y")
        fold_carry = absorb_chunk(
            fold_carry, query_rows, along_y[1::2], blocks[1::2], row_limit, score_scale
        )
        fold_carry = absorb_chunk(
            fold_carry, query_rows, along_y[2], blocks[2], row_limit, score_scale
        )
        return fold_carry

    noisy_ok = jnp.broadcast_to((jnp.arange(rows_all) >= block_len)[:, None], (rows_all, block_len))
    noisy_state = jax.vmap(absorb, in_axes=(0, 0, 0, 0, None, None))(
        empty_state(2, group_size, rows_all, head_dim),
        query_rows, key_rows[:, 1], value_rows[:, 1], noisy_ok, score_scale,
    )
    near = chain(clean, 0)
    far = chain(swap(clean, "zh"), 1)
    highest, denominator, numerator = merge(merge(noisy_state, near), far)
    attended = jnp.transpose(numerator / denominator[..., None], (0, 2, 1, 3))
    attended = attended.astype(jnp.bfloat16).reshape(2, 2, block_len, group_width)
    returned = swap(attended[1], "core")
    first = jnp.where(core == 0, attended[0], returned)
    second = jnp.where(core == 0, returned, attended[0])
    result = jnp.concatenate([first, second], axis=-1)
    return result.reshape(2, 1, block_len, heads_kv * group_width)


def solution(mesh):
    axis_sizes = dict(zip(mesh.axis_names, mesh.devices.shape))
    assert axis_sizes["ctx"] == 64
    fine = Mesh(mesh.devices.reshape(4, 4, 2, 2, axis_sizes["fsdp"]), CTX + ("fsdp",))
    return jax.shard_map(
        local,
        mesh=fine,
        in_specs=(
            P(None, "fsdp", CTX, None),
            P(None, "fsdp", CTX, None),
            P(None, "fsdp", None),
            P("fsdp", None),
        ),
        out_specs=P(None, "fsdp", CTX, None),
        check_vma=False,
    )
```

profile of v0, /device:TPU:1, one launch (start us, length us, event | category | flops | bytes accessed | tf_op | source)
XLA Modules:
  0.0 197.2 jit_solution(16367661253474790934)
XLA Ops:
  1.6 4.5 %collective-permute-start.1 = (bf16[224,256]{1,0:T(8,128)(2,1)}, bf16[224,256]{1,0:T(8,128)(2,1)}, u32[]{:S(2)}, u32[]{:S(2)}) collective-permute-start(bf16[224,256]{1,0:T(8,128)(2,1)} %get-tuple-element.35), channel_id=1, source_target_pairs={{0,1},{1,2},{2,3},{3,4},{4,5},{5,6},{6,7},{7,8},{8,9},{9,10},{10,1... | collective-permute-start | bytes 344072 | tf_op jit(solution)/shard_map/ppermute | solution.py:145
  6.1 16.8 %collective-permute-start.2 = (bf16[224,256]{1,0:T(8,128)(2,1)}, bf16[224,256]{1,0:T(8,128)(2,1)}, u32[]{:S(2)}, u32[]{:S(2)}) collective-permute-start(bf16[224,256]{1,0:T(8,128)(2,1)} %get-tuple-element.35), channel_id=1, source_target_pairs={{0,47},{1,0},{2,1},{3,2},{4,3},{5,4},{6,5},{7,6},{8,7},{9,8},{10,9... | collective-permute-start | bytes 344072 | tf_op jit(solution)/shard_map/ppermute | solution.py:148
  25.0 2.9 %collective-permute-start.16 = (bf16[2,64,896]{2,1,0:T(8,128)(2,1)S(1)}, bf16[2,64,896]{2,1,0:T(8,128)(2,1)}, u32[]{:S(2)}, u32[]{:S(2)}) collective-permute-start(bf16[2,64,896]{2,1,0:T(8,128)(2,1)S(1)} %bitcast.647), channel_id=1, source_target_pairs={{0,16},{16,0},{1,17},{17,1},{2,18},{18,2},{3,19},{19,3},{4,20},{20... | collective-permute-start | bytes 688136 | tf_op jit(solution)/shard_map/ppermute | solution.py:102
  27.8 1.9 collective-permute-start
  37.5 1.9 collective-permute-start.3
  39.4 4.6 %collective-permute-start.4 = (bf16[224,256]{1,0:T(8,128)(2,1)}, bf16[224,256]{1,0:T(8,128)(2,1)}, u32[]{:S(2)}, u32[]{:S(2)}) collective-permute-start(bf16[224,256]{1,0:T(8,128)(2,1)} %collective-permute-done.2), channel_id=1, source_target_pairs={{0,47},{1,0},{2,1},{3,2},{4,3},{5,4},{6,5},{7,6},{8,7},{9,8},{10,9... | collective-permute-start | bytes 344072 | tf_op jit(solution)/shard_map/ppermute | solution.py:148
  49.1 4.6 %collective-permute-start.6 = (bf16[224,256]{1,0:T(8,128)(2,1)}, bf16[224,256]{1,0:T(8,128)(2,1)S(1)}, u32[]{:S(2)}, u32[]{:S(2)}) collective-permute-start(bf16[224,256]{1,0:T(8,128)(2,1)} %collective-permute-done.4), channel_id=1, source_target_pairs={{0,47},{1,0},{2,1},{3,2},{4,3},{5,4},{6,5},{7,6},{8,7},{9,8},{10,9... | collective-permute-start | bytes 344072 | tf_op jit(solution)/shard_map/ppermute | solution.py:148
  55.5 1.9 collective-permute-start.7
  57.4 4.6 %collective-permute-start.8 = (bf16[224,256]{1,0:T(8,128)(2,1)S(1)}, bf16[224,256]{1,0:T(8,128)(2,1)S(1)}, u32[]{:S(2)}, u32[]{:S(2)}) collective-permute-start(bf16[224,256]{1,0:T(8,128)(2,1)S(1)} %collective-permute-done.6), channel_id=1, source_target_pairs={{0,47},{1,0},{2,1},{3,2},{4,3},{5,4},{6,5},{7,6},{8,7},{9,8},{10,9... | collective-permute-start | bytes 344072 | tf_op jit(solution)/shard_map/ppermute | solution.py:148
  64.1 4.6 %collective-permute-start.10 = (bf16[224,256]{1,0:T(8,128)(2,1)S(1)}, bf16[224,256]{1,0:T(8,128)(2,1)S(1)}, u32[]{:S(2)}, u32[]{:S(2)}) collective-permute-start(bf16[224,256]{1,0:T(8,128)(2,1)S(1)} %collective-permute-done.8), channel_id=1, source_target_pairs={{0,47},{1,0},{2,1},{3,2},{4,3},{5,4},{6,5},{7,6},{8,7},{9,8},{10,9... | collective-permute-start | bytes 344072 | tf_op jit(solution)/shard_map/ppermute | solution.py:148
  70.9 4.6 %collective-permute-start.12 = (bf16[224,256]{1,0:T(8,128)(2,1)S(1)}, bf16[224,256]{1,0:T(8,128)(2,1)S(1)}, u32[]{:S(2)}, u32[]{:S(2)}) collective-permute-start(bf16[224,256]{1,0:T(8,128)(2,1)S(1)} %collective-permute-done.10), channel_id=1, source_target_pairs={{0,47},{1,0},{2,1},{3,2},{4,3},{5,4},{6,5},{7,6},{8,7},{9,8},{10,9... | collective-permute-start | bytes 344072 | tf_op jit(solution)/shard_map/ppermute | solution.py:148
  77.6 4.6 %collective-permute-start.14 = (bf16[224,256]{1,0:T(8,128)(2,1)S(1)}, bf16[224,256]{1,0:T(8,128)(2,1)S(1)}, u32[]{:S(2)}, u32[]{:S(2)}) collective-permute-start(bf16[224,256]{1,0:T(8,128)(2,1)S(1)} %collective-permute-done.12), channel_id=1, source_target_pairs={{0,47},{1,0},{2,1},{3,2},{4,3},{5,4},{6,5},{7,6},{8,7},{9,8},{10,9... | collective-permute-start | bytes 344072 | tf_op jit(solution)/shard_map/ppermute | solution.py:148
  84.4 4.8 %collective-permute-done.15 = bf16[224,256]{1,0:T(8,128)(2,1)S(1)} collective-permute-done((bf16[224,256]{1,0:T(8,128)(2,1)S(1)}, bf16[224,256]{1,0:T(8,128)(2,1)S(1)}, u32[]{:S(2)}, u32[]{:S(2)}) %collective-permute-start.15) | collective-permute-done | bytes 114720 | tf_op jit(solution)/shard_map/ppermute | solution.py:145
  89.2 2.1 %fusion.205 = (bf16[2,2,64,256]{3,2,1,0:T(8,128)(2,1)S(1)}, f32[2,2,64,256]{3,2,1,0:T(8,128)S(1)}) fusion(bf16[3584,256,1,1]{1,0,3,2:T(8,128)(2,1)S(1)} %bitcast.617, bf16[1,2,64,3584]{3,2,1,0:T(8,128)(2,1)} %bitcast.2, bf16[1,2,64,3584]{3,2,1,0:T(8,128)(2,1)} %bitcast), kind=kOutput, calls=%fused_computation.345 | convolution fusion | flops 470745088 | bytes 4063232 | tf_op jit(solution)/shard_map/bctd,de->bcte/dot_general | solution.py:163
  91.7 15.1 %collective-permute-start.23 = (bf16[2,64,256]{2,1,0:T(8,128)(2,1)S(1)}, bf16[2,64,256]{2,1,0:T(8,128)(2,1)S(1)}, u32[]{:S(2)}, u32[]{:S(2)}) collective-permute-start(bf16[2,64,256]{2,1,0:T(8,128)(2,1)S(1)} %get-tuple-element.40), channel_id=1, source_target_pairs={{0,32},{32,0},{1,33},{33,1},{2,34},{34,2},{3,35},{35,3},{4,36},{36... | collective-permute-start | bytes 196616 | tf_op jit(solution)/shard_map/ppermute | solution.py:102
  106.8 4.4 %collective-permute-start.19 = (bf16[2,64,256]{2,1,0:T(8,128)(2,1)S(1)}, bf16[2,64,256]{2,1,0:T(8,128)(2,1)S(1)}, u32[]{:S(2)}, u32[]{:S(2)}) collective-permute-start(bf16[2,64,256]{2,1,0:T(8,128)(2,1)S(1)} %get-tuple-element.40), channel_id=1, source_target_pairs={{0,768},{256,0},{512,256},{768,512},{1,769},{257,1},{513,257},{769... | collective-permute-start | bytes 196616 | tf_op jit(solution)/shard_map/ppermute | solution.py:110
  111.2 1.9 collective-permute-start.17
  113.9 3.8 %collective-permute-done.17 = bf16[2,64,256]{2,1,0:T(8,128)(2,1)S(1)} collective-permute-done((bf16[2,64,256]{2,1,0:T(8,128)(2,1)S(1)}, bf16[2,64,256]{2,1,0:T(8,128)(2,1)S(1)}, u32[]{:S(2)}, u32[]{:S(2)}) %collective-permute-start.17) | collective-permute-done | bytes 65568 | tf_op jit(solution)/shard_map/ppermute | solution.py:109
  120.0 4.6 %collective-permute-start.26 = (bf16[2,64,256]{2,1,0:T(8,128)(2,1)S(1)}, bf16[2,64,256]{2,1,0:T(8,128)(2,1)S(1)}, u32[]{:S(2)}, u32[]{:S(2)}) collective-permute-start(bf16[2,64,256]{2,1,0:T(8,128)(2,1)S(1)} %collective-permute-done.23), channel_id=1, source_target_pairs={{0,768},{256,0},{512,256},{768,512},{1,769},{257,1},{513,257},{769... | collective-permute-start | bytes 196616 | tf_op jit(solution)/shard_map/ppermute | solution.py:110
  124.6 1.9 collective-permute-start.24
  126.6 3.2 %collective-permute-start.20 = (bf16[4,2,64,256]{3,2,1,0:T(8,128)(2,1)S(1)}, bf16[4,2,64,256]{3,2,1,0:T(8,128)(2,1)S(1)}, u32[]{:S(2)}, u32[]{:S(2)}) collective-permute-start(bf16[4,2,64,256]{3,2,1,0:T(8,128)(2,1)S(1)} %pad_maximum_fusion.2), channel_id=1, source_target_pairs={{0,64},{64,128},{128,192},{192,0},{1,65},{65,129},{129,193},{193,1... | collective-permute-start | bytes 786440 | tf_op jit(solution)/shard_map/ppermute | solution.py:109
  129.8 3.4 %collective-permute-start.22 = (bf16[4,2,64,256]{3,2,1,0:T(8,128)(2,1)S(1)}, bf16[4,2,64,256]{3,2,1,0:T(8,128)(2,1)S(1)}, u32[]{:S(2)}, u32[]{:S(2)}) collective-permute-start(bf16[4,2,64,256]{3,2,1,0:T(8,128)(2,1)S(1)} %pad_maximum_fusion.2), channel_id=1, source_target_pairs={{0,192},{64,0},{128,64},{192,128},{1,193},{65,1},{129,65},{193,129... | collective-permute-start | bytes 786440 | tf_op jit(solution)/shard_map/ppermute | solution.py:110
  133.6 1.9 collective-permute-start.25
  135.9 4.0 %collective-permute-done.25 = bf16[2,64,256]{2,1,0:T(8,128)(2,1)S(1)} collective-permute-done((bf16[2,64,256]{2,1,0:T(8,128)(2,1)S(1)}, bf16[2,64,256]{2,1,0:T(8,128)(2,1)S(1)}, u32[]{:S(2)}, u32[]{:S(2)}) %collective-permute-start.25) | collective-permute-done | bytes 65568 | tf_op jit(solution)/shard_map/ppermute | solution.py:111
  139.9 1.9 collective-permute-start.27
  141.8 4.6 %collective-permute-start.29 = (bf16[4,2,64,256]{3,2,1,0:T(8,128)(2,1)S(1)}, bf16[4,2,64,256]{3,2,1,0:T(8,128)(2,1)S(1)}, u32[]{:S(2)}, u32[]{:S(2)}) collective-permute-start(bf16[4,2,64,256]{3,2,1,0:T(8,128)(2,1)S(1)} %pad_maximum_fusion.3), channel_id=1, source_target_pairs={{0,192},{64,0},{128,64},{192,128},{1,193},{65,1},{129,65},{193,129... | collective-permute-start | bytes 786440 | tf_op jit(solution)/shard_map/ppermute | solution.py:110
  146.9 1.9 collective-permute-start.21
  149.1 2.2 %collective-permute-start.28 = (bf16[4,2,64,256]{3,2,1,0:T(8,128)(2,1)S(1)}, bf16[4,2,64,256]{3,2,1,0:T(8,128)(2,1)S(1)}, u32[]{:S(2)}, u32[]{:S(2)}) collective-permute-start(bf16[4,2,64,256]{3,2,1,0:T(8,128)(2,1)S(1)} %collective-permute-done.27), channel_id=1, source_target_pairs={{0,64},{64,128},{128,192},{192,0},{1,65},{65,129},{129,193},{193,1... | collective-permute-start | bytes 786440 | tf_op jit(solution)/shard_map/ppermute | solution.py:111
  151.3 3.9 %collective-permute-done.21 = bf16[4,2,64,256]{3,2,1,0:T(8,128)(2,1)S(1)} collective-permute-done((bf16[4,2,64,256]{3,2,1,0:T(8,128)(2,1)S(1)}, bf16[4,2,64,256]{3,2,1,0:T(8,128)(2,1)S(1)}, u32[]{:S(2)}, u32[]{:S(2)}) %collective-permute-start.21) | collective-permute-done | bytes 262176 | tf_op jit(solution)/shard_map/ppermute | solution.py:111
  161.2 2.2 %fusion.36 = f32[2,128,7,128]{3,1,2,0:T(8,128)S(1)} fusion(f32[1024,2,128,7]{2,0,3,1:T(8,128)S(1)} %get-tuple-element.86, f32[2,7,128]{2,1,0:T(8,128)S(1)} %get-tuple-element.18, pred[2,128,1024]{1,2,0:T(8,128)(4,1)S(1)} %get-tuple-element.61, bf16[1024,256]{1,0:T(8,128)(2,1)S(1)} %bitcast.619), kind=kOutput, calls=%fused_computation.46 | convolution fusion | flops 478937088 | bytes 8790016 | tf_op jit(solution)/shard_map/vmap(ptu,ud->ptd)/dot_general | solution.py:42
  169.5 2.2 %fusion.39 = f32[2,128,7,128]{3,1,2,0:T(8,128)S(1)} fusion(f32[1024,2,128,7]{2,0,3,1:T(8,128)S(1)} %get-tuple-element.76, f32[2,7,128]{2,1,0:T(8,128)S(1)} %get-tuple-element.22, pred[2,128,1024]{1,2,0:T(8,128)(4,1)S(1)} %get-tuple-element.62, bf16[1024,256]{1,0:T(8,128)(2,1)S(1)} %bitcast.621), kind=kOutput, calls=%fused_computation.47 | convolution fusion | flops 478937088 | bytes 8790016 | tf_op jit(solution)/shard_map/vmap(ptu,ud->ptd)/dot_general | solution.py:42
  180.6 14.6 %collective-permute-start.30 = (bf16[2,64,896]{2,1,0:T(8,128)(2,1)S(1)}, bf16[2,64,896]{2,1,0:T(8,128)(2,1)S(1)}, u32[]{:S(2)}, u32[]{:S(2)}) collective-permute-start(bf16[2,64,896]{2,1,0:T(8,128)(2,1)S(1)} %squeeze.63), channel_id=1, source_target_pairs={{0,16},{16,0},{1,17},{17,1},{2,18},{18,2},{3,19},{19,3},{4,20},{20... | collective-permute-start | bytes 688136 | tf_op jit(solution)/shard_map/ppermute | solution.py:102
  (189 shorter events, 53.9 us)
Async XLA Ops:
  0.0 30.4 %copy-start = (s32[1,64]{1,0:T(1,128)S(1)}, s32[1,64]{1,0:T(1,128)}, u32[]{:S(2)}) copy-start(s32[1,64]{1,0:T(1,128)} %param.8) | copy-start | bytes 772
  1.6 35.8 %collective-permute-start.1 = (bf16[224,256]{1,0:T(8,128)(2,1)}, bf16[224,256]{1,0:T(8,128)(2,1)}, u32[]{:S(2)}, u32[]{:S(2)}) collective-permute-start(bf16[224,256]{1,0:T(8,128)(2,1)} %get-tuple-element.35), channel_id=1, source_target_pairs={{0,1},{1,2},{2,3},{3,4},{4,5},{5,6},{6,7},{7,8},{8,9},{9,10},{10,1... | collective-permute-start | bytes 344072 | tf_op jit(solution)/shard_map/ppermute | solution.py:145
  6.1 33.3 %collective-permute-start.2 = (bf16[224,256]{1,0:T(8,128)(2,1)}, bf16[224,256]{1,0:T(8,128)(2,1)}, u32[]{:S(2)}, u32[]{:S(2)}) collective-permute-start(bf16[224,256]{1,0:T(8,128)(2,1)} %get-tuple-element.35), channel_id=1, source_target_pairs={{0,47},{1,0},{2,1},{3,2},{4,3},{5,4},{6,5},{7,6},{8,7},{9,8},{10,9... | collective-permute-start | bytes 344072 | tf_op jit(solution)/shard_map/ppermute | solution.py:148
  25.0 20.8 %collective-permute-start.16 = (bf16[2,64,896]{2,1,0:T(8,128)(2,1)S(1)}, bf16[2,64,896]{2,1,0:T(8,128)(2,1)}, u32[]{:S(2)}, u32[]{:S(2)}) collective-permute-start(bf16[2,64,896]{2,1,0:T(8,128)(2,1)S(1)} %bitcast.647), channel_id=1, source_target_pairs={{0,16},{16,0},{1,17},{17,1},{2,18},{18,2},{3,19},{19,3},{4,20},{20... | collective-permute-start | bytes 688136 | tf_op jit(solution)/shard_map/ppermute | solution.py:102
  27.8 61.4 %collective-permute-start = (bf16[2,64,3584]{2,1,0:T(8,128)(2,1)}, bf16[2,64,3584]{2,1,0:T(8,128)(2,1)}, u32[]{:S(2)}, u32[]{:S(2)}) collective-permute-start(bf16[2,64,3584]{2,1,0:T(8,128)(2,1)} %bitcast.1), channel_id=1, source_target_pairs={{0,16},{16,0},{1,17},{17,1},{2,18},{18,2},{3,19},{19,3},{4,20},{20... | collective-permute-start | bytes 2752520 | tf_op jit(solution)/shard_map/ppermute | solution.py:102
  37.5 9.6 %collective-permute-start.3 = (bf16[224,256]{1,0:T(8,128)(2,1)}, bf16[224,256]{1,0:T(8,128)(2,1)}, u32[]{:S(2)}, u32[]{:S(2)}) collective-permute-start(bf16[224,256]{1,0:T(8,128)(2,1)} %collective-permute-done.1), channel_id=1, source_target_pairs={{0,1},{1,2},{2,3},{3,4},{4,5},{5,6},{6,7},{7,8},{8,9},{9,10},{10,1... | collective-permute-start | bytes 344072 | tf_op jit(solution)/shard_map/ppermute | solution.py:145
  39.4 9.6 %collective-permute-start.4 = (bf16[224,256]{1,0:T(8,128)(2,1)}, bf16[224,256]{1,0:T(8,128)(2,1)}, u32[]{:S(2)}, u32[]{:S(2)}) collective-permute-start(bf16[224,256]{1,0:T(8,128)(2,1)} %collective-permute-done.2), channel_id=1, source_target_pairs={{0,47},{1,0},{2,1},{3,2},{4,3},{5,4},{6,5},{7,6},{8,7},{9,8},{10,9... | collective-permute-start | bytes 344072 | tf_op jit(solution)/shard_map/ppermute | solution.py:148
  47.1 8.4 %collective-permute-start.5 = (bf16[224,256]{1,0:T(8,128)(2,1)}, bf16[224,256]{1,0:T(8,128)(2,1)S(1)}, u32[]{:S(2)}, u32[]{:S(2)}) collective-permute-start(bf16[224,256]{1,0:T(8,128)(2,1)} %collective-permute-done.3), channel_id=1, source_target_pairs={{0,1},{1,2},{2,3},{3,4},{4,5},{5,6},{6,7},{7,8},{8,9},{9,10},{10,1... | collective-permute-start | bytes 344072 | tf_op jit(solution)/shard_map/ppermute | solution.py:145
  49.1 8.4 %collective-permute-start.6 = (bf16[224,256]{1,0:T(8,128)(2,1)}, bf16[224,256]{1,0:T(8,128)(2,1)S(1)}, u32[]{:S(2)}, u32[]{:S(2)}) collective-permute-start(bf16[224,256]{1,0:T(8,128)(2,1)} %collective-permute-done.4), channel_id=1, source_target_pairs={{0,47},{1,0},{2,1},{3,2},{4,3},{5,4},{6,5},{7,6},{8,7},{9,8},{10,9... | collective-permute-start | bytes 344072 | tf_op jit(solution)/shard_map/ppermute | solution.py:148
  55.5 6.7 %collective-permute-start.7 = (bf16[224,256]{1,0:T(8,128)(2,1)S(1)}, bf16[224,256]{1,0:T(8,128)(2,1)S(1)}, u32[]{:S(2)}, u32[]{:S(2)}) collective-permute-start(bf16[224,256]{1,0:T(8,128)(2,1)S(1)} %collective-permute-done.5), channel_id=1, source_target_pairs={{0,1},{1,2},{2,3},{3,4},{4,5},{5,6},{6,7},{7,8},{8,9},{9,10},{10,1... | collective-permute-start | bytes 344072 | tf_op jit(solution)/shard_map/ppermute | solution.py:145
  57.4 6.7 %collective-permute-start.8 = (bf16[224,256]{1,0:T(8,128)(2,1)S(1)}, bf16[224,256]{1,0:T(8,128)(2,1)S(1)}, u32[]{:S(2)}, u32[]{:S(2)}) collective-permute-start(bf16[224,256]{1,0:T(8,128)(2,1)S(1)} %collective-permute-done.6), channel_id=1, source_target_pairs={{0,47},{1,0},{2,1},{3,2},{4,3},{5,4},{6,5},{7,6},{8,7},{9,8},{10,9... | collective-permute-start | bytes 344072 | tf_op jit(solution)/shard_map/ppermute | solution.py:148
  62.2 6.7 %collective-permute-start.9 = (bf16[224,256]{1,0:T(8,128)(2,1)S(1)}, bf16[224,256]{1,0:T(8,128)(2,1)S(1)}, u32[]{:S(2)}, u32[]{:S(2)}) collective-permute-start(bf16[224,256]{1,0:T(8,128)(2,1)S(1)} %collective-permute-done.7), channel_id=1, source_target_pairs={{0,1},{1,2},{2,3},{3,4},{4,5},{5,6},{6,7},{7,8},{8,9},{9,10},{10,1... | collective-permute-start | bytes 344072 | tf_op jit(solution)/shard_map/ppermute | solution.py:145
  64.1 6.7 %collective-permute-start.10 = (bf16[224,256]{1,0:T(8,128)(2,1)S(1)}, bf16[224,256]{1,0:T(8,128)(2,1)S(1)}, u32[]{:S(2)}, u32[]{:S(2)}) collective-permute-start(bf16[224,256]{1,0:T(8,128)(2,1)S(1)} %collective-permute-done.8), channel_id=1, source_target_pairs={{0,47},{1,0},{2,1},{3,2},{4,3},{5,4},{6,5},{7,6},{8,7},{9,8},{10,9... | collective-permute-start | bytes 344072 | tf_op jit(solution)/shard_map/ppermute | solution.py:148
  69.0 6.7 %collective-permute-start.11 = (bf16[224,256]{1,0:T(8,128)(2,1)S(1)}, bf16[224,256]{1,0:T(8,128)(2,1)S(1)}, u32[]{:S(2)}, u32[]{:S(2)}) collective-permute-start(bf16[224,256]{1,0:T(8,128)(2,1)S(1)} %collective-permute-done.9), channel_id=1, source_target_pairs={{0,1},{1,2},{2,3},{3,4},{4,5},{5,6},{6,7},{7,8},{8,9},{9,10},{10,1... | collective-permute-start | bytes 344072 | tf_op jit(solution)/shard_map/ppermute | solution.py:145
  70.9 6.7 %collective-permute-start.12 = (bf16[224,256]{1,0:T(8,128)(2,1)S(1)}, bf16[224,256]{1,0:T(8,128)(2,1)S(1)}, u32[]{:S(2)}, u32[]{:S(2)}) collective-permute-start(bf16[224,256]{1,0:T(8,128)(2,1)S(1)} %collective-permute-done.10), channel_id=1, source_target_pairs={{0,47},{1,0},{2,1},{3,2},{4,3},{5,4},{6,5},{7,6},{8,7},{9,8},{10,9... | collective-permute-start | bytes 344072 | tf_op jit(solution)/shard_map/ppermute | solution.py:148
  75.7 6.7 %collective-permute-start.13 = (bf16[224,256]{1,0:T(8,128)(2,1)S(1)}, bf16[224,256]{1,0:T(8,128)(2,1)S(1)}, u32[]{:S(2)}, u32[]{:S(2)}) collective-permute-start(bf16[224,256]{1,0:T(8,128)(2,1)S(1)} %collective-permute-done.11), channel_id=1, source_target_pairs={{0,1},{1,2},{2,3},{3,4},{4,5},{5,6},{6,7},{7,8},{8,9},{9,10},{10,1... | collective-permute-start | bytes 344072 | tf_op jit(solution)/shard_map/ppermute | solution.py:145
  77.6 6.8 %collective-permute-start.14 = (bf16[224,256]{1,0:T(8,128)(2,1)S(1)}, bf16[224,256]{1,0:T(8,128)(2,1)S(1)}, u32[]{:S(2)}, u32[]{:S(2)}) collective-permute-start(bf16[224,256]{1,0:T(8,128)(2,1)S(1)} %collective-permute-done.12), channel_id=1, source_target_pairs={{0,47},{1,0},{2,1},{3,2},{4,3},{5,4},{6,5},{7,6},{8,7},{9,8},{10,9... | collective-permute-start | bytes 344072 | tf_op jit(solution)/shard_map/ppermute | solution.py:148
  82.4 6.8 %collective-permute-start.15 = (bf16[224,256]{1,0:T(8,128)(2,1)S(1)}, bf16[224,256]{1,0:T(8,128)(2,1)S(1)}, u32[]{:S(2)}, u32[]{:S(2)}) collective-permute-start(bf16[224,256]{1,0:T(8,128)(2,1)S(1)} %collective-permute-done.13), channel_id=1, source_target_pairs={{0,1},{1,2},{2,3},{3,4},{4,5},{5,6},{6,7},{7,8},{8,9},{9,10},{10,1... | collective-permute-start | bytes 344072 | tf_op jit(solution)/shard_map/ppermute | solution.py:145
  91.7 28.0 %collective-permute-start.23 = (bf16[2,64,256]{2,1,0:T(8,128)(2,1)S(1)}, bf16[2,64,256]{2,1,0:T(8,128)(2,1)S(1)}, u32[]{:S(2)}, u32[]{:S(2)}) collective-permute-start(bf16[2,64,256]{2,1,0:T(8,128)(2,1)S(1)} %get-tuple-element.40), channel_id=1, source_target_pairs={{0,32},{32,0},{1,33},{33,1},{2,34},{34,2},{3,35},{35,3},{4,36},{36... | collective-permute-start | bytes 196616 | tf_op jit(solution)/shard_map/ppermute | solution.py:102
  106.8 19.7 %collective-permute-start.19 = (bf16[2,64,256]{2,1,0:T(8,128)(2,1)S(1)}, bf16[2,64,256]{2,1,0:T(8,128)(2,1)S(1)}, u32[]{:S(2)}, u32[]{:S(2)}) collective-permute-start(bf16[2,64,256]{2,1,0:T(8,128)(2,1)S(1)} %get-tuple-element.40), channel_id=1, source_target_pairs={{0,768},{256,0},{512,256},{768,512},{1,769},{257,1},{513,257},{769... | collective-permute-start | bytes 196616 | tf_op jit(solution)/shard_map/ppermute | solution.py:110
  111.2 6.5 %collective-permute-start.17 = (bf16[2,64,256]{2,1,0:T(8,128)(2,1)S(1)}, bf16[2,64,256]{2,1,0:T(8,128)(2,1)S(1)}, u32[]{:S(2)}, u32[]{:S(2)}) collective-permute-start(bf16[2,64,256]{2,1,0:T(8,128)(2,1)S(1)} %get-tuple-element.40), channel_id=1, source_target_pairs={{0,256},{256,512},{512,768},{768,0},{1,257},{257,513},{513,769},{7... | collective-permute-start | bytes 196616 | tf_op jit(solution)/shard_map/ppermute | solution.py:109
  117.8 8.8 %collective-permute-start.18 = (bf16[2,64,256]{2,1,0:T(8,128)(2,1)S(1)}, bf16[2,64,256]{2,1,0:T(8,128)(2,1)S(1)}, u32[]{:S(2)}, u32[]{:S(2)}) collective-permute-start(bf16[2,64,256]{2,1,0:T(8,128)(2,1)S(1)} %collective-permute-done.17), channel_id=1, source_target_pairs={{0,256},{256,512},{512,768},{768,0},{1,257},{257,513},{513,769},{7... | collective-permute-start | bytes 196616 | tf_op jit(solution)/shard_map/ppermute | solution.py:111
  120.0 15.9 %collective-permute-start.26 = (bf16[2,64,256]{2,1,0:T(8,128)(2,1)S(1)}, bf16[2,64,256]{2,1,0:T(8,128)(2,1)S(1)}, u32[]{:S(2)}, u32[]{:S(2)}) collective-permute-start(bf16[2,64,256]{2,1,0:T(8,128)(2,1)S(1)} %collective-permute-done.23), channel_id=1, source_target_pairs={{0,768},{256,0},{512,256},{768,512},{1,769},{257,1},{513,257},{769... | collective-permute-start | bytes 196616 | tf_op jit(solution)/shard_map/ppermute | solution.py:110
  124.6 9.0 %collective-permute-start.24 = (bf16[2,64,256]{2,1,0:T(8,128)(2,1)S(1)}, bf16[2,64,256]{2,1,0:T(8,128)(2,1)S(1)}, u32[]{:S(2)}, u32[]{:S(2)}) collective-permute-start(bf16[2,64,256]{2,1,0:T(8,128)(2,1)S(1)} %collective-permute-done.23), channel_id=1, source_target_pairs={{0,256},{256,512},{512,768},{768,0},{1,257},{257,513},{513,769},{7... | collective-permute-start | bytes 196616 | tf_op jit(solution)/shard_map/ppermute | solution.py:109
  126.6 20.3 %collective-permute-start.20 = (bf16[4,2,64,256]{3,2,1,0:T(8,128)(2,1)S(1)}, bf16[4,2,64,256]{3,2,1,0:T(8,128)(2,1)S(1)}, u32[]{:S(2)}, u32[]{:S(2)}) collective-permute-start(bf16[4,2,64,256]{3,2,1,0:T(8,128)(2,1)S(1)} %pad_maximum_fusion.2), channel_id=1, source_target_pairs={{0,64},{64,128},{128,192},{192,0},{1,65},{65,129},{129,193},{193,1... | collective-permute-start | bytes 786440 | tf_op jit(solution)/shard_map/ppermute | solution.py:109
  129.8 21.5 %collective-permute-start.22 = (bf16[4,2,64,256]{3,2,1,0:T(8,128)(2,1)S(1)}, bf16[4,2,64,256]{3,2,1,0:T(8,128)(2,1)S(1)}, u32[]{:S(2)}, u32[]{:S(2)}) collective-permute-start(bf16[4,2,64,256]{3,2,1,0:T(8,128)(2,1)S(1)} %pad_maximum_fusion.2), channel_id=1, source_target_pairs={{0,192},{64,0},{128,64},{192,128},{1,193},{65,1},{129,65},{193,129... | collective-permute-start | bytes 786440 | tf_op jit(solution)/shard_map/ppermute | solution.py:110
  133.6 6.2 %collective-permute-start.25 = (bf16[2,64,256]{2,1,0:T(8,128)(2,1)S(1)}, bf16[2,64,256]{2,1,0:T(8,128)(2,1)S(1)}, u32[]{:S(2)}, u32[]{:S(2)}) collective-permute-start(bf16[2,64,256]{2,1,0:T(8,128)(2,1)S(1)} %collective-permute-done.24), channel_id=1, source_target_pairs={{0,256},{256,512},{512,768},{768,0},{1,257},{257,513},{513,769},{7... | collective-permute-start | bytes 196616 | tf_op jit(solution)/shard_map/ppermute | solution.py:111
  139.9 9.2 %collective-permute-start.27 = (bf16[4,2,64,256]{3,2,1,0:T(8,128)(2,1)S(1)}, bf16[4,2,64,256]{3,2,1,0:T(8,128)(2,1)S(1)}, u32[]{:S(2)}, u32[]{:S(2)}) collective-permute-start(bf16[4,2,64,256]{3,2,1,0:T(8,128)(2,1)S(1)} %pad_maximum_fusion.3), channel_id=1, source_target_pairs={{0,64},{64,128},{128,192},{192,0},{1,65},{65,129},{129,193},{193,1... | collective-permute-start | bytes 786440 | tf_op jit(solution)/shard_map/ppermute | solution.py:109
  141.8 23.4 %collective-permute-start.29 = (bf16[4,2,64,256]{3,2,1,0:T(8,128)(2,1)S(1)}, bf16[4,2,64,256]{3,2,1,0:T(8,128)(2,1)S(1)}, u32[]{:S(2)}, u32[]{:S(2)}) collective-permute-start(bf16[4,2,64,256]{3,2,1,0:T(8,128)(2,1)S(1)} %pad_maximum_fusion.3), channel_id=1, source_target_pairs={{0,192},{64,0},{128,64},{192,128},{1,193},{65,1},{129,65},{193,129... | collective-permute-start | bytes 786440 | tf_op jit(solution)/shard_map/ppermute | solution.py:110
  146.9 8.3 %collective-permute-start.21 = (bf16[4,2,64,256]{3,2,1,0:T(8,128)(2,1)S(1)}, bf16[4,2,64,256]{3,2,1,0:T(8,128)(2,1)S(1)}, u32[]{:S(2)}, u32[]{:S(2)}) collective-permute-start(bf16[4,2,64,256]{3,2,1,0:T(8,128)(2,1)S(1)} %collective-permute-done.20), channel_id=1, source_target_pairs={{0,64},{64,128},{128,192},{192,0},{1,65},{65,129},{129,193},{193,1... | collective-permute-start | bytes 786440 | tf_op jit(solution)/shard_map/ppermute | solution.py:111
  149.1 16.1 %collective-permute-start.28 = (bf16[4,2,64,256]{3,2,1,0:T(8,128)(2,1)S(1)}, bf16[4,2,64,256]{3,2,1,0:T(8,128)(2,1)S(1)}, u32[]{:S(2)}, u32[]{:S(2)}) collective-permute-start(bf16[4,2,64,256]{3,2,1,0:T(8,128)(2,1)S(1)} %collective-permute-done.27), channel_id=1, source_target_pairs={{0,64},{64,128},{128,192},{192,0},{1,65},{65,129},{129,193},{193,1... | collective-permute-start | bytes 786440 | tf_op jit(solution)/shard_map/ppermute | solution.py:111
  180.6 15.7 %collective-permute-start.30 = (bf16[2,64,896]{2,1,0:T(8,128)(2,1)S(1)}, bf16[2,64,896]{2,1,0:T(8,128)(2,1)S(1)}, u32[]{:S(2)}, u32[]{:S(2)}) collective-permute-start(bf16[2,64,896]{2,1,0:T(8,128)(2,1)S(1)} %squeeze.63), channel_id=1, source_target_pairs={{0,16},{16,0},{1,17},{17,1},{2,18},{18,2},{3,19},{19,3},{4,20},{20... | collective-permute-start | bytes 688136 | tf_op jit(solution)/shard_map/ppermute | solution.py:102
  (8 other events, 116.5 us)
where the time goes:
time: 198 us; the launch traced here: 197 us
  starting transfers between devices  130 us (66%)
  matrix products  22 us (11%)
  waiting for transfers between devices  17.8 us (9%)
  local copies, waits for them, and re-layouts  13.9 us (7%)
  other arithmetic  11.6 us (6%)
    ppermute x7, starting transfers between devices, local(): going_down = lax.ppermute(going_down, ('zh', 'fsdp'), backward)  44.2 us
    ppermute x4, starting transfers between devices, swap(): return lax.ppermute(value, axis, [(0, 1), (1, 0)])  34.5 us
    ppermute x8, starting transfers between devices, local(): going_up = lax.ppermute(going_up, ('zh', 'fsdp'), forward)  17.9 us
    ppermute x4, starting transfers between devices, ring4(): from_right = lax.ppermute(value, axis, backward)  16.9 us
    dot_general x11, matrix products, absorb(): jnp.einsum('ptu,ud->ptd', weights.astype(jnp.bfloat16), value_part, prefe...  13.5 us
    ppermute x4, starting transfers between devices, ring4(): from_left = lax.ppermute(value, axis, forward)  8.98 us
    ppermute x4, starting transfers between devices, ring4(): from_left2 = lax.ppermute(from_left, axis, forward)  7.93 us
    ppermute x4, waiting for transfers between devices, ring4(): from_left2 = lax.ppermute(from_left, axis, forward)  7.84 us
  transfers between devices with their start and end apart: 31, of which 9 were waited for; matrix products, arithmetic and copies ran while one was open for 14% of the time, Pallas kernels for 0%

commit v1 on v0

--- a/solution.py
+++ b/solution.py
@@ -100,19 +100,6 @@
 
 def swap(value, axis):
     return lax.ppermute(value, axis, [(0, 1), (1, 0)])
-
-
-def ring4(value, axis):
-    size = 4
-    forward = [(i, (i + 1) % size) for i in range(size)]
-    backward = [(i, (i - 1) % size) for i in range(size)]
-    from_left = lax.ppermute(value, axis, forward)
-    from_right = lax.ppermute(value, axis, backward)
-    from_left2 = lax.ppermute(from_left, axis, forward)
-    return jnp.stack([value, from_left, from_left2, from_right])
-
-
-RING_SHIFT = (0, -1, -2, 1)
 
 
 def local(hidden, queries, kv_panel, layout):
@@ -175,9 +162,8 @@
     row_limit = own_blocks[:, None] + jnp.concatenate(
         [jnp.ones((block_len,), jnp.int32), jnp.zeros((block_len,), jnp.int32)]
     )[None, :]
-    shifts = jnp.array(RING_SHIFT, jnp.int32)
-    src_x = (x + shifts) % 4
-    src_y = (y + shifts) % 4
+    src_x = jnp.arange(4)
+    src_y = jnp.arange(4)
     src_zh = (zh + jnp.arange(2)) % 2
     src_core = (core + jnp.arange(2)) % 2
     src = (
@@ -187,25 +173,14 @@
     every_block = block_table[src.reshape(-1)].reshape(2, 4, 4, 2)
 
     def chain(rows, side):
-        blocks = every_block[side]
+        blocks = jnp.swapaxes(every_block[side], 0, 1).reshape(-1, 4, 2)
+        spread = jnp.broadcast_to(rows[None], (16,) + rows.shape)
+        gathered = lax.all_to_all(spread, ("x", "y"), 0, 0, tiled=True).reshape(-1, 4, *rows.shape)
         fold_carry = empty_state(2, group_size, rows_all, head_dim)
-        fold_carry = absorb_chunk(
-            fold_carry, query_rows, rows, blocks[0, 0], row_limit, score_scale
-        )
-        along_x = ring4(rows, "x")
-        fold_carry = absorb_chunk(
-            fold_carry, query_rows, along_x[1::2], blocks[0, 1::2], row_limit, score_scale
-        )
-        fold_carry = absorb_chunk(
-            fold_carry, query_rows, along_x[2], blocks[0, 2], row_limit, score_scale
-        )
-        along_y = ring4(along_x, "y")
-        fold_carry = absorb_chunk(
-            fold_carry, query_rows, along_y[1::2], blocks[1::2], row_limit, score_scale
-        )
-        fold_carry = absorb_chunk(
-            fold_carry, query_rows, along_y[2], blocks[2], row_limit, score_scale
-        )
+        for part in range(gathered.shape[0]):
+            fold_carry = absorb_chunk(
+                fold_carry, query_rows, gathered[part], blocks[part], row_limit, score_scale
+            )
         return fold_carry
 
     noisy_ok = jnp.broadcast_to((jnp.arange(rows_all) >= block_len)[:, None], (rows_all, block_len))

time: 198 us -> 187 us (0.944)
  starting transfers between devices: 130 us -> 107 us
  waiting for transfers between devices: 17.8 us -> 26.1 us
  local copies, waits for them, and re-layouts: 13.9 us -> 19.3 us
    ppermute x12 -> x0, starting transfers between devices: 33.8 us -> none  [the longest x4 16.9 us: ring4(): from_right = lax.ppermute(value, axis, backward)]
    all_to_all x0 -> x2, starting transfers between devices: none -> 13.6 us  [chain(): lax.all_to_all(spread, ('x', 'y'), 0, 0, tiled=True)]
    ppermute x12 -> x0, waiting for transfers between devices: 11.7 us -> none  [the longest x4 7.84 us: ring4(): from_left2 = lax.ppermute(from_left, axis, forward)]
    ppermute x4, waiting for transfers between devices: 0.64 us -> 11.6 us  [swap(): return lax.ppermute(value, axis, [(0, 1), (1, 0)])]
    ppermute x8, waiting for transfers between devices: 5.51 us -> 11 us  [local(): going_up = lax.ppermute(going_up, ('zh', 'fsdp'), forward)]
    ppermute x4, starting transfers between devices: 34.5 us -> 30.1 us  [swap(): return lax.ppermute(value, axis, [(0, 1), (1, 0)])]
    unnamed x20 -> x74, local copies, waits for them, and re-layouts: 0.86 us -> 4.8 us
    all_to_all x0 -> x2, waiting for transfers between devices: none -> 3.51 us  [chain(): lax.all_to_all(spread, ('x', 'y'), 0, 0, tiled=True)]
  transfers between devices with their start and end apart: 31 -> 21, of which waited for: 9 -> 5; matrix products, arithmetic and copies ran while one was open for 14% -> 13% of each run, Pallas kernels for 0% -> 0%
where the time goes in v1:
time: 187 us; the launch traced here: 186 us
  starting transfers between devices  107 us (57%)
  waiting for transfers between devices  26.1 us (14%)
  matrix products  20.6 us (11%)
  local copies, waits for them, and re-layouts  19.3 us (10%)
  other arithmetic  11.9 us (6%)
    ppermute x7, starting transfers between devices, local(): going_down = lax.ppermute(going_down, ('zh', 'fsdp'), backward)  47.6 us
    ppermute x4, starting transfers between devices, swap(): return lax.ppermute(value, axis, [(0, 1), (1, 0)])  30.1 us
    ppermute x8, starting transfers between devices, local(): going_up = lax.ppermute(going_up, ('zh', 'fsdp'), forward)  15.3 us
    all_to_all x2, starting transfers between devices, chain(): lax.all_to_all(spread, ('x', 'y'), 0, 0, tiled=True)  13.6 us
    dot_general x9, matrix products, absorb(): jnp.einsum('ptu,ud->ptd', weights.astype(jnp.bfloat16), value_part, prefe...  12.5 us
    ppermute x4, waiting for transfers between devices, swap(): return lax.ppermute(value, axis, [(0, 1), (1, 0)])  11.6 us
    ppermute x8, waiting for transfers between devices, local(): going_up = lax.ppermute(going_up, ('zh', 'fsdp'), forward)  11 us
    reduce_sum x9, other arithmetic, absorb(): denominator = denominator * factor + jnp.sum(weights, axis=-1)  8.01 us
  transfers between devices with their start and end apart: 21, of which 5 were waited for; matrix products, arithmetic and copies ran while one was open for 13% of the time, Pallas kernels for 0%

profile of v1, /device:TPU:1, one launch (start us, length us, event | category | flops | bytes accessed | tf_op | source)
XLA Modules:
  0.0 186.0 jit_solution(3048908602964084494)
XLA Ops:
  0.2 1.6 dynamic-slice_bitcast_fusion
  1.7 19.2 %collective-permute-start.2 = (bf16[224,256]{1,0:T(8,128)(2,1)}, bf16[224,256]{1,0:T(8,128)(2,1)}, u32[]{:S(2)}, u32[]{:S(2)}) collective-permute-start(bf16[224,256]{1,0:T(8,128)(2,1)} %get-tuple-element.48), channel_id=1, source_target_pairs={{0,47},{1,0},{2,1},{3,2},{4,3},{5,4},{6,5},{7,6},{8,7},{9,8},{10,9... | collective-permute-start | bytes 344072 | tf_op jit(solution)/shard_map/ppermute | solution.py:135
  21.0 1.9 %collective-permute-start.1 = (bf16[224,256]{1,0:T(8,128)(2,1)}, bf16[224,256]{1,0:T(8,128)(2,1)S(1)}, u32[]{:S(2)}, u32[]{:S(2)}) collective-permute-start(bf16[224,256]{1,0:T(8,128)(2,1)} %get-tuple-element.48), channel_id=1, source_target_pairs={{0,1},{1,2},{2,3},{3,4},{4,5},{5,6},{6,7},{7,8},{8,9},{9,10},{10,1... | collective-permute-start | bytes 344072 | tf_op jit(solution)/shard_map/ppermute | solution.py:132
  24.0 1.9 %constant_dynamic-slice_fusion = (bf16[2,64,1,896]{3,2,1,0:T(2,128)(2,1)S(1)}, bf16[2,64,896]{2,1,0:T(8,128)(2,1)S(1)}) fusion(bf16[2,64,2,896]{3,2,1,0:T(2,128)(2,1)S(1)} %reshape.576, s32[]{:T(128)S(6)} %select_n.264, s32[]{:T(128)S(6)} %select_n.231), kind=kLoop, calls=%fused_computation.225 | loop fusion | bytes 917512 | tf_op jit(solution)/shard_map/jit(dynamic_index_in_dim)/dynamic_slice | solution.py:145
  26.6 2.9 %collective-permute-start.16 = (bf16[2,64,896]{2,1,0:T(8,128)(2,1)}, bf16[2,64,896]{2,1,0:T(8,128)(2,1)}, u32[]{:S(2)}, u32[]{:S(2)}) collective-permute-start(bf16[2,64,896]{2,1,0:T(8,128)(2,1)} %bitcast.554), channel_id=1, source_target_pairs={{0,16},{16,0},{1,17},{17,1},{2,18},{18,2},{3,19},{19,3},{4,20},{20... | collective-permute-start | bytes 688136 | tf_op jit(solution)/shard_map/ppermute | solution.py:102
  29.5 1.9 %collective-permute-start = (bf16[2,64,3584]{2,1,0:T(8,128)(2,1)}, bf16[2,64,3584]{2,1,0:T(8,128)(2,1)}, u32[]{:S(2)}, u32[]{:S(2)}) collective-permute-start(bf16[2,64,3584]{2,1,0:T(8,128)(2,1)} %bitcast.576), channel_id=1, source_target_pairs={{0,16},{16,0},{1,17},{17,1},{2,18},{18,2},{3,19},{19,3},{4,20},{20... | collective-permute-start | bytes 2752520 | tf_op jit(solution)/shard_map/ppermute | solution.py:102
  36.3 1.5 broadcast_compare_fusion.7
  38.1 4.9 %collective-permute-start.4 = (bf16[224,256]{1,0:T(8,128)(2,1)}, bf16[224,256]{1,0:T(8,128)(2,1)S(1)}, u32[]{:S(2)}, u32[]{:S(2)}) collective-permute-start(bf16[224,256]{1,0:T(8,128)(2,1)} %collective-permute-done.2), channel_id=1, source_target_pairs={{0,47},{1,0},{2,1},{3,2},{4,3},{5,4},{6,5},{7,6},{8,7},{9,8},{10,9... | collective-permute-start | bytes 344072 | tf_op jit(solution)/shard_map/ppermute | solution.py:135
  43.0 1.9 %collective-permute-start.3 = (bf16[224,256]{1,0:T(8,128)(2,1)S(1)}, bf16[224,256]{1,0:T(8,128)(2,1)S(1)}, u32[]{:S(2)}, u32[]{:S(2)}) collective-permute-start(bf16[224,256]{1,0:T(8,128)(2,1)S(1)} %collective-permute-done.1), channel_id=1, source_target_pairs={{0,1},{1,2},{2,3},{3,4},{4,5},{5,6},{6,7},{7,8},{8,9},{9,10},{10,1... | collective-permute-start | bytes 344072 | tf_op jit(solution)/shard_map/ppermute | solution.py:132
  45.9 4.6 %collective-permute-start.6 = (bf16[224,256]{1,0:T(8,128)(2,1)S(1)}, bf16[224,256]{1,0:T(8,128)(2,1)S(1)}, u32[]{:S(2)}, u32[]{:S(2)}) collective-permute-start(bf16[224,256]{1,0:T(8,128)(2,1)S(1)} %collective-permute-done.4), channel_id=1, source_target_pairs={{0,47},{1,0},{2,1},{3,2},{4,3},{5,4},{6,5},{7,6},{8,7},{9,8},{10,9... | collective-permute-start | bytes 344072 | tf_op jit(solution)/shard_map/ppermute | solution.py:135
  50.5 1.9 %collective-permute-start.5 = (bf16[224,256]{1,0:T(8,128)(2,1)S(1)}, bf16[224,256]{1,0:T(8,128)(2,1)S(1)}, u32[]{:S(2)}, u32[]{:S(2)}) collective-permute-start(bf16[224,256]{1,0:T(8,128)(2,1)S(1)} %collective-permute-done.3), channel_id=1, source_target_pairs={{0,1},{1,2},{2,3},{3,4},{4,5},{5,6},{6,7},{7,8},{8,9},{9,10},{10,1... | collective-permute-start | bytes 344072 | tf_op jit(solution)/shard_map/ppermute | solution.py:132
  52.5 4.7 %collective-permute-start.8 = (bf16[224,256]{1,0:T(8,128)(2,1)S(1)}, bf16[224,256]{1,0:T(8,128)(2,1)S(1)}, u32[]{:S(2)}, u32[]{:S(2)}) collective-permute-start(bf16[224,256]{1,0:T(8,128)(2,1)S(1)} %collective-permute-done.6), channel_id=1, source_target_pairs={{0,47},{1,0},{2,1},{3,2},{4,3},{5,4},{6,5},{7,6},{8,7},{9,8},{10,9... | collective-permute-start | bytes 344072 | tf_op jit(solution)/shard_map/ppermute | solution.py:135
  57.2 1.9 %collective-permute-start.7 = (bf16[224,256]{1,0:T(8,128)(2,1)S(1)}, bf16[224,256]{1,0:T(8,128)(2,1)S(1)}, u32[]{:S(2)}, u32[]{:S(2)}) collective-permute-start(bf16[224,256]{1,0:T(8,128)(2,1)S(1)} %collective-permute-done.5), channel_id=1, source_target_pairs={{0,1},{1,2},{2,3},{3,4},{4,5},{5,6},{6,7},{7,8},{8,9},{9,10},{10,1... | collective-permute-start | bytes 344072 | tf_op jit(solution)/shard_map/ppermute | solution.py:132
  59.2 4.7 %collective-permute-start.10 = (bf16[224,256]{1,0:T(8,128)(2,1)S(1)}, bf16[224,256]{1,0:T(8,128)(2,1)S(1)}, u32[]{:S(2)}, u32[]{:S(2)}) collective-permute-start(bf16[224,256]{1,0:T(8,128)(2,1)S(1)} %collective-permute-done.8), channel_id=1, source_target_pairs={{0,47},{1,0},{2,1},{3,2},{4,3},{5,4},{6,5},{7,6},{8,7},{9,8},{10,9... | collective-permute-start | bytes 344072 | tf_op jit(solution)/shard_map/ppermute | solution.py:135
  64.0 1.9 %collective-permute-start.9 = (bf16[224,256]{1,0:T(8,128)(2,1)S(1)}, bf16[224,256]{1,0:T(8,128)(2,1)S(1)}, u32[]{:S(2)}, u32[]{:S(2)}) collective-permute-start(bf16[224,256]{1,0:T(8,128)(2,1)S(1)} %collective-permute-done.7), channel_id=1, source_target_pairs={{0,1},{1,2},{2,3},{3,4},{4,5},{5,6},{6,7},{7,8},{8,9},{9,10},{10,1... | collective-permute-start | bytes 344072 | tf_op jit(solution)/shard_map/ppermute | solution.py:132
  66.0 4.7 %collective-permute-start.12 = (bf16[224,256]{1,0:T(8,128)(2,1)S(1)}, bf16[224,256]{1,0:T(8,128)(2,1)S(1)}, u32[]{:S(2)}, u32[]{:S(2)}) collective-permute-start(bf16[224,256]{1,0:T(8,128)(2,1)S(1)} %collective-permute-done.10), channel_id=1, source_target_pairs={{0,47},{1,0},{2,1},{3,2},{4,3},{5,4},{6,5},{7,6},{8,7},{9,8},{10,9... | collective-permute-start | bytes 344072 | tf_op jit(solution)/shard_map/ppermute | solution.py:135
  70.7 1.9 %collective-permute-start.11 = (bf16[224,256]{1,0:T(8,128)(2,1)S(1)}, bf16[224,256]{1,0:T(8,128)(2,1)S(1)}, u32[]{:S(2)}, u32[]{:S(2)}) collective-permute-start(bf16[224,256]{1,0:T(8,128)(2,1)S(1)} %collective-permute-done.9), channel_id=1, source_target_pairs={{0,1},{1,2},{2,3},{3,4},{4,5},{5,6},{6,7},{7,8},{8,9},{9,10},{10,1... | collective-permute-start | bytes 344072 | tf_op jit(solution)/shard_map/ppermute | solution.py:132
  72.7 4.7 %collective-permute-start.14 = (bf16[224,256]{1,0:T(8,128)(2,1)S(1)}, bf16[224,256]{1,0:T(8,128)(2,1)S(1)}, u32[]{:S(2)}, u32[]{:S(2)}) collective-permute-start(bf16[224,256]{1,0:T(8,128)(2,1)S(1)} %collective-permute-done.12), channel_id=1, source_target_pairs={{0,47},{1,0},{2,1},{3,2},{4,3},{5,4},{6,5},{7,6},{8,7},{9,8},{10,9... | collective-permute-start | bytes 344072 | tf_op jit(solution)/shard_map/ppermute | solution.py:135
  77.4 1.9 %collective-permute-start.13 = (bf16[224,256]{1,0:T(8,128)(2,1)S(1)}, bf16[224,256]{1,0:T(8,128)(2,1)S(1)}, u32[]{:S(2)}, u32[]{:S(2)}) collective-permute-start(bf16[224,256]{1,0:T(8,128)(2,1)S(1)} %collective-permute-done.11), channel_id=1, source_target_pairs={{0,1},{1,2},{2,3},{3,4},{4,5},{5,6},{6,7},{7,8},{8,9},{9,10},{10,1... | collective-permute-start | bytes 344072 | tf_op jit(solution)/shard_map/ppermute | solution.py:132
  79.4 4.8 %collective-permute-done.13 = bf16[224,256]{1,0:T(8,128)(2,1)S(1)} collective-permute-done((bf16[224,256]{1,0:T(8,128)(2,1)S(1)}, bf16[224,256]{1,0:T(8,128)(2,1)S(1)}, u32[]{:S(2)}, u32[]{:S(2)}) %collective-permute-start.13) | collective-permute-done | bytes 114720 | tf_op jit(solution)/shard_map/ppermute | solution.py:132
  84.2 1.9 %collective-permute-start.15 = (bf16[224,256]{1,0:T(8,128)(2,1)S(1)}, bf16[224,256]{1,0:T(8,128)(2,1)S(1)}, u32[]{:S(2)}, u32[]{:S(2)}) collective-permute-start(bf16[224,256]{1,0:T(8,128)(2,1)S(1)} %collective-permute-done.13), channel_id=1, source_target_pairs={{0,1},{1,2},{2,3},{3,4},{4,5},{5,6},{6,7},{7,8},{8,9},{9,10},{10,1... | collective-permute-start | bytes 344072 | tf_op jit(solution)/shard_map/ppermute | solution.py:132
  86.2 6.1 %collective-permute-done.15 = bf16[224,256]{1,0:T(8,128)(2,1)S(1)} collective-permute-done((bf16[224,256]{1,0:T(8,128)(2,1)S(1)}, bf16[224,256]{1,0:T(8,128)(2,1)S(1)}, u32[]{:S(2)}, u32[]{:S(2)}) %collective-permute-start.15) | collective-permute-done | bytes 114720 | tf_op jit(solution)/shard_map/ppermute | solution.py:132
  92.3 2.1 %fusion.219 = (bf16[2,2,64,256]{3,2,1,0:T(8,128)(2,1)S(1)}, f32[2,2,64,256]{3,2,1,0:T(8,128)S(1)}) fusion(bf16[3584,256,1,1]{1,0,3,2:T(8,128)(2,1)S(1)} %bitcast.557, bf16[1,2,64,3584]{3,2,1,0:T(8,128)(2,1)} %bitcast.2, bf16[1,2,64,3584]{3,2,1,0:T(8,128)(2,1)} %bitcast.577), kind=kOutput, calls=%fused_computation.295 | convolution fusion | flops 470745088 | bytes 4063232 | tf_op jit(solution)/shard_map/bctd,de->bcte/dot_general | solution.py:150
  96.2 6.8 %all-to-all-start = ((bf16[16,2,64,256]{3,2,1,0:T(8,128)(2,1)}), bf16[16,2,64,256]{3,2,1,0:T(8,128)(2,1)S(1)}, u32[]{:S(2)}, u32[]{:S(2)}) async-start(bf16[16,2,64,256]{3,2,1,0:T(8,128)(2,1)} %broadcast_in_dim.268), calls=%async_computation | async-start | bytes 2097152 | tf_op jit(solution)/shard_map/all_to_all | solution.py:178
  104.3 12.0 %collective-permute-start.17 = (bf16[2,64,256]{2,1,0:T(8,128)(2,1)S(1)}, bf16[2,64,256]{2,1,0:T(8,128)(2,1)S(1)}, u32[]{:S(2)}, u32[]{:S(2)}) collective-permute-start(bf16[2,64,256]{2,1,0:T(8,128)(2,1)S(1)} %pad_maximum_fusion), channel_id=1, source_target_pairs={{0,32},{32,0},{1,33},{33,1},{2,34},{34,2},{3,35},{35,3},{4,36},{36... | collective-permute-start | bytes 196616 | tf_op jit(solution)/shard_map/ppermute | solution.py:102
  117.4 10.9 %collective-permute-done.17 = bf16[2,64,256]{2,1,0:T(8,128)(2,1)S(1)} collective-permute-done((bf16[2,64,256]{2,1,0:T(8,128)(2,1)S(1)}, bf16[2,64,256]{2,1,0:T(8,128)(2,1)S(1)}, u32[]{:S(2)}, u32[]{:S(2)}) %collective-permute-start.17) | collective-permute-done | bytes 65568 | tf_op jit(solution)/shard_map/ppermute | solution.py:102
  129.4 6.8 %all-to-all-start.1 = ((bf16[16,2,64,256]{3,2,1,0:T(8,128)(2,1)}), bf16[16,2,64,256]{3,2,1,0:T(8,128)(2,1)S(1)}, u32[]{:S(2)}, u32[]{:S(2)}) async-start(bf16[16,2,64,256]{3,2,1,0:T(8,128)(2,1)} %broadcast_in_dim.279), calls=%async_computation.1 | async-start | bytes 2097152 | tf_op jit(solution)/shard_map/all_to_all | solution.py:178
  144.4 3.5 %all-to-all-done.1 = bf16[16,2,64,256]{3,2,1,0:T(8,128)(2,1)S(1)} async-done(((bf16[16,2,64,256]{3,2,1,0:T(8,128)(2,1)}), bf16[16,2,64,256]{3,2,1,0:T(8,128)(2,1)S(1)}, u32[]{:S(2)}, u32[]{:S(2)}) %all-to-all-start.1) | async-done | bytes 1048608 | tf_op jit(solution)/shard_map/all_to_all | solution.py:178
  154.8 1.4 fusion.103
  156.8 1.4 fusion.127
  168.3 1.9 %fusion.130 = bf16[2,128,7,128]{3,1,2,0:T(8,128)(2,1)S(1)} fusion(f32[2,128,7,128]{3,1,2,0:T(8,128)S(1)} %fusion.85, f32[2,128,7,128]{3,1,2,0:T(8,128)S(1)} %fusion.109, f32[2,128,7]{1,2,0:T(8,128)S(1)} %get-tuple-element.13, f32[2,128,7]{1,2,0:T(8,128)S(1)} %get-tuple-element.15, f32[2,128,7]{1,2,0:T(8,128)S(1)} %get-tuple-element.14, ...), kind=kOutput, calls=%fused_computation.93 | convolution fusion | flops 31309824 | bytes 2821248 | tf_op jit(solution)/shard_map/vmap(ptu,ud->ptd)/dot_general | solution.py:42
  170.8 13.3 %collective-permute-start.18 = (bf16[2,64,896]{2,1,0:T(8,128)(2,1)S(1)}, bf16[2,64,896]{2,1,0:T(8,128)(2,1)S(1)}, u32[]{:S(2)}, u32[]{:S(2)}) collective-permute-start(bf16[2,64,896]{2,1,0:T(8,128)(2,1)S(1)} %squeeze.47), channel_id=1, source_target_pairs={{0,16},{16,0},{1,17},{17,1},{2,18},{18,2},{3,19},{19,3},{4,20},{20... | collective-permute-start | bytes 688136 | tf_op jit(solution)/shard_map/ppermute | solution.py:102
  (203 shorter events, 40.7 us)
Async XLA Ops:
  0.0 31.8 %copy-start = (s32[1,64]{1,0:T(1,128)S(1)}, s32[1,64]{1,0:T(1,128)}, u32[]{:S(2)}) copy-start(s32[1,64]{1,0:T(1,128)} %param.7) | copy-start | bytes 772
  0.0 32.5 %copy-start.35 = (s32[128]{0:T(128)S(1)}, s32[128]{0:T(128)}, u32[]{:S(2)}) copy-start(s32[128]{0:T(128)} %constant.218.clone.1) | copy-start | bytes 1540
  1.7 36.4 %collective-permute-start.2 = (bf16[224,256]{1,0:T(8,128)(2,1)}, bf16[224,256]{1,0:T(8,128)(2,1)}, u32[]{:S(2)}, u32[]{:S(2)}) collective-permute-start(bf16[224,256]{1,0:T(8,128)(2,1)} %get-tuple-element.48), channel_id=1, source_target_pairs={{0,47},{1,0},{2,1},{3,2},{4,3},{5,4},{6,5},{7,6},{8,7},{9,8},{10,9... | collective-permute-start | bytes 344072 | tf_op jit(solution)/shard_map/ppermute | solution.py:135
  21.0 22.0 %collective-permute-start.1 = (bf16[224,256]{1,0:T(8,128)(2,1)}, bf16[224,256]{1,0:T(8,128)(2,1)S(1)}, u32[]{:S(2)}, u32[]{:S(2)}) collective-permute-start(bf16[224,256]{1,0:T(8,128)(2,1)} %get-tuple-element.48), channel_id=1, source_target_pairs={{0,1},{1,2},{2,3},{3,4},{4,5},{5,6},{6,7},{7,8},{8,9},{9,10},{10,1... | collective-permute-start | bytes 344072 | tf_op jit(solution)/shard_map/ppermute | solution.py:132
  26.6 76.4 %collective-permute-start.16 = (bf16[2,64,896]{2,1,0:T(8,128)(2,1)}, bf16[2,64,896]{2,1,0:T(8,128)(2,1)}, u32[]{:S(2)}, u32[]{:S(2)}) collective-permute-start(bf16[2,64,896]{2,1,0:T(8,128)(2,1)} %bitcast.554), channel_id=1, source_target_pairs={{0,16},{16,0},{1,17},{17,1},{2,18},{18,2},{3,19},{19,3},{4,20},{20... | collective-permute-start | bytes 688136 | tf_op jit(solution)/shard_map/ppermute | solution.py:102
  29.5 62.8 %collective-permute-start = (bf16[2,64,3584]{2,1,0:T(8,128)(2,1)}, bf16[2,64,3584]{2,1,0:T(8,128)(2,1)}, u32[]{:S(2)}, u32[]{:S(2)}) collective-permute-start(bf16[2,64,3584]{2,1,0:T(8,128)(2,1)} %bitcast.576), channel_id=1, source_target_pairs={{0,16},{16,0},{1,17},{17,1},{2,18},{18,2},{3,19},{19,3},{4,20},{20... | collective-permute-start | bytes 2752520 | tf_op jit(solution)/shard_map/ppermute | solution.py:102
  38.1 7.7 %collective-permute-start.4 = (bf16[224,256]{1,0:T(8,128)(2,1)}, bf16[224,256]{1,0:T(8,128)(2,1)S(1)}, u32[]{:S(2)}, u32[]{:S(2)}) collective-permute-start(bf16[224,256]{1,0:T(8,128)(2,1)} %collective-permute-done.2), channel_id=1, source_target_pairs={{0,47},{1,0},{2,1},{3,2},{4,3},{5,4},{6,5},{7,6},{8,7},{9,8},{10,9... | collective-permute-start | bytes 344072 | tf_op jit(solution)/shard_map/ppermute | solution.py:135
  43.0 7.5 %collective-permute-start.3 = (bf16[224,256]{1,0:T(8,128)(2,1)S(1)}, bf16[224,256]{1,0:T(8,128)(2,1)S(1)}, u32[]{:S(2)}, u32[]{:S(2)}) collective-permute-start(bf16[224,256]{1,0:T(8,128)(2,1)S(1)} %collective-permute-done.1), channel_id=1, source_target_pairs={{0,1},{1,2},{2,3},{3,4},{4,5},{5,6},{6,7},{7,8},{8,9},{9,10},{10,1... | collective-permute-start | bytes 344072 | tf_op jit(solution)/shard_map/ppermute | solution.py:132
  45.9 6.6 %collective-permute-start.6 = (bf16[224,256]{1,0:T(8,128)(2,1)S(1)}, bf16[224,256]{1,0:T(8,128)(2,1)S(1)}, u32[]{:S(2)}, u32[]{:S(2)}) collective-permute-start(bf16[224,256]{1,0:T(8,128)(2,1)S(1)} %collective-permute-done.4), channel_id=1, source_target_pairs={{0,47},{1,0},{2,1},{3,2},{4,3},{5,4},{6,5},{7,6},{8,7},{9,8},{10,9... | collective-permute-start | bytes 344072 | tf_op jit(solution)/shard_map/ppermute | solution.py:135
  50.5 6.7 %collective-permute-start.5 = (bf16[224,256]{1,0:T(8,128)(2,1)S(1)}, bf16[224,256]{1,0:T(8,128)(2,1)S(1)}, u32[]{:S(2)}, u32[]{:S(2)}) collective-permute-start(bf16[224,256]{1,0:T(8,128)(2,1)S(1)} %collective-permute-done.3), channel_id=1, source_target_pairs={{0,1},{1,2},{2,3},{3,4},{4,5},{5,6},{6,7},{7,8},{8,9},{9,10},{10,1... | collective-permute-start | bytes 344072 | tf_op jit(solution)/shard_map/ppermute | solution.py:132
  52.5 6.7 %collective-permute-start.8 = (bf16[224,256]{1,0:T(8,128)(2,1)S(1)}, bf16[224,256]{1,0:T(8,128)(2,1)S(1)}, u32[]{:S(2)}, u32[]{:S(2)}) collective-permute-start(bf16[224,256]{1,0:T(8,128)(2,1)S(1)} %collective-permute-done.6), channel_id=1, source_target_pairs={{0,47},{1,0},{2,1},{3,2},{4,3},{5,4},{6,5},{7,6},{8,7},{9,8},{10,9... | collective-permute-start | bytes 344072 | tf_op jit(solution)/shard_map/ppermute | solution.py:135
  57.2 6.7 %collective-permute-start.7 = (bf16[224,256]{1,0:T(8,128)(2,1)S(1)}, bf16[224,256]{1,0:T(8,128)(2,1)S(1)}, u32[]{:S(2)}, u32[]{:S(2)}) collective-permute-start(bf16[224,256]{1,0:T(8,128)(2,1)S(1)} %collective-permute-done.5), channel_id=1, source_target_pairs={{0,1},{1,2},{2,3},{3,4},{4,5},{5,6},{6,7},{7,8},{8,9},{9,10},{10,1... | collective-permute-start | bytes 344072 | tf_op jit(solution)/shard_map/ppermute | solution.py:132
  59.2 6.7 %collective-permute-start.10 = (bf16[224,256]{1,0:T(8,128)(2,1)S(1)}, bf16[224,256]{1,0:T(8,128)(2,1)S(1)}, u32[]{:S(2)}, u32[]{:S(2)}) collective-permute-start(bf16[224,256]{1,0:T(8,128)(2,1)S(1)} %collective-permute-done.8), channel_id=1, source_target_pairs={{0,47},{1,0},{2,1},{3,2},{4,3},{5,4},{6,5},{7,6},{8,7},{9,8},{10,9... | collective-permute-start | bytes 344072 | tf_op jit(solution)/shard_map/ppermute | solution.py:135
  64.0 6.7 %collective-permute-start.9 = (bf16[224,256]{1,0:T(8,128)(2,1)S(1)}, bf16[224,256]{1,0:T(8,128)(2,1)S(1)}, u32[]{:S(2)}, u32[]{:S(2)}) collective-permute-start(bf16[224,256]{1,0:T(8,128)(2,1)S(1)} %collective-permute-done.7), channel_id=1, source_target_pairs={{0,1},{1,2},{2,3},{3,4},{4,5},{5,6},{6,7},{7,8},{8,9},{9,10},{10,1... | collective-permute-start | bytes 344072 | tf_op jit(solution)/shard_map/ppermute | solution.py:132
  66.0 6.7 %collective-permute-start.12 = (bf16[224,256]{1,0:T(8,128)(2,1)S(1)}, bf16[224,256]{1,0:T(8,128)(2,1)S(1)}, u32[]{:S(2)}, u32[]{:S(2)}) collective-permute-start(bf16[224,256]{1,0:T(8,128)(2,1)S(1)} %collective-permute-done.10), channel_id=1, source_target_pairs={{0,47},{1,0},{2,1},{3,2},{4,3},{5,4},{6,5},{7,6},{8,7},{9,8},{10,9... | collective-permute-start | bytes 344072 | tf_op jit(solution)/shard_map/ppermute | solution.py:135
  70.7 6.7 %collective-permute-start.11 = (bf16[224,256]{1,0:T(8,128)(2,1)S(1)}, bf16[224,256]{1,0:T(8,128)(2,1)S(1)}, u32[]{:S(2)}, u32[]{:S(2)}) collective-permute-start(bf16[224,256]{1,0:T(8,128)(2,1)S(1)} %collective-permute-done.9), channel_id=1, source_target_pairs={{0,1},{1,2},{2,3},{3,4},{4,5},{5,6},{6,7},{7,8},{8,9},{9,10},{10,1... | collective-permute-start | bytes 344072 | tf_op jit(solution)/shard_map/ppermute | solution.py:132
  72.7 13.5 %collective-permute-start.14 = (bf16[224,256]{1,0:T(8,128)(2,1)S(1)}, bf16[224,256]{1,0:T(8,128)(2,1)S(1)}, u32[]{:S(2)}, u32[]{:S(2)}) collective-permute-start(bf16[224,256]{1,0:T(8,128)(2,1)S(1)} %collective-permute-done.12), channel_id=1, source_target_pairs={{0,47},{1,0},{2,1},{3,2},{4,3},{5,4},{6,5},{7,6},{8,7},{9,8},{10,9... | collective-permute-start | bytes 344072 | tf_op jit(solution)/shard_map/ppermute | solution.py:135
  77.4 6.8 %collective-permute-start.13 = (bf16[224,256]{1,0:T(8,128)(2,1)S(1)}, bf16[224,256]{1,0:T(8,128)(2,1)S(1)}, u32[]{:S(2)}, u32[]{:S(2)}) collective-permute-start(bf16[224,256]{1,0:T(8,128)(2,1)S(1)} %collective-permute-done.11), channel_id=1, source_target_pairs={{0,1},{1,2},{2,3},{3,4},{4,5},{5,6},{6,7},{7,8},{8,9},{9,10},{10,1... | collective-permute-start | bytes 344072 | tf_op jit(solution)/shard_map/ppermute | solution.py:132
  84.2 8.1 %collective-permute-start.15 = (bf16[224,256]{1,0:T(8,128)(2,1)S(1)}, bf16[224,256]{1,0:T(8,128)(2,1)S(1)}, u32[]{:S(2)}, u32[]{:S(2)}) collective-permute-start(bf16[224,256]{1,0:T(8,128)(2,1)S(1)} %collective-permute-done.13), channel_id=1, source_target_pairs={{0,1},{1,2},{2,3},{3,4},{4,5},{5,6},{6,7},{7,8},{8,9},{9,10},{10,1... | collective-permute-start | bytes 344072 | tf_op jit(solution)/shard_map/ppermute | solution.py:132
  96.2 32.1 %all-to-all-start = ((bf16[16,2,64,256]{3,2,1,0:T(8,128)(2,1)}), bf16[16,2,64,256]{3,2,1,0:T(8,128)(2,1)S(1)}, u32[]{:S(2)}, u32[]{:S(2)}) async-start(bf16[16,2,64,256]{3,2,1,0:T(8,128)(2,1)} %broadcast_in_dim.268), calls=%async_computation | async-start | bytes 2097152 | tf_op jit(solution)/shard_map/all_to_all | solution.py:178
  104.3 24.0 %collective-permute-start.17 = (bf16[2,64,256]{2,1,0:T(8,128)(2,1)S(1)}, bf16[2,64,256]{2,1,0:T(8,128)(2,1)S(1)}, u32[]{:S(2)}, u32[]{:S(2)}) collective-permute-start(bf16[2,64,256]{2,1,0:T(8,128)(2,1)S(1)} %pad_maximum_fusion), channel_id=1, source_target_pairs={{0,32},{32,0},{1,33},{33,1},{2,34},{34,2},{3,35},{35,3},{4,36},{36... | collective-permute-start | bytes 196616 | tf_op jit(solution)/shard_map/ppermute | solution.py:102
  116.7 12.8 %copy-start.23 = (f32[2,7,128]{2,1,0:T(8,128)}, f32[2,7,128]{2,1,0:T(8,128)S(1)}, u32[]{:S(2)}) copy-start(f32[2,7,128]{2,1,0:T(8,128)S(1)} %broadcast_maximum_fusion.2) | copy-start | bytes 21508
  129.4 18.4 %all-to-all-start.1 = ((bf16[16,2,64,256]{3,2,1,0:T(8,128)(2,1)}), bf16[16,2,64,256]{3,2,1,0:T(8,128)(2,1)S(1)}, u32[]{:S(2)}, u32[]{:S(2)}) async-start(bf16[16,2,64,256]{3,2,1,0:T(8,128)(2,1)} %broadcast_in_dim.279), calls=%async_computation.1 | async-start | bytes 2097152 | tf_op jit(solution)/shard_map/all_to_all | solution.py:178
  137.9 5.5 %copy-start.7 = (f32[512,2,128,7]{2,0,3,1:T(8,128)}, f32[512,2,128,7]{2,0,3,1:T(8,128)S(1)}, u32[]{:S(2)}) copy-start(f32[512,2,128,7]{2,0,3,1:T(8,128)S(1)} %get-tuple-element.86) | copy-start | bytes 11010052
  138.7 2.3 %copy-start.3 = (f32[512,2,128,7]{2,0,3,1:T(8,128)}, f32[512,2,128,7]{2,0,3,1:T(8,128)S(1)}, u32[]{:S(2)}) copy-start(f32[512,2,128,7]{2,0,3,1:T(8,128)S(1)} %get-tuple-element.82) | copy-start | bytes 11010052
  139.4 3.1 %copy-start.5 = (f32[512,2,128,7]{2,0,3,1:T(8,128)}, f32[512,2,128,7]{2,0,3,1:T(8,128)S(1)}, u32[]{:S(2)}) copy-start(f32[512,2,128,7]{2,0,3,1:T(8,128)S(1)} %get-tuple-element.84) | copy-start | bytes 11010052
  139.4 2.5 %copy-start.25 = (f32[2,7,128]{2,1,0:T(8,128)}, f32[2,7,128]{2,1,0:T(8,128)S(1)}, u32[]{:S(2)}) copy-start(f32[2,7,128]{2,1,0:T(8,128)S(1)} %get-tuple-element.22) | copy-start | bytes 21508
  139.4 2.5 %copy-start.27 = (f32[2,7,128]{2,1,0:T(8,128)}, f32[2,7,128]{2,1,0:T(8,128)S(1)}, u32[]{:S(2)}) copy-start(f32[2,7,128]{2,1,0:T(8,128)S(1)} %get-tuple-element.23) | copy-start | bytes 21508
  139.4 3.1 %copy-start.29 = (f32[2,7,128]{2,1,0:T(8,128)}, f32[2,7,128]{2,1,0:T(8,128)S(1)}, u32[]{:S(2)}) copy-start(f32[2,7,128]{2,1,0:T(8,128)S(1)} %get-tuple-element.24) | copy-start | bytes 21508
  139.4 4.0 %copy-start.31 = (f32[2,7,128]{2,1,0:T(8,128)}, f32[2,7,128]{2,1,0:T(8,128)S(1)}, u32[]{:S(2)}) copy-start(f32[2,7,128]{2,1,0:T(8,128)S(1)} %get-tuple-element.55) | copy-start | bytes 21508
  144.3 4.3 %copy-start.9 = (pred[2,128,512]{1,2,0:T(8,128)(4,1)S(1)}, pred[2,128,512]{1,2,0:T(8,128)(4,1)}, u32[]{:S(2)}) copy-start(pred[2,128,512]{1,2,0:T(8,128)(4,1)} %get-tuple-element.65) | copy-start | bytes 393220
  170.8 14.4 %collective-permute-start.18 = (bf16[2,64,896]{2,1,0:T(8,128)(2,1)S(1)}, bf16[2,64,896]{2,1,0:T(8,128)(2,1)S(1)}, u32[]{:S(2)}, u32[]{:S(2)}) collective-permute-start(bf16[2,64,896]{2,1,0:T(8,128)(2,1)S(1)} %squeeze.47), channel_id=1, source_target_pairs={{0,16},{16,0},{1,17},{17,1},{2,18},{18,2},{3,19},{19,3},{4,20},{20... | collective-permute-start | bytes 688136 | tf_op jit(solution)/shard_map/ppermute | solution.py:102
  (25 other events, 45.6 us)

commit v2 on v1

--- a/solution.py
+++ b/solution.py
@@ -124,22 +124,21 @@
     forward = [(z, (z + 1) % z_size) for z in range(z_size)]
     backward = [(z, (z - 1) % z_size) for z in range(z_size)]
     mine = lax.dynamic_index_in_dim(kv_panel, core, 0, keepdims=False)
-    panel = jnp.zeros((n_chunks,) + mine.shape, mine.dtype)
-    panel = lax.dynamic_update_index_in_dim(panel, mine, fsdp, 0)
     going_up = mine
     going_down = mine
+    from_below = []
+    from_above = []
     for step in range(1, n_chunks // 2 + 1):
         going_up = lax.ppermute(going_up, ("zh", "fsdp"), forward)
-        panel = lax.dynamic_update_index_in_dim(panel, going_up, (fsdp - step) % n_chunks, 0)
+        from_below.append(going_up)
         if step < n_chunks // 2:
             going_down = lax.ppermute(going_down, ("zh", "fsdp"), backward)
-            panel = lax.dynamic_update_index_in_dim(
-                panel, going_down, (fsdp + step) % n_chunks, 0
-            )
-    panel = panel.reshape(model_width, 2 * head_dim)
+            from_above.append(going_down)
+    panel = jnp.concatenate([mine] + from_above + from_below[::-1], axis=0)
 
     own_rows = hidden.reshape(2, block_len, model_width)
     token_rows = jnp.stack([own_rows, swap(own_rows, "core")])
+    token_rows = jnp.roll(token_rows, -fsdp * chunk_rows, axis=-1)
     own_queries = queries.reshape(2, block_len, heads_kv, group_width)
     query_mine = lax.dynamic_index_in_dim(own_queries, core, 2, keepdims=False)
     query_other = lax.dynamic_index_in_dim(own_queries, 1 - core, 2, keepdims=False)

time: 187 us -> 186 us (level)
  waiting for transfers between devices: 26.1 us -> 15.9 us
  local copies, waits for them, and re-layouts: 19.3 us -> 25.7 us
    unnamed x74 -> x89, local copies, waits for them, and re-layouts: 4.8 us -> 14.4 us
    ppermute x8, waiting for transfers between devices: 11 us -> 4.32 us  [local(): going_up = lax.ppermute(going_up, ('zh', 'fsdp'), forward)]
    ppermute x4, waiting for transfers between devices: 11.6 us -> 8.04 us  [swap(): return lax.ppermute(value, axis, [(0, 1), (1, 0)])]
    ppermute x7, starting transfers between devices: 47.6 us -> 44.2 us  [local(): going_down = lax.ppermute(going_down, ('zh', 'fsdp'), backward)]
    ppermute x4, starting transfers between devices: 30.1 us -> 32.7 us  [swap(): return lax.ppermute(value, axis, [(0, 1), (1, 0)])]
    ppermute x8, starting transfers between devices: 15.3 us -> 17.7 us  [local(): going_up = lax.ppermute(going_up, ('zh', 'fsdp'), forward)]
  transfers between devices with their start and end apart: 21 -> 21, of which waited for: 5 -> 5; matrix products, arithmetic and copies ran while one was open for 13% -> 18% of each run, Pallas kernels for 0% -> 0%
where the time goes in v2:
time: 186 us; the launch traced here: 185 us
  starting transfers between devices  108 us (58%)
  local copies, waits for them, and re-layouts  25.7 us (14%)
  matrix products  22.2 us (12%)
  waiting for transfers between devices  15.9 us (9%)
  other arithmetic  11.9 us (6%)
    ppermute x7, starting transfers between devices, local(): going_down = lax.ppermute(going_down, ('zh', 'fsdp'), backward)  44.2 us
    ppermute x4, starting transfers between devices, swap(): return lax.ppermute(value, axis, [(0, 1), (1, 0)])  32.7 us
    ppermute x8, starting transfers between devices, local(): going_up = lax.ppermute(going_up, ('zh', 'fsdp'), forward)  17.7 us
    unnamed x89, local copies, waits for them, and re-layouts  14.4 us
    all_to_all x2, starting transfers between devices, chain(): lax.all_to_all(spread, ('x', 'y'), 0, 0, tiled=True)  13.7 us
    dot_general x9, matrix products, absorb(): jnp.einsum('ptu,ud->ptd', weights.astype(jnp.bfloat16), value_part, prefe...  12.5 us
    ppermute x4, waiting for transfers between devices, swap(): return lax.ppermute(value, axis, [(0, 1), (1, 0)])  8.04 us
    reduce_sum x9, other arithmetic, absorb(): denominator = denominator * factor + jnp.sum(weights, axis=-1)  8.01 us
  transfers between devices with their start and end apart: 21, of which 5 were waited for; matrix products, arithmetic and copies ran while one was open for 18% of the time, Pallas kernels for 0%

profile of v2, /device:TPU:1, one launch (start us, length us, event | category | flops | bytes accessed | tf_op | source)
XLA Modules:
  0.0 185.2 jit_solution(8377863932623762701)
XLA Ops:
  0.0 1.6 constant_dynamic-update-slice_fusion.15
  1.6 4.4 %collective-permute-start.8 = (bf16[224,256]{1,0:T(8,128)(2,1)S(1)}, bf16[224,256]{1,0:T(8,128)(2,1)S(1)}, u32[]{:S(2)}, u32[]{:S(2)}) collective-permute-start(bf16[224,256]{1,0:T(8,128)(2,1)S(1)} %get-tuple-element.31), channel_id=1, source_target_pairs={{0,1},{1,2},{2,3},{3,4},{4,5},{5,6},{6,7},{7,8},{8,9},{9,10},{10,1... | collective-permute-start | bytes 344072 | tf_op jit(solution)/shard_map/ppermute | solution.py:132
  6.0 16.8 %collective-permute-start.1 = (bf16[224,256]{1,0:T(8,128)(2,1)S(1)}, bf16[224,256]{1,0:T(8,128)(2,1)S(1)}, u32[]{:S(2)}, u32[]{:S(2)}) collective-permute-start(bf16[224,256]{1,0:T(8,128)(2,1)S(1)} %get-tuple-element.31), channel_id=1, source_target_pairs={{0,47},{1,0},{2,1},{3,2},{4,3},{5,4},{6,5},{7,6},{8,7},{9,8},{10,9... | collective-permute-start | bytes 344072 | tf_op jit(solution)/shard_map/ppermute | solution.py:135
  23.9 1.9 %constant_dynamic-slice_fusion = (bf16[2,64,1,896]{3,2,1,0:T(2,128)(2,1)S(1)}, bf16[2,64,896]{2,1,0:T(8,128)(2,1)S(1)}) fusion(bf16[2,64,2,896]{3,2,1,0:T(2,128)(2,1)S(1)} %reshape.572, s32[]{:T(128)S(6)} %select_n.136, s32[]{:T(128)S(6)} %select_n.134), kind=kLoop, calls=%fused_computation.254 | loop fusion | bytes 917512 | tf_op jit(solution)/shard_map/jit(dynamic_index_in_dim)/dynamic_slice | solution.py:144
  25.8 2.9 %collective-permute-start.16 = (bf16[2,64,896]{2,1,0:T(8,128)(2,1)S(1)}, bf16[2,64,896]{2,1,0:T(8,128)(2,1)S(1)}, u32[]{:S(2)}, u32[]{:S(2)}) collective-permute-start(bf16[2,64,896]{2,1,0:T(8,128)(2,1)S(1)} %bitcast.545), channel_id=1, source_target_pairs={{0,16},{16,0},{1,17},{17,1},{2,18},{18,2},{3,19},{19,3},{4,20},{20... | collective-permute-start | bytes 688136 | tf_op jit(solution)/shard_map/ppermute | solution.py:102
  28.7 1.9 %collective-permute-start = (bf16[2,64,3584]{2,1,0:T(8,128)(2,1)}, bf16[2,64,3584]{2,1,0:T(8,128)(2,1)}, u32[]{:S(2)}, u32[]{:S(2)}) collective-permute-start(bf16[2,64,3584]{2,1,0:T(8,128)(2,1)} %bitcast.548), channel_id=1, source_target_pairs={{0,16},{16,0},{1,17},{17,1},{2,18},{18,2},{3,19},{19,3},{4,20},{20... | collective-permute-start | bytes 2752520 | tf_op jit(solution)/shard_map/ppermute | solution.py:102
  35.2 1.5 broadcast_compare_fusion.7
  37.0 1.9 %collective-permute-start.9 = (bf16[224,256]{1,0:T(8,128)(2,1)S(1)}, bf16[224,256]{1,0:T(8,128)(2,1)S(1)}, u32[]{:S(2)}, u32[]{:S(2)}) collective-permute-start(bf16[224,256]{1,0:T(8,128)(2,1)S(1)} %collective-permute-done.8), channel_id=1, source_target_pairs={{0,1},{1,2},{2,3},{3,4},{4,5},{5,6},{6,7},{7,8},{8,9},{9,10},{10,1... | collective-permute-start | bytes 344072 | tf_op jit(solution)/shard_map/ppermute | solution.py:132
  38.9 4.6 %collective-permute-start.2 = (bf16[224,256]{1,0:T(8,128)(2,1)S(1)}, bf16[224,256]{1,0:T(8,128)(2,1)S(1)}, u32[]{:S(2)}, u32[]{:S(2)}) collective-permute-start(bf16[224,256]{1,0:T(8,128)(2,1)S(1)} %collective-permute-done.1), channel_id=1, source_target_pairs={{0,47},{1,0},{2,1},{3,2},{4,3},{5,4},{6,5},{7,6},{8,7},{9,8},{10,9... | collective-permute-start | bytes 344072 | tf_op jit(solution)/shard_map/ppermute | solution.py:135
  44.3 1.9 %collective-permute-start.10 = (bf16[224,256]{1,0:T(8,128)(2,1)S(1)}, bf16[224,256]{1,0:T(8,128)(2,1)S(1)}, u32[]{:S(2)}, u32[]{:S(2)}) collective-permute-start(bf16[224,256]{1,0:T(8,128)(2,1)S(1)} %collective-permute-done.9), channel_id=1, source_target_pairs={{0,1},{1,2},{2,3},{3,4},{4,5},{5,6},{6,7},{7,8},{8,9},{9,10},{10,1... | collective-permute-start | bytes 344072 | tf_op jit(solution)/shard_map/ppermute | solution.py:132
  46.2 4.6 %collective-permute-start.3 = (bf16[224,256]{1,0:T(8,128)(2,1)S(1)}, bf16[224,256]{1,0:T(8,128)(2,1)S(1)}, u32[]{:S(2)}, u32[]{:S(2)}) collective-permute-start(bf16[224,256]{1,0:T(8,128)(2,1)S(1)} %collective-permute-done.2), channel_id=1, source_target_pairs={{0,47},{1,0},{2,1},{3,2},{4,3},{5,4},{6,5},{7,6},{8,7},{9,8},{10,9... | collective-permute-start | bytes 344072 | tf_op jit(solution)/shard_map/ppermute | solution.py:135
  51.5 1.9 %collective-permute-start.11 = (bf16[224,256]{1,0:T(8,128)(2,1)S(1)}, bf16[224,256]{1,0:T(8,128)(2,1)S(1)}, u32[]{:S(2)}, u32[]{:S(2)}) collective-permute-start(bf16[224,256]{1,0:T(8,128)(2,1)S(1)} %collective-permute-done.10), channel_id=1, source_target_pairs={{0,1},{1,2},{2,3},{3,4},{4,5},{5,6},{6,7},{7,8},{8,9},{9,10},{10,1... | collective-permute-start | bytes 344072 | tf_op jit(solution)/shard_map/ppermute | solution.py:132
  53.4 4.6 %collective-permute-start.4 = (bf16[224,256]{1,0:T(8,128)(2,1)S(1)}, bf16[224,256]{1,0:T(8,128)(2,1)S(1)}, u32[]{:S(2)}, u32[]{:S(2)}) collective-permute-start(bf16[224,256]{1,0:T(8,128)(2,1)S(1)} %collective-permute-done.3), channel_id=1, source_target_pairs={{0,47},{1,0},{2,1},{3,2},{4,3},{5,4},{6,5},{7,6},{8,7},{9,8},{10,9... | collective-permute-start | bytes 344072 | tf_op jit(solution)/shard_map/ppermute | solution.py:135
  58.6 1.9 %collective-permute-start.12 = (bf16[224,256]{1,0:T(8,128)(2,1)S(1)}, bf16[224,256]{1,0:T(8,128)(2,1)S(1)}, u32[]{:S(2)}, u32[]{:S(2)}) collective-permute-start(bf16[224,256]{1,0:T(8,128)(2,1)S(1)} %collective-permute-done.11), channel_id=1, source_target_pairs={{0,1},{1,2},{2,3},{3,4},{4,5},{5,6},{6,7},{7,8},{8,9},{9,10},{10,1... | collective-permute-start | bytes 344072 | tf_op jit(solution)/shard_map/ppermute | solution.py:132
  60.6 4.6 %collective-permute-start.5 = (bf16[224,256]{1,0:T(8,128)(2,1)S(1)}, bf16[224,256]{1,0:T(8,128)(2,1)S(1)}, u32[]{:S(2)}, u32[]{:S(2)}) collective-permute-start(bf16[224,256]{1,0:T(8,128)(2,1)S(1)} %collective-permute-done.4), channel_id=1, source_target_pairs={{0,47},{1,0},{2,1},{3,2},{4,3},{5,4},{6,5},{7,6},{8,7},{9,8},{10,9... | collective-permute-start | bytes 344072 | tf_op jit(solution)/shard_map/ppermute | solution.py:135
  65.8 1.9 %collective-permute-start.13 = (bf16[224,256]{1,0:T(8,128)(2,1)S(1)}, bf16[224,256]{1,0:T(8,128)(2,1)S(1)}, u32[]{:S(2)}, u32[]{:S(2)}) collective-permute-start(bf16[224,256]{1,0:T(8,128)(2,1)S(1)} %collective-permute-done.12), channel_id=1, source_target_pairs={{0,1},{1,2},{2,3},{3,4},{4,5},{5,6},{6,7},{7,8},{8,9},{9,10},{10,1... | collective-permute-start | bytes 344072 | tf_op jit(solution)/shard_map/ppermute | solution.py:132
  67.7 4.6 %collective-permute-start.6 = (bf16[224,256]{1,0:T(8,128)(2,1)S(1)}, bf16[224,256]{1,0:T(8,128)(2,1)S(1)}, u32[]{:S(2)}, u32[]{:S(2)}) collective-permute-start(bf16[224,256]{1,0:T(8,128)(2,1)S(1)} %collective-permute-done.5), channel_id=1, source_target_pairs={{0,47},{1,0},{2,1},{3,2},{4,3},{5,4},{6,5},{7,6},{8,7},{9,8},{10,9... | collective-permute-start | bytes 344072 | tf_op jit(solution)/shard_map/ppermute | solution.py:135
  73.0 1.9 %collective-permute-start.14 = (bf16[224,256]{1,0:T(8,128)(2,1)S(1)}, bf16[224,256]{1,0:T(8,128)(2,1)S(1)}, u32[]{:S(2)}, u32[]{:S(2)}) collective-permute-start(bf16[224,256]{1,0:T(8,128)(2,1)S(1)} %collective-permute-done.13), channel_id=1, source_target_pairs={{0,1},{1,2},{2,3},{3,4},{4,5},{5,6},{6,7},{7,8},{8,9},{9,10},{10,1... | collective-permute-start | bytes 344072 | tf_op jit(solution)/shard_map/ppermute | solution.py:132
  74.9 4.6 %collective-permute-start.7 = (bf16[224,256]{1,0:T(8,128)(2,1)S(1)}, bf16[224,256]{1,0:T(8,128)(2,1)S(1)}, u32[]{:S(2)}, u32[]{:S(2)}) collective-permute-start(bf16[224,256]{1,0:T(8,128)(2,1)S(1)} %collective-permute-done.6), channel_id=1, source_target_pairs={{0,47},{1,0},{2,1},{3,2},{4,3},{5,4},{6,5},{7,6},{8,7},{9,8},{10,9... | collective-permute-start | bytes 344072 | tf_op jit(solution)/shard_map/ppermute | solution.py:135
  80.1 1.9 %collective-permute-start.15 = (bf16[224,256]{1,0:T(8,128)(2,1)S(1)}, bf16[224,256]{1,0:T(8,128)(2,1)S(1)}, u32[]{:S(2)}, u32[]{:S(2)}) collective-permute-start(bf16[224,256]{1,0:T(8,128)(2,1)S(1)} %collective-permute-done.14), channel_id=1, source_target_pairs={{0,1},{1,2},{2,3},{3,4},{4,5},{5,6},{6,7},{7,8},{8,9},{9,10},{10,1... | collective-permute-start | bytes 344072 | tf_op jit(solution)/shard_map/ppermute | solution.py:132
  82.7 4.2 %collective-permute-done.15 = bf16[224,256]{1,0:T(8,128)(2,1)S(1)} collective-permute-done((bf16[224,256]{1,0:T(8,128)(2,1)S(1)}, bf16[224,256]{1,0:T(8,128)(2,1)S(1)}, u32[]{:S(2)}, u32[]{:S(2)}) %collective-permute-start.15) | collective-permute-done | bytes 114720 | tf_op jit(solution)/shard_map/ppermute | solution.py:132
  92.1 3.7 %fusion.222 = (bf16[2,2,64,256]{3,2,1,0:T(8,128)(2,1)S(1)}, f32[2,2,64,256]{3,2,1,0:T(8,128)S(1)}) fusion(bf16[3584,256]{1,0:T(8,128)(2,1)} %constant_dynamic-update-slice_fusion, s32[]{:T(128)S(6)} %select_n.133, bf16[1,2,64,3584]{3,2,1,0:T(8,128)(2,1)} %bitcast.549, bf16[1,2,64,3584]{3,2,1,0:T(8,128)(2,1)} %bitcast.2), kind=kOutput, calls=%fused_computation.301 | convolution fusion | flops 477167616 | bytes 4063236 | tf_op jit(solution)/shard_map/bctd,de->bcte/dot_general | solution.py:149
  97.1 6.8 %all-to-all-start = ((bf16[16,2,64,256]{3,2,1,0:T(8,128)(2,1)}), bf16[16,2,64,256]{3,2,1,0:T(8,128)(2,1)S(1)}, u32[]{:S(2)}, u32[]{:S(2)}) async-start(bf16[16,2,64,256]{3,2,1,0:T(8,128)(2,1)} %broadcast_in_dim.202), calls=%async_computation | async-start | bytes 2097152 | tf_op jit(solution)/shard_map/all_to_all | solution.py:177
  104.3 15.2 %collective-permute-start.17 = (bf16[2,64,256]{2,1,0:T(8,128)(2,1)S(1)}, bf16[2,64,256]{2,1,0:T(8,128)(2,1)S(1)}, u32[]{:S(2)}, u32[]{:S(2)}) collective-permute-start(bf16[2,64,256]{2,1,0:T(8,128)(2,1)S(1)} %pad_maximum_fusion), channel_id=1, source_target_pairs={{0,32},{32,0},{1,33},{33,1},{2,34},{34,2},{3,35},{35,3},{4,36},{36... | collective-permute-start | bytes 196616 | tf_op jit(solution)/shard_map/ppermute | solution.py:102
  120.5 7.4 %collective-permute-done.17 = bf16[2,64,256]{2,1,0:T(8,128)(2,1)S(1)} collective-permute-done((bf16[2,64,256]{2,1,0:T(8,128)(2,1)S(1)}, bf16[2,64,256]{2,1,0:T(8,128)(2,1)S(1)}, u32[]{:S(2)}, u32[]{:S(2)}) %collective-permute-start.17) | collective-permute-done | bytes 65568 | tf_op jit(solution)/shard_map/ppermute | solution.py:102
  129.0 6.9 %all-to-all-start.1 = ((bf16[16,2,64,256]{3,2,1,0:T(8,128)(2,1)}), bf16[16,2,64,256]{3,2,1,0:T(8,128)(2,1)S(1)}, u32[]{:S(2)}, u32[]{:S(2)}) async-start(bf16[16,2,64,256]{3,2,1,0:T(8,128)(2,1)} %broadcast_in_dim.213), calls=%async_computation.1 | async-start | bytes 2097152 | tf_op jit(solution)/shard_map/all_to_all | solution.py:177
  144.0 3.5 %all-to-all-done.1 = bf16[16,2,64,256]{3,2,1,0:T(8,128)(2,1)S(1)} async-done(((bf16[16,2,64,256]{3,2,1,0:T(8,128)(2,1)}), bf16[16,2,64,256]{3,2,1,0:T(8,128)(2,1)S(1)}, u32[]{:S(2)}, u32[]{:S(2)}) %all-to-all-start.1) | async-done | bytes 1048608 | tf_op jit(solution)/shard_map/all_to_all | solution.py:177
  154.5 1.4 fusion.105
  156.5 1.4 fusion.129
  160.6 1.3 fusion.87
  168.0 1.9 %fusion.132 = bf16[2,128,7,128]{3,1,2,0:T(8,128)(2,1)S(1)} fusion(f32[2,128,7,128]{3,1,2,0:T(8,128)S(1)} %fusion.87, f32[2,128,7,128]{3,1,2,0:T(8,128)S(1)} %fusion.111, f32[2,128,7]{1,2,0:T(8,128)S(1)} %get-tuple-element.13, f32[2,128,7]{1,2,0:T(8,128)S(1)} %get-tuple-element.15, f32[2,128,7]{1,2,0:T(8,128)S(1)} %get-tuple-element.14, ...), kind=kOutput, calls=%fused_computation.98 | convolution fusion | flops 31309824 | bytes 2821248 | tf_op jit(solution)/shard_map/vmap(ptu,ud->ptd)/dot_general | solution.py:42
  170.5 12.8 %collective-permute-start.18 = (bf16[2,64,896]{2,1,0:T(8,128)(2,1)S(1)}, bf16[2,64,896]{2,1,0:T(8,128)(2,1)S(1)}, u32[]{:S(2)}, u32[]{:S(2)}) collective-permute-start(bf16[2,64,896]{2,1,0:T(8,128)(2,1)S(1)} %squeeze.47), channel_id=1, source_target_pairs={{0,16},{16,0},{1,17},{17,1},{2,18},{18,2},{3,19},{19,3},{4,20},{20... | collective-permute-start | bytes 688136 | tf_op jit(solution)/shard_map/ppermute | solution.py:102
  (202 shorter events, 45.9 us)
Async XLA Ops:
  0.0 30.8 %copy-start = (s32[1,64]{1,0:T(1,128)S(1)}, s32[1,64]{1,0:T(1,128)}, u32[]{:S(2)}) copy-start(s32[1,64]{1,0:T(1,128)} %param.7) | copy-start | bytes 772
  0.0 31.5 %copy-start.35 = (s32[128]{0:T(128)S(1)}, s32[128]{0:T(128)}, u32[]{:S(2)}) copy-start(s32[128]{0:T(128)} %constant.110.clone.1) | copy-start | bytes 1540
  1.6 35.4 %collective-permute-start.8 = (bf16[224,256]{1,0:T(8,128)(2,1)S(1)}, bf16[224,256]{1,0:T(8,128)(2,1)S(1)}, u32[]{:S(2)}, u32[]{:S(2)}) collective-permute-start(bf16[224,256]{1,0:T(8,128)(2,1)S(1)} %get-tuple-element.31), channel_id=1, source_target_pairs={{0,1},{1,2},{2,3},{3,4},{4,5},{5,6},{6,7},{7,8},{8,9},{9,10},{10,1... | collective-permute-start | bytes 344072 | tf_op jit(solution)/shard_map/ppermute | solution.py:132
  6.0 33.0 %collective-permute-start.1 = (bf16[224,256]{1,0:T(8,128)(2,1)S(1)}, bf16[224,256]{1,0:T(8,128)(2,1)S(1)}, u32[]{:S(2)}, u32[]{:S(2)}) collective-permute-start(bf16[224,256]{1,0:T(8,128)(2,1)S(1)} %get-tuple-element.31), channel_id=1, source_target_pairs={{0,47},{1,0},{2,1},{3,2},{4,3},{5,4},{6,5},{7,6},{8,7},{9,8},{10,9... | collective-permute-start | bytes 344072 | tf_op jit(solution)/shard_map/ppermute | solution.py:135
  25.8 78.1 %collective-permute-start.16 = (bf16[2,64,896]{2,1,0:T(8,128)(2,1)S(1)}, bf16[2,64,896]{2,1,0:T(8,128)(2,1)S(1)}, u32[]{:S(2)}, u32[]{:S(2)}) collective-permute-start(bf16[2,64,896]{2,1,0:T(8,128)(2,1)S(1)} %bitcast.545), channel_id=1, source_target_pairs={{0,16},{16,0},{1,17},{17,1},{2,18},{18,2},{3,19},{19,3},{4,20},{20... | collective-permute-start | bytes 688136 | tf_op jit(solution)/shard_map/ppermute | solution.py:102
  28.7 63.4 %collective-permute-start = (bf16[2,64,3584]{2,1,0:T(8,128)(2,1)}, bf16[2,64,3584]{2,1,0:T(8,128)(2,1)}, u32[]{:S(2)}, u32[]{:S(2)}) collective-permute-start(bf16[2,64,3584]{2,1,0:T(8,128)(2,1)} %bitcast.548), channel_id=1, source_target_pairs={{0,16},{16,0},{1,17},{17,1},{2,18},{18,2},{3,19},{19,3},{4,20},{20... | collective-permute-start | bytes 2752520 | tf_op jit(solution)/shard_map/ppermute | solution.py:102
  37.0 7.3 %collective-permute-start.9 = (bf16[224,256]{1,0:T(8,128)(2,1)S(1)}, bf16[224,256]{1,0:T(8,128)(2,1)S(1)}, u32[]{:S(2)}, u32[]{:S(2)}) collective-permute-start(bf16[224,256]{1,0:T(8,128)(2,1)S(1)} %collective-permute-done.8), channel_id=1, source_target_pairs={{0,1},{1,2},{2,3},{3,4},{4,5},{5,6},{6,7},{7,8},{8,9},{9,10},{10,1... | collective-permute-start | bytes 344072 | tf_op jit(solution)/shard_map/ppermute | solution.py:132
  38.9 7.3 %collective-permute-start.2 = (bf16[224,256]{1,0:T(8,128)(2,1)S(1)}, bf16[224,256]{1,0:T(8,128)(2,1)S(1)}, u32[]{:S(2)}, u32[]{:S(2)}) collective-permute-start(bf16[224,256]{1,0:T(8,128)(2,1)S(1)} %collective-permute-done.1), channel_id=1, source_target_pairs={{0,47},{1,0},{2,1},{3,2},{4,3},{5,4},{6,5},{7,6},{8,7},{9,8},{10,9... | collective-permute-start | bytes 344072 | tf_op jit(solution)/shard_map/ppermute | solution.py:135
  44.3 7.2 %collective-permute-start.10 = (bf16[224,256]{1,0:T(8,128)(2,1)S(1)}, bf16[224,256]{1,0:T(8,128)(2,1)S(1)}, u32[]{:S(2)}, u32[]{:S(2)}) collective-permute-start(bf16[224,256]{1,0:T(8,128)(2,1)S(1)} %collective-permute-done.9), channel_id=1, source_target_pairs={{0,1},{1,2},{2,3},{3,4},{4,5},{5,6},{6,7},{7,8},{8,9},{9,10},{10,1... | collective-permute-start | bytes 344072 | tf_op jit(solution)/shard_map/ppermute | solution.py:132
  46.2 7.2 %collective-permute-start.3 = (bf16[224,256]{1,0:T(8,128)(2,1)S(1)}, bf16[224,256]{1,0:T(8,128)(2,1)S(1)}, u32[]{:S(2)}, u32[]{:S(2)}) collective-permute-start(bf16[224,256]{1,0:T(8,128)(2,1)S(1)} %collective-permute-done.2), channel_id=1, source_target_pairs={{0,47},{1,0},{2,1},{3,2},{4,3},{5,4},{6,5},{7,6},{8,7},{9,8},{10,9... | collective-permute-start | bytes 344072 | tf_op jit(solution)/shard_map/ppermute | solution.py:135
  51.5 7.2 %collective-permute-start.11 = (bf16[224,256]{1,0:T(8,128)(2,1)S(1)}, bf16[224,256]{1,0:T(8,128)(2,1)S(1)}, u32[]{:S(2)}, u32[]{:S(2)}) collective-permute-start(bf16[224,256]{1,0:T(8,128)(2,1)S(1)} %collective-permute-done.10), channel_id=1, source_target_pairs={{0,1},{1,2},{2,3},{3,4},{4,5},{5,6},{6,7},{7,8},{8,9},{9,10},{10,1... | collective-permute-start | bytes 344072 | tf_op jit(solution)/shard_map/ppermute | solution.py:132
  53.4 7.1 %collective-permute-start.4 = (bf16[224,256]{1,0:T(8,128)(2,1)S(1)}, bf16[224,256]{1,0:T(8,128)(2,1)S(1)}, u32[]{:S(2)}, u32[]{:S(2)}) collective-permute-start(bf16[224,256]{1,0:T(8,128)(2,1)S(1)} %collective-permute-done.3), channel_id=1, source_target_pairs={{0,47},{1,0},{2,1},{3,2},{4,3},{5,4},{6,5},{7,6},{8,7},{9,8},{10,9... | collective-permute-start | bytes 344072 | tf_op jit(solution)/shard_map/ppermute | solution.py:135
  58.6 7.2 %collective-permute-start.12 = (bf16[224,256]{1,0:T(8,128)(2,1)S(1)}, bf16[224,256]{1,0:T(8,128)(2,1)S(1)}, u32[]{:S(2)}, u32[]{:S(2)}) collective-permute-start(bf16[224,256]{1,0:T(8,128)(2,1)S(1)} %collective-permute-done.11), channel_id=1, source_target_pairs={{0,1},{1,2},{2,3},{3,4},{4,5},{5,6},{6,7},{7,8},{8,9},{9,10},{10,1... | collective-permute-start | bytes 344072 | tf_op jit(solution)/shard_map/ppermute | solution.py:132
  60.6 7.2 %collective-permute-start.5 = (bf16[224,256]{1,0:T(8,128)(2,1)S(1)}, bf16[224,256]{1,0:T(8,128)(2,1)S(1)}, u32[]{:S(2)}, u32[]{:S(2)}) collective-permute-start(bf16[224,256]{1,0:T(8,128)(2,1)S(1)} %collective-permute-done.4), channel_id=1, source_target_pairs={{0,47},{1,0},{2,1},{3,2},{4,3},{5,4},{6,5},{7,6},{8,7},{9,8},{10,9... | collective-permute-start | bytes 344072 | tf_op jit(solution)/shard_map/ppermute | solution.py:135
  65.8 7.2 %collective-permute-start.13 = (bf16[224,256]{1,0:T(8,128)(2,1)S(1)}, bf16[224,256]{1,0:T(8,128)(2,1)S(1)}, u32[]{:S(2)}, u32[]{:S(2)}) collective-permute-start(bf16[224,256]{1,0:T(8,128)(2,1)S(1)} %collective-permute-done.12), channel_id=1, source_target_pairs={{0,1},{1,2},{2,3},{3,4},{4,5},{5,6},{6,7},{7,8},{8,9},{9,10},{10,1... | collective-permute-start | bytes 344072 | tf_op jit(solution)/shard_map/ppermute | solution.py:132
  67.7 7.1 %collective-permute-start.6 = (bf16[224,256]{1,0:T(8,128)(2,1)S(1)}, bf16[224,256]{1,0:T(8,128)(2,1)S(1)}, u32[]{:S(2)}, u32[]{:S(2)}) collective-permute-start(bf16[224,256]{1,0:T(8,128)(2,1)S(1)} %collective-permute-done.5), channel_id=1, source_target_pairs={{0,47},{1,0},{2,1},{3,2},{4,3},{5,4},{6,5},{7,6},{8,7},{9,8},{10,9... | collective-permute-start | bytes 344072 | tf_op jit(solution)/shard_map/ppermute | solution.py:135
  73.0 7.2 %collective-permute-start.14 = (bf16[224,256]{1,0:T(8,128)(2,1)S(1)}, bf16[224,256]{1,0:T(8,128)(2,1)S(1)}, u32[]{:S(2)}, u32[]{:S(2)}) collective-permute-start(bf16[224,256]{1,0:T(8,128)(2,1)S(1)} %collective-permute-done.13), channel_id=1, source_target_pairs={{0,1},{1,2},{2,3},{3,4},{4,5},{5,6},{6,7},{7,8},{8,9},{9,10},{10,1... | collective-permute-start | bytes 344072 | tf_op jit(solution)/shard_map/ppermute | solution.py:132
  74.9 7.1 %collective-permute-start.7 = (bf16[224,256]{1,0:T(8,128)(2,1)S(1)}, bf16[224,256]{1,0:T(8,128)(2,1)S(1)}, u32[]{:S(2)}, u32[]{:S(2)}) collective-permute-start(bf16[224,256]{1,0:T(8,128)(2,1)S(1)} %collective-permute-done.6), channel_id=1, source_target_pairs={{0,47},{1,0},{2,1},{3,2},{4,3},{5,4},{6,5},{7,6},{8,7},{9,8},{10,9... | collective-permute-start | bytes 344072 | tf_op jit(solution)/shard_map/ppermute | solution.py:135
  80.1 6.7 %collective-permute-start.15 = (bf16[224,256]{1,0:T(8,128)(2,1)S(1)}, bf16[224,256]{1,0:T(8,128)(2,1)S(1)}, u32[]{:S(2)}, u32[]{:S(2)}) collective-permute-start(bf16[224,256]{1,0:T(8,128)(2,1)S(1)} %collective-permute-done.14), channel_id=1, source_target_pairs={{0,1},{1,2},{2,3},{3,4},{4,5},{5,6},{6,7},{7,8},{8,9},{9,10},{10,1... | collective-permute-start | bytes 344072 | tf_op jit(solution)/shard_map/ppermute | solution.py:132
  97.1 30.8 %all-to-all-start = ((bf16[16,2,64,256]{3,2,1,0:T(8,128)(2,1)}), bf16[16,2,64,256]{3,2,1,0:T(8,128)(2,1)S(1)}, u32[]{:S(2)}, u32[]{:S(2)}) async-start(bf16[16,2,64,256]{3,2,1,0:T(8,128)(2,1)} %broadcast_in_dim.202), calls=%async_computation | async-start | bytes 2097152 | tf_op jit(solution)/shard_map/all_to_all | solution.py:177
  104.3 23.6 %collective-permute-start.17 = (bf16[2,64,256]{2,1,0:T(8,128)(2,1)S(1)}, bf16[2,64,256]{2,1,0:T(8,128)(2,1)S(1)}, u32[]{:S(2)}, u32[]{:S(2)}) collective-permute-start(bf16[2,64,256]{2,1,0:T(8,128)(2,1)S(1)} %pad_maximum_fusion), channel_id=1, source_target_pairs={{0,32},{32,0},{1,33},{33,1},{2,34},{34,2},{3,35},{35,3},{4,36},{36... | collective-permute-start | bytes 196616 | tf_op jit(solution)/shard_map/ppermute | solution.py:102
  119.8 9.2 %copy-start.23 = (f32[2,7,128]{2,1,0:T(8,128)}, f32[2,7,128]{2,1,0:T(8,128)S(1)}, u32[]{:S(2)}) copy-start(f32[2,7,128]{2,1,0:T(8,128)S(1)} %broadcast_maximum_fusion.2) | copy-start | bytes 21508
  129.0 18.5 %all-to-all-start.1 = ((bf16[16,2,64,256]{3,2,1,0:T(8,128)(2,1)}), bf16[16,2,64,256]{3,2,1,0:T(8,128)(2,1)S(1)}, u32[]{:S(2)}, u32[]{:S(2)}) async-start(bf16[16,2,64,256]{3,2,1,0:T(8,128)(2,1)} %broadcast_in_dim.213), calls=%async_computation.1 | async-start | bytes 2097152 | tf_op jit(solution)/shard_map/all_to_all | solution.py:177
  137.6 5.5 %copy-start.7 = (f32[512,2,128,7]{2,0,3,1:T(8,128)}, f32[512,2,128,7]{2,0,3,1:T(8,128)S(1)}, u32[]{:S(2)}) copy-start(f32[512,2,128,7]{2,0,3,1:T(8,128)S(1)} %get-tuple-element.86) | copy-start | bytes 11010052
  138.3 2.3 %copy-start.3 = (f32[512,2,128,7]{2,0,3,1:T(8,128)}, f32[512,2,128,7]{2,0,3,1:T(8,128)S(1)}, u32[]{:S(2)}) copy-start(f32[512,2,128,7]{2,0,3,1:T(8,128)S(1)} %get-tuple-element.82) | copy-start | bytes 11010052
  139.1 3.1 %copy-start.5 = (f32[512,2,128,7]{2,0,3,1:T(8,128)}, f32[512,2,128,7]{2,0,3,1:T(8,128)S(1)}, u32[]{:S(2)}) copy-start(f32[512,2,128,7]{2,0,3,1:T(8,128)S(1)} %get-tuple-element.84) | copy-start | bytes 11010052
  139.1 2.5 %copy-start.25 = (f32[2,7,128]{2,1,0:T(8,128)}, f32[2,7,128]{2,1,0:T(8,128)S(1)}, u32[]{:S(2)}) copy-start(f32[2,7,128]{2,1,0:T(8,128)S(1)} %get-tuple-element.22) | copy-start | bytes 21508
  139.1 2.5 %copy-start.27 = (f32[2,7,128]{2,1,0:T(8,128)}, f32[2,7,128]{2,1,0:T(8,128)S(1)}, u32[]{:S(2)}) copy-start(f32[2,7,128]{2,1,0:T(8,128)S(1)} %get-tuple-element.23) | copy-start | bytes 21508
  139.1 3.1 %copy-start.29 = (f32[2,7,128]{2,1,0:T(8,128)}, f32[2,7,128]{2,1,0:T(8,128)S(1)}, u32[]{:S(2)}) copy-start(f32[2,7,128]{2,1,0:T(8,128)S(1)} %get-tuple-element.24) | copy-start | bytes 21508
  139.1 4.0 %copy-start.31 = (f32[2,7,128]{2,1,0:T(8,128)}, f32[2,7,128]{2,1,0:T(8,128)S(1)}, u32[]{:S(2)}) copy-start(f32[2,7,128]{2,1,0:T(8,128)S(1)} %get-tuple-element.55) | copy-start | bytes 21508
  144.0 4.3 %copy-start.9 = (pred[2,128,512]{1,2,0:T(8,128)(4,1)S(1)}, pred[2,128,512]{1,2,0:T(8,128)(4,1)}, u32[]{:S(2)}) copy-start(pred[2,128,512]{1,2,0:T(8,128)(4,1)} %get-tuple-element.65) | copy-start | bytes 393220
  170.5 13.9 %collective-permute-start.18 = (bf16[2,64,896]{2,1,0:T(8,128)(2,1)S(1)}, bf16[2,64,896]{2,1,0:T(8,128)(2,1)S(1)}, u32[]{:S(2)}, u32[]{:S(2)}) collective-permute-start(bf16[2,64,896]{2,1,0:T(8,128)(2,1)S(1)} %squeeze.47), channel_id=1, source_target_pairs={{0,16},{16,0},{1,17},{17,1},{2,18},{18,2},{3,19},{19,3},{4,20},{20... | collective-permute-start | bytes 688136 | tf_op jit(solution)/shard_map/ppermute | solution.py:102
  (25 other events, 46.3 us)

commit v3 on v2

--- a/solution.py
+++ b/solution.py
@@ -171,16 +171,31 @@
     ) * 2 + src_core
     every_block = block_table[src.reshape(-1)].reshape(2, 4, 4, 2)
 
+    visible = jnp.max(own_blocks) + 1
+
     def chain(rows, side):
-        blocks = jnp.swapaxes(every_block[side], 0, 1).reshape(-1, 4, 2)
+        blocks = jnp.swapaxes(every_block[side], 0, 1).reshape(-1)
         spread = jnp.broadcast_to(rows[None], (16,) + rows.shape)
-        gathered = lax.all_to_all(spread, ("x", "y"), 0, 0, tiled=True).reshape(-1, 4, *rows.shape)
+        gathered = lax.all_to_all(spread, ("x", "y"), 0, 0, tiled=True)
+        gathered = gathered.reshape(blocks.shape[0], block_len, 2 * head_dim)
+        rank = jnp.sum(blocks[None, :] < blocks[:, None], axis=1)
+        order = jnp.argmax(rank[None, :] == jnp.arange(blocks.shape[0])[:, None], axis=1)
+        sorted_rows = gathered[order]
+        sorted_blocks = blocks[order]
+        tile_blocks = 8
+        tiles = (jnp.sum(blocks < visible) + tile_blocks - 1) // tile_blocks
+
+        def one_tile(tile_index, fold_carry):
+            first = tile_index * tile_blocks
+            return absorb_chunk(
+                fold_carry, query_rows,
+                lax.dynamic_slice_in_dim(sorted_rows, first, tile_blocks, 0),
+                lax.dynamic_slice_in_dim(sorted_blocks, first, tile_blocks, 0),
+                row_limit, score_scale,
+            )
+
         fold_carry = empty_state(2, group_size, rows_all, head_dim)
-        for part in range(gathered.shape[0]):
-            fold_carry = absorb_chunk(
-                fold_carry, query_rows, gathered[part], blocks[part], row_limit, score_scale
-            )
-        return fold_carry
+        return lax.fori_loop(0, tiles, one_tile, fold_carry)
 
     noisy_ok = jnp.broadcast_to((jnp.arange(rows_all) >= block_len)[:, None], (rows_all, block_len))
     noisy_state = jax.vmap(absorb, in_axes=(0, 0, 0, 0, None, None))(

time: 186 us -> 191 us (1.027)
  the two profiles are of different devices: /device:TPU:1 before, /device:TPU:3 now
where the time goes in v3:
time: 191 us; the launch traced here: 190 us
  starting transfers between devices  106 us (55%)
  waiting for transfers between devices  23.3 us (12%)
  matrix products  23.1 us (12%)
  local copies, waits for them, and re-layouts  20.7 us (11%)
  other arithmetic  14.4 us (8%)
  between operations  2.68 us (1%)
    ppermute x7, starting transfers between devices, local(): going_down = lax.ppermute(going_down, ('zh', 'fsdp'), backward)  47.6 us
    ppermute x4, starting transfers between devices, swap(): return lax.ppermute(value, axis, [(0, 1), (1, 0)])  29.2 us
    ppermute x8, starting transfers between devices, local(): going_up = lax.ppermute(going_up, ('zh', 'fsdp'), forward)  15.3 us
    dot_general x9, matrix products, absorb(): jnp.einsum('ptu,ud->ptd', weights.astype(jnp.bfloat16), value_part, prefe...  14 us
    all_to_all x2, starting transfers between devices, chain(): gathered = lax.all_to_all(spread, ('x', 'y'), 0, 0, tiled=True)  13.6 us
    ppermute x4, waiting for transfers between devices, swap(): return lax.ppermute(value, axis, [(0, 1), (1, 0)])  12.2 us
    ppermute x8, waiting for transfers between devices, local(): going_up = lax.ppermute(going_up, ('zh', 'fsdp'), forward)  11.1 us
    reduce_sum x9, other arithmetic, absorb(): denominator = denominator * factor + jnp.sum(weights, axis=-1)  7.2 us
  transfers between devices with their start and end apart: 21, of which 4 were waited for; matrix products, arithmetic and copies ran while one was open for 17% of the time, Pallas kernels for 0%

profile of v3, /device:TPU:3, one launch (start us, length us, event | category | flops | bytes accessed | tf_op | source)
XLA Modules:
  0.0 190.5 jit_solution(13339882885944842703)
XLA Ops:
  0.9 18.4 %collective-permute-start.1 = (bf16[224,256]{1,0:T(8,128)(2,1)S(1)}, bf16[224,256]{1,0:T(8,128)(2,1)S(1)}, u32[]{:S(2)}, u32[]{:S(2)}) collective-permute-start(bf16[224,256]{1,0:T(8,128)(2,1)S(1)} %get-tuple-element.213), channel_id=1, source_target_pairs={{0,47},{1,0},{2,1},{3,2},{4,3},{5,4},{6,5},{7,6},{8,7},{9,8},{10,9... | collective-permute-start | bytes 344072 | tf_op jit(solution)/shard_map/ppermute | solution.py:135
  19.3 1.9 %collective-permute-start.8 = (bf16[224,256]{1,0:T(8,128)(2,1)S(1)}, bf16[224,256]{1,0:T(8,128)(2,1)S(1)}, u32[]{:S(2)}, u32[]{:S(2)}) collective-permute-start(bf16[224,256]{1,0:T(8,128)(2,1)S(1)} %get-tuple-element.213), channel_id=1, source_target_pairs={{0,1},{1,2},{2,3},{3,4},{4,5},{5,6},{6,7},{7,8},{8,9},{9,10},{10,1... | collective-permute-start | bytes 344072 | tf_op jit(solution)/shard_map/ppermute | solution.py:132
  21.3 2.9 %collective-permute-start = (bf16[2,64,3584]{2,1,0:T(8,128)(2,1)}, bf16[2,64,3584]{2,1,0:T(8,128)(2,1)}, u32[]{:S(2)}, u32[]{:S(2)}) collective-permute-start(bf16[2,64,3584]{2,1,0:T(8,128)(2,1)} %bitcast.150), channel_id=1, source_target_pairs={{0,16},{16,0},{1,17},{17,1},{2,18},{18,2},{3,19},{19,3},{4,20},{20... | collective-permute-start | bytes 2752520 | tf_op jit(solution)/shard_map/ppermute | solution.py:102
  25.3 1.9 constant_dynamic-slice_fusion.2
  27.2 1.9 %collective-permute-start.16 = (bf16[2,64,896]{2,1,0:T(8,128)(2,1)S(1)}, bf16[2,64,896]{2,1,0:T(8,128)(2,1)S(1)}, u32[]{:S(2)}, u32[]{:S(2)}) collective-permute-start(bf16[2,64,896]{2,1,0:T(8,128)(2,1)S(1)} %bitcast.147), channel_id=1, source_target_pairs={{0,16},{16,0},{1,17},{17,1},{2,18},{18,2},{3,19},{19,3},{4,20},{20... | collective-permute-start | bytes 688136 | tf_op jit(solution)/shard_map/ppermute | solution.py:102
  36.5 4.8 %collective-permute-start.2 = (bf16[224,256]{1,0:T(8,128)(2,1)S(1)}, bf16[224,256]{1,0:T(8,128)(2,1)S(1)}, u32[]{:S(2)}, u32[]{:S(2)}) collective-permute-start(bf16[224,256]{1,0:T(8,128)(2,1)S(1)} %collective-permute-done.1), channel_id=1, source_target_pairs={{0,47},{1,0},{2,1},{3,2},{4,3},{5,4},{6,5},{7,6},{8,7},{9,8},{10,9... | collective-permute-start | bytes 344072 | tf_op jit(solution)/shard_map/ppermute | solution.py:135
  41.4 1.9 %collective-permute-start.9 = (bf16[224,256]{1,0:T(8,128)(2,1)S(1)}, bf16[224,256]{1,0:T(8,128)(2,1)S(1)}, u32[]{:S(2)}, u32[]{:S(2)}) collective-permute-start(bf16[224,256]{1,0:T(8,128)(2,1)S(1)} %collective-permute-done.8), channel_id=1, source_target_pairs={{0,1},{1,2},{2,3},{3,4},{4,5},{5,6},{6,7},{7,8},{8,9},{9,10},{10,1... | collective-permute-start | bytes 344072 | tf_op jit(solution)/shard_map/ppermute | solution.py:132
  43.4 5.3 %collective-permute-start.3 = (bf16[224,256]{1,0:T(8,128)(2,1)S(1)}, bf16[224,256]{1,0:T(8,128)(2,1)S(1)}, u32[]{:S(2)}, u32[]{:S(2)}) collective-permute-start(bf16[224,256]{1,0:T(8,128)(2,1)S(1)} %collective-permute-done.2), channel_id=1, source_target_pairs={{0,47},{1,0},{2,1},{3,2},{4,3},{5,4},{6,5},{7,6},{8,7},{9,8},{10,9... | collective-permute-start | bytes 344072 | tf_op jit(solution)/shard_map/ppermute | solution.py:135
  48.7 1.9 %collective-permute-start.10 = (bf16[224,256]{1,0:T(8,128)(2,1)S(1)}, bf16[224,256]{1,0:T(8,128)(2,1)S(1)}, u32[]{:S(2)}, u32[]{:S(2)}) collective-permute-start(bf16[224,256]{1,0:T(8,128)(2,1)S(1)} %collective-permute-done.9), channel_id=1, source_target_pairs={{0,1},{1,2},{2,3},{3,4},{4,5},{5,6},{6,7},{7,8},{8,9},{9,10},{10,1... | collective-permute-start | bytes 344072 | tf_op jit(solution)/shard_map/ppermute | solution.py:132
  50.7 4.8 %collective-permute-start.4 = (bf16[224,256]{1,0:T(8,128)(2,1)S(1)}, bf16[224,256]{1,0:T(8,128)(2,1)S(1)}, u32[]{:S(2)}, u32[]{:S(2)}) collective-permute-start(bf16[224,256]{1,0:T(8,128)(2,1)S(1)} %collective-permute-done.3), channel_id=1, source_target_pairs={{0,47},{1,0},{2,1},{3,2},{4,3},{5,4},{6,5},{7,6},{8,7},{9,8},{10,9... | collective-permute-start | bytes 344072 | tf_op jit(solution)/shard_map/ppermute | solution.py:135
  55.4 1.9 %collective-permute-start.11 = (bf16[224,256]{1,0:T(8,128)(2,1)S(1)}, bf16[224,256]{1,0:T(8,128)(2,1)S(1)}, u32[]{:S(2)}, u32[]{:S(2)}) collective-permute-start(bf16[224,256]{1,0:T(8,128)(2,1)S(1)} %collective-permute-done.10), channel_id=1, source_target_pairs={{0,1},{1,2},{2,3},{3,4},{4,5},{5,6},{6,7},{7,8},{8,9},{9,10},{10,1... | collective-permute-start | bytes 344072 | tf_op jit(solution)/shard_map/ppermute | solution.py:132
  57.4 4.8 %collective-permute-start.5 = (bf16[224,256]{1,0:T(8,128)(2,1)S(1)}, bf16[224,256]{1,0:T(8,128)(2,1)S(1)}, u32[]{:S(2)}, u32[]{:S(2)}) collective-permute-start(bf16[224,256]{1,0:T(8,128)(2,1)S(1)} %collective-permute-done.4), channel_id=1, source_target_pairs={{0,47},{1,0},{2,1},{3,2},{4,3},{5,4},{6,5},{7,6},{8,7},{9,8},{10,9... | collective-permute-start | bytes 344072 | tf_op jit(solution)/shard_map/ppermute | solution.py:135
  62.2 1.9 %collective-permute-start.12 = (bf16[224,256]{1,0:T(8,128)(2,1)S(1)}, bf16[224,256]{1,0:T(8,128)(2,1)S(1)}, u32[]{:S(2)}, u32[]{:S(2)}) collective-permute-start(bf16[224,256]{1,0:T(8,128)(2,1)S(1)} %collective-permute-done.11), channel_id=1, source_target_pairs={{0,1},{1,2},{2,3},{3,4},{4,5},{5,6},{6,7},{7,8},{8,9},{9,10},{10,1... | collective-permute-start | bytes 344072 | tf_op jit(solution)/shard_map/ppermute | solution.py:132
  64.1 4.8 %collective-permute-start.6 = (bf16[224,256]{1,0:T(8,128)(2,1)S(1)}, bf16[224,256]{1,0:T(8,128)(2,1)S(1)}, u32[]{:S(2)}, u32[]{:S(2)}) collective-permute-start(bf16[224,256]{1,0:T(8,128)(2,1)S(1)} %collective-permute-done.5), channel_id=1, source_target_pairs={{0,47},{1,0},{2,1},{3,2},{4,3},{5,4},{6,5},{7,6},{8,7},{9,8},{10,9... | collective-permute-start | bytes 344072 | tf_op jit(solution)/shard_map/ppermute | solution.py:135
  68.9 1.9 %collective-permute-start.13 = (bf16[224,256]{1,0:T(8,128)(2,1)S(1)}, bf16[224,256]{1,0:T(8,128)(2,1)S(1)}, u32[]{:S(2)}, u32[]{:S(2)}) collective-permute-start(bf16[224,256]{1,0:T(8,128)(2,1)S(1)} %collective-permute-done.12), channel_id=1, source_target_pairs={{0,1},{1,2},{2,3},{3,4},{4,5},{5,6},{6,7},{7,8},{8,9},{9,10},{10,1... | collective-permute-start | bytes 344072 | tf_op jit(solution)/shard_map/ppermute | solution.py:132
  70.9 4.8 %collective-permute-start.7 = (bf16[224,256]{1,0:T(8,128)(2,1)S(1)}, bf16[224,256]{1,0:T(8,128)(2,1)S(1)}, u32[]{:S(2)}, u32[]{:S(2)}) collective-permute-start(bf16[224,256]{1,0:T(8,128)(2,1)S(1)} %collective-permute-done.6), channel_id=1, source_target_pairs={{0,47},{1,0},{2,1},{3,2},{4,3},{5,4},{6,5},{7,6},{8,7},{9,8},{10,9... | collective-permute-start | bytes 344072 | tf_op jit(solution)/shard_map/ppermute | solution.py:135
  75.7 1.9 %collective-permute-start.14 = (bf16[224,256]{1,0:T(8,128)(2,1)S(1)}, bf16[224,256]{1,0:T(8,128)(2,1)S(1)}, u32[]{:S(2)}, u32[]{:S(2)}) collective-permute-start(bf16[224,256]{1,0:T(8,128)(2,1)S(1)} %collective-permute-done.13), channel_id=1, source_target_pairs={{0,1},{1,2},{2,3},{3,4},{4,5},{5,6},{6,7},{7,8},{8,9},{9,10},{10,1... | collective-permute-start | bytes 344072 | tf_op jit(solution)/shard_map/ppermute | solution.py:132
  77.6 4.8 %collective-permute-done.14 = bf16[224,256]{1,0:T(8,128)(2,1)S(1)} collective-permute-done((bf16[224,256]{1,0:T(8,128)(2,1)S(1)}, bf16[224,256]{1,0:T(8,128)(2,1)S(1)}, u32[]{:S(2)}, u32[]{:S(2)}) %collective-permute-start.14) | collective-permute-done | bytes 114720 | tf_op jit(solution)/shard_map/ppermute | solution.py:132
  82.4 1.9 %collective-permute-start.15 = (bf16[224,256]{1,0:T(8,128)(2,1)S(1)}, bf16[224,256]{1,0:T(8,128)(2,1)S(1)}, u32[]{:S(2)}, u32[]{:S(2)}) collective-permute-start(bf16[224,256]{1,0:T(8,128)(2,1)S(1)} %collective-permute-done.14), channel_id=1, source_target_pairs={{0,1},{1,2},{2,3},{3,4},{4,5},{5,6},{6,7},{7,8},{8,9},{9,10},{10,1... | collective-permute-start | bytes 344072 | tf_op jit(solution)/shard_map/ppermute | solution.py:132
  84.4 6.2 %collective-permute-done.15 = bf16[224,256]{1,0:T(8,128)(2,1)S(1)} collective-permute-done((bf16[224,256]{1,0:T(8,128)(2,1)S(1)}, bf16[224,256]{1,0:T(8,128)(2,1)S(1)}, u32[]{:S(2)}, u32[]{:S(2)}) %collective-permute-start.15) | collective-permute-done | bytes 114720 | tf_op jit(solution)/shard_map/ppermute | solution.py:132
  90.7 3.1 %fusion.70 = (bf16[2,2,64,256]{3,2,1,0:T(8,128)(2,1)S(1)}, f32[2,2,64,256]{3,2,1,0:T(8,128)S(1)}) fusion(bf16[3584,256]{1,0:T(8,128)(2,1)S(1)} %constant_dynamic-update-slice_fusion, s32[]{:T(128)S(6)} %select_n.126, bf16[1,2,64,3584]{3,2,1,0:T(8,128)(2,1)} %bitcast.151, bf16[1,2,64,3584]{3,2,1,0:T(8,128)(2,1)} %bitcast.2), kind=kOutput, calls=%fused_computation.160 | convolution fusion | flops 477167616 | bytes 4063236 | tf_op jit(solution)/shard_map/bctd,de->bcte/dot_general | solution.py:149
  95.2 6.9 %all-to-all-start = ((bf16[16,2,64,256]{3,2,1,0:T(8,128)(2,1)}), bf16[16,2,64,256]{3,2,1,0:T(8,128)(2,1)S(1)}, u32[]{:S(2)}, u32[]{:S(2)}) async-start(bf16[16,2,64,256]{3,2,1,0:T(8,128)(2,1)} %broadcast_in_dim.115), calls=%async_computation | async-start | bytes 2097152 | tf_op jit(solution)/shard_map/all_to_all | solution.py:179
  105.2 12.0 %collective-permute-start.17 = (bf16[2,64,256]{2,1,0:T(8,128)(2,1)S(1)}, bf16[2,64,256]{2,1,0:T(8,128)(2,1)S(1)}, u32[]{:S(2)}, u32[]{:S(2)}) collective-permute-start(bf16[2,64,256]{2,1,0:T(8,128)(2,1)S(1)} %pad_maximum_fusion), channel_id=1, source_target_pairs={{0,32},{32,0},{1,33},{33,1},{2,34},{34,2},{3,35},{35,3},{4,36},{36... | collective-permute-start | bytes 196616 | tf_op jit(solution)/shard_map/ppermute | solution.py:102
  117.7 11.5 %collective-permute-done.17 = bf16[2,64,256]{2,1,0:T(8,128)(2,1)S(1)} collective-permute-done((bf16[2,64,256]{2,1,0:T(8,128)(2,1)S(1)}, bf16[2,64,256]{2,1,0:T(8,128)(2,1)S(1)}, u32[]{:S(2)}, u32[]{:S(2)}) %collective-permute-start.17) | collective-permute-done | bytes 65568 | tf_op jit(solution)/shard_map/ppermute | solution.py:102
  130.4 6.7 %all-to-all-start.1 = ((bf16[16,2,64,256]{3,2,1,0:T(8,128)(2,1)}), bf16[16,2,64,256]{3,2,1,0:T(8,128)(2,1)}, u32[]{:S(2)}, u32[]{:S(2)}) async-start(bf16[16,2,64,256]{3,2,1,0:T(8,128)(2,1)} %broadcast_in_dim.117), calls=%async_computation.1 | async-start | bytes 2097152 | tf_op jit(solution)/shard_map/all_to_all | solution.py:179
  138.7 18.0 %while.30 = (s32[]{:T(128)}, f32[2,7,128]{2,1,0:T(8,128)S(1)}, f32[2,7,128]{2,1,0:T(8,128)S(1)}, f32[2,7,128,128]{3,2,1,0:T(8,128)}, s32[]{:T(128)}, /*index=5*/...) while((s32[]{:T(128)}, f32[2,7,128]{2,1,0:T(8,128)S(1)}, ...), condition=%wide.region_8.9_spmd.clone, body=%wide.region_5.8_spmd.clone.sunk | while | flops 482283264 | bytes 22082404 | solution.py:198
  145.4 1.4 fusion.89
  154.3 1.4 fusion.89
  156.7 1.8 gather_fusion.5
  158.6 14.2 %while.31 = (s32[]{:T(128)}, f32[2,7,128]{2,1,0:T(8,128)S(1)}, f32[2,7,128]{2,1,0:T(8,128)S(1)}, f32[2,7,128,128]{3,2,1,0:T(8,128)S(1)}, s32[]{:T(128)}, /*index...) while((s32[]{:T(128)}, f32[2,7,128]{2,1,0:T(8,128)S(1)}, ...), condition=%wide.region_15.16_spmd.clone, body=%wide.region_12.15_spmd.clone.sunk | while | flops 482283264 | bytes 14742315 | solution.py:198
  172.9 2.8 %fusion.42 = bf16[2,128,7,128]{3,1,2,0:T(8,128)(2,1)S(1)} fusion(f32[2,7,128,128]{3,2,1,0:T(8,128)S(1)} %get-tuple-element.112, f32[2,7,128,128]{3,2,1,0:T(8,128)} %get-tuple-element.109, f32[2,7,128]{2,1,0:T(8,128)S(1)} %get-tuple-element.209, f32[2,7,128]{2,1,0:T(8,128)S(1)} %get-tuple-element.211, f32[2,7,128]{2,1,0:T(8,128)S(1)} %get-tuple-element.210, ...), kind=kOutput, calls=%fused_computation.62 | convolution fusion | flops 31768576 | bytes 2843136 | tf_op jit(solution)/shard_map/vmap(ptu,ud->ptd)/dot_general | solution.py:42
  176.2 12.3 %collective-permute-start.18 = (bf16[2,64,896]{2,1,0:T(8,128)(2,1)S(1)}, bf16[2,64,896]{2,1,0:T(8,128)(2,1)S(1)}, u32[]{:S(2)}, u32[]{:S(2)}) collective-permute-start(bf16[2,64,896]{2,1,0:T(8,128)(2,1)S(1)} %squeeze.47), channel_id=1, source_target_pairs={{0,16},{16,0},{1,17},{17,1},{2,18},{18,2},{3,19},{19,3},{4,20},{20... | collective-permute-start | bytes 688136 | tf_op jit(solution)/shard_map/ppermute | solution.py:102
  (215 shorter events, 46.5 us)
Async XLA Ops:
  0.0 29.3 %copy-start = (s32[1,64]{1,0:T(1,128)S(1)}, s32[1,64]{1,0:T(1,128)}, u32[]{:S(2)}) copy-start(s32[1,64]{1,0:T(1,128)} %param.11) | copy-start | bytes 772
  0.9 35.6 %collective-permute-start.1 = (bf16[224,256]{1,0:T(8,128)(2,1)S(1)}, bf16[224,256]{1,0:T(8,128)(2,1)S(1)}, u32[]{:S(2)}, u32[]{:S(2)}) collective-permute-start(bf16[224,256]{1,0:T(8,128)(2,1)S(1)} %get-tuple-element.213), channel_id=1, source_target_pairs={{0,47},{1,0},{2,1},{3,2},{4,3},{5,4},{6,5},{7,6},{8,7},{9,8},{10,9... | collective-permute-start | bytes 344072 | tf_op jit(solution)/shard_map/ppermute | solution.py:135
  19.3 22.0 %collective-permute-start.8 = (bf16[224,256]{1,0:T(8,128)(2,1)S(1)}, bf16[224,256]{1,0:T(8,128)(2,1)S(1)}, u32[]{:S(2)}, u32[]{:S(2)}) collective-permute-start(bf16[224,256]{1,0:T(8,128)(2,1)S(1)} %get-tuple-element.213), channel_id=1, source_target_pairs={{0,1},{1,2},{2,3},{3,4},{4,5},{5,6},{6,7},{7,8},{8,9},{9,10},{10,1... | collective-permute-start | bytes 344072 | tf_op jit(solution)/shard_map/ppermute | solution.py:132
  21.3 69.4 %collective-permute-start = (bf16[2,64,3584]{2,1,0:T(8,128)(2,1)}, bf16[2,64,3584]{2,1,0:T(8,128)(2,1)}, u32[]{:S(2)}, u32[]{:S(2)}) collective-permute-start(bf16[2,64,3584]{2,1,0:T(8,128)(2,1)} %bitcast.150), channel_id=1, source_target_pairs={{0,16},{16,0},{1,17},{17,1},{2,18},{18,2},{3,19},{19,3},{4,20},{20... | collective-permute-start | bytes 2752520 | tf_op jit(solution)/shard_map/ppermute | solution.py:102
  27.2 77.6 %collective-permute-start.16 = (bf16[2,64,896]{2,1,0:T(8,128)(2,1)S(1)}, bf16[2,64,896]{2,1,0:T(8,128)(2,1)S(1)}, u32[]{:S(2)}, u32[]{:S(2)}) collective-permute-start(bf16[2,64,896]{2,1,0:T(8,128)(2,1)S(1)} %bitcast.147), channel_id=1, source_target_pairs={{0,16},{16,0},{1,17},{17,1},{2,18},{18,2},{3,19},{19,3},{4,20},{20... | collective-permute-start | bytes 688136 | tf_op jit(solution)/shard_map/ppermute | solution.py:102
  36.5 6.8 %collective-permute-start.2 = (bf16[224,256]{1,0:T(8,128)(2,1)S(1)}, bf16[224,256]{1,0:T(8,128)(2,1)S(1)}, u32[]{:S(2)}, u32[]{:S(2)}) collective-permute-start(bf16[224,256]{1,0:T(8,128)(2,1)S(1)} %collective-permute-done.1), channel_id=1, source_target_pairs={{0,47},{1,0},{2,1},{3,2},{4,3},{5,4},{6,5},{7,6},{8,7},{9,8},{10,9... | collective-permute-start | bytes 344072 | tf_op jit(solution)/shard_map/ppermute | solution.py:135
  41.4 7.3 %collective-permute-start.9 = (bf16[224,256]{1,0:T(8,128)(2,1)S(1)}, bf16[224,256]{1,0:T(8,128)(2,1)S(1)}, u32[]{:S(2)}, u32[]{:S(2)}) collective-permute-start(bf16[224,256]{1,0:T(8,128)(2,1)S(1)} %collective-permute-done.8), channel_id=1, source_target_pairs={{0,1},{1,2},{2,3},{3,4},{4,5},{5,6},{6,7},{7,8},{8,9},{9,10},{10,1... | collective-permute-start | bytes 344072 | tf_op jit(solution)/shard_map/ppermute | solution.py:132
  43.4 7.3 %collective-permute-start.3 = (bf16[224,256]{1,0:T(8,128)(2,1)S(1)}, bf16[224,256]{1,0:T(8,128)(2,1)S(1)}, u32[]{:S(2)}, u32[]{:S(2)}) collective-permute-start(bf16[224,256]{1,0:T(8,128)(2,1)S(1)} %collective-permute-done.2), channel_id=1, source_target_pairs={{0,47},{1,0},{2,1},{3,2},{4,3},{5,4},{6,5},{7,6},{8,7},{9,8},{10,9... | collective-permute-start | bytes 344072 | tf_op jit(solution)/shard_map/ppermute | solution.py:135
  48.7 6.7 %collective-permute-start.10 = (bf16[224,256]{1,0:T(8,128)(2,1)S(1)}, bf16[224,256]{1,0:T(8,128)(2,1)S(1)}, u32[]{:S(2)}, u32[]{:S(2)}) collective-permute-start(bf16[224,256]{1,0:T(8,128)(2,1)S(1)} %collective-permute-done.9), channel_id=1, source_target_pairs={{0,1},{1,2},{2,3},{3,4},{4,5},{5,6},{6,7},{7,8},{8,9},{9,10},{10,1... | collective-permute-start | bytes 344072 | tf_op jit(solution)/shard_map/ppermute | solution.py:132
  50.7 6.7 %collective-permute-start.4 = (bf16[224,256]{1,0:T(8,128)(2,1)S(1)}, bf16[224,256]{1,0:T(8,128)(2,1)S(1)}, u32[]{:S(2)}, u32[]{:S(2)}) collective-permute-start(bf16[224,256]{1,0:T(8,128)(2,1)S(1)} %collective-permute-done.3), channel_id=1, source_target_pairs={{0,47},{1,0},{2,1},{3,2},{4,3},{5,4},{6,5},{7,6},{8,7},{9,8},{10,9... | collective-permute-start | bytes 344072 | tf_op jit(solution)/shard_map/ppermute | solution.py:135
  55.4 6.7 %collective-permute-start.11 = (bf16[224,256]{1,0:T(8,128)(2,1)S(1)}, bf16[224,256]{1,0:T(8,128)(2,1)S(1)}, u32[]{:S(2)}, u32[]{:S(2)}) collective-permute-start(bf16[224,256]{1,0:T(8,128)(2,1)S(1)} %collective-permute-done.10), channel_id=1, source_target_pairs={{0,1},{1,2},{2,3},{3,4},{4,5},{5,6},{6,7},{7,8},{8,9},{9,10},{10,1... | collective-permute-start | bytes 344072 | tf_op jit(solution)/shard_map/ppermute | solution.py:132
  57.4 6.7 %collective-permute-start.5 = (bf16[224,256]{1,0:T(8,128)(2,1)S(1)}, bf16[224,256]{1,0:T(8,128)(2,1)S(1)}, u32[]{:S(2)}, u32[]{:S(2)}) collective-permute-start(bf16[224,256]{1,0:T(8,128)(2,1)S(1)} %collective-permute-done.4), channel_id=1, source_target_pairs={{0,47},{1,0},{2,1},{3,2},{4,3},{5,4},{6,5},{7,6},{8,7},{9,8},{10,9... | collective-permute-start | bytes 344072 | tf_op jit(solution)/shard_map/ppermute | solution.py:135
  62.2 6.7 %collective-permute-start.12 = (bf16[224,256]{1,0:T(8,128)(2,1)S(1)}, bf16[224,256]{1,0:T(8,128)(2,1)S(1)}, u32[]{:S(2)}, u32[]{:S(2)}) collective-permute-start(bf16[224,256]{1,0:T(8,128)(2,1)S(1)} %collective-permute-done.11), channel_id=1, source_target_pairs={{0,1},{1,2},{2,3},{3,4},{4,5},{5,6},{6,7},{7,8},{8,9},{9,10},{10,1... | collective-permute-start | bytes 344072 | tf_op jit(solution)/shard_map/ppermute | solution.py:132
  64.1 6.7 %collective-permute-start.6 = (bf16[224,256]{1,0:T(8,128)(2,1)S(1)}, bf16[224,256]{1,0:T(8,128)(2,1)S(1)}, u32[]{:S(2)}, u32[]{:S(2)}) collective-permute-start(bf16[224,256]{1,0:T(8,128)(2,1)S(1)} %collective-permute-done.5), channel_id=1, source_target_pairs={{0,47},{1,0},{2,1},{3,2},{4,3},{5,4},{6,5},{7,6},{8,7},{9,8},{10,9... | collective-permute-start | bytes 344072 | tf_op jit(solution)/shard_map/ppermute | solution.py:135
  68.9 6.7 %collective-permute-start.13 = (bf16[224,256]{1,0:T(8,128)(2,1)S(1)}, bf16[224,256]{1,0:T(8,128)(2,1)S(1)}, u32[]{:S(2)}, u32[]{:S(2)}) collective-permute-start(bf16[224,256]{1,0:T(8,128)(2,1)S(1)} %collective-permute-done.12), channel_id=1, source_target_pairs={{0,1},{1,2},{2,3},{3,4},{4,5},{5,6},{6,7},{7,8},{8,9},{9,10},{10,1... | collective-permute-start | bytes 344072 | tf_op jit(solution)/shard_map/ppermute | solution.py:132
  70.9 13.5 %collective-permute-start.7 = (bf16[224,256]{1,0:T(8,128)(2,1)S(1)}, bf16[224,256]{1,0:T(8,128)(2,1)S(1)}, u32[]{:S(2)}, u32[]{:S(2)}) collective-permute-start(bf16[224,256]{1,0:T(8,128)(2,1)S(1)} %collective-permute-done.6), channel_id=1, source_target_pairs={{0,47},{1,0},{2,1},{3,2},{4,3},{5,4},{6,5},{7,6},{8,7},{9,8},{10,9... | collective-permute-start | bytes 344072 | tf_op jit(solution)/shard_map/ppermute | solution.py:135
  75.7 6.8 %collective-permute-start.14 = (bf16[224,256]{1,0:T(8,128)(2,1)S(1)}, bf16[224,256]{1,0:T(8,128)(2,1)S(1)}, u32[]{:S(2)}, u32[]{:S(2)}) collective-permute-start(bf16[224,256]{1,0:T(8,128)(2,1)S(1)} %collective-permute-done.13), channel_id=1, source_target_pairs={{0,1},{1,2},{2,3},{3,4},{4,5},{5,6},{6,7},{7,8},{8,9},{9,10},{10,1... | collective-permute-start | bytes 344072 | tf_op jit(solution)/shard_map/ppermute | solution.py:132
  82.4 8.1 %collective-permute-start.15 = (bf16[224,256]{1,0:T(8,128)(2,1)S(1)}, bf16[224,256]{1,0:T(8,128)(2,1)S(1)}, u32[]{:S(2)}, u32[]{:S(2)}) collective-permute-start(bf16[224,256]{1,0:T(8,128)(2,1)S(1)} %collective-permute-done.14), channel_id=1, source_target_pairs={{0,1},{1,2},{2,3},{3,4},{4,5},{5,6},{6,7},{7,8},{8,9},{9,10},{10,1... | collective-permute-start | bytes 344072 | tf_op jit(solution)/shard_map/ppermute | solution.py:132
  95.2 34.0 %all-to-all-start = ((bf16[16,2,64,256]{3,2,1,0:T(8,128)(2,1)}), bf16[16,2,64,256]{3,2,1,0:T(8,128)(2,1)S(1)}, u32[]{:S(2)}, u32[]{:S(2)}) async-start(bf16[16,2,64,256]{3,2,1,0:T(8,128)(2,1)} %broadcast_in_dim.115), calls=%async_computation | async-start | bytes 2097152 | tf_op jit(solution)/shard_map/all_to_all | solution.py:179
  105.2 33.5 %copy-start.3 = (s32[128]{0:T(128)S(1)}, s32[128]{0:T(128)}, u32[]{:S(2)}) copy-start(s32[128]{0:T(128)} %constant.177.clone.1) | copy-start | bytes 1540
  105.2 24.0 %collective-permute-start.17 = (bf16[2,64,256]{2,1,0:T(8,128)(2,1)S(1)}, bf16[2,64,256]{2,1,0:T(8,128)(2,1)S(1)}, u32[]{:S(2)}, u32[]{:S(2)}) collective-permute-start(bf16[2,64,256]{2,1,0:T(8,128)(2,1)S(1)} %pad_maximum_fusion), channel_id=1, source_target_pairs={{0,32},{32,0},{1,33},{33,1},{2,34},{34,2},{3,35},{35,3},{4,36},{36... | collective-permute-start | bytes 196616 | tf_op jit(solution)/shard_map/ppermute | solution.py:102
  130.4 26.3 %all-to-all-start.1 = ((bf16[16,2,64,256]{3,2,1,0:T(8,128)(2,1)}), bf16[16,2,64,256]{3,2,1,0:T(8,128)(2,1)}, u32[]{:S(2)}, u32[]{:S(2)}) async-start(bf16[16,2,64,256]{3,2,1,0:T(8,128)(2,1)} %broadcast_in_dim.117), calls=%async_computation.1 | async-start | bytes 2097152 | tf_op jit(solution)/shard_map/all_to_all | solution.py:179
  139.2 1.7 copy-start.1
  142.3 0.9 copy-start.2
  143.7 1.7 copy-start.1
  146.8 0.9 copy-start.2
  148.2 1.7 copy-start.1
  151.3 0.9 copy-start.2
  152.7 1.7 copy-start.1
  155.8 0.9 copy-start.2
  176.2 13.4 %collective-permute-start.18 = (bf16[2,64,896]{2,1,0:T(8,128)(2,1)S(1)}, bf16[2,64,896]{2,1,0:T(8,128)(2,1)S(1)}, u32[]{:S(2)}, u32[]{:S(2)}) collective-permute-start(bf16[2,64,896]{2,1,0:T(8,128)(2,1)S(1)} %squeeze.47), channel_id=1, source_target_pairs={{0,16},{16,0},{1,17},{17,1},{2,18},{18,2},{3,19},{19,3},{4,20},{20... | collective-permute-start | bytes 688136 | tf_op jit(solution)/shard_map/ppermute | solution.py:102

commit v4 on v2

--- a/solution.py
+++ b/solution.py
@@ -175,12 +175,17 @@
         blocks = jnp.swapaxes(every_block[side], 0, 1).reshape(-1, 4, 2)
         spread = jnp.broadcast_to(rows[None], (16,) + rows.shape)
         gathered = lax.all_to_all(spread, ("x", "y"), 0, 0, tiled=True).reshape(-1, 4, *rows.shape)
+
+        def one_part(part, fold_carry):
+            return absorb_chunk(
+                fold_carry, query_rows,
+                lax.dynamic_index_in_dim(gathered, part, 0, keepdims=False),
+                lax.dynamic_index_in_dim(blocks, part, 0, keepdims=False),
+                row_limit, score_scale,
+            )
+
         fold_carry = empty_state(2, group_size, rows_all, head_dim)
-        for part in range(gathered.shape[0]):
-            fold_carry = absorb_chunk(
-                fold_carry, query_rows, gathered[part], blocks[part], row_limit, score_scale
-            )
-        return fold_carry
+        return lax.fori_loop(0, gathered.shape[0], one_part, fold_carry)
 
     noisy_ok = jnp.broadcast_to((jnp.arange(rows_all) >= block_len)[:, None], (rows_all, block_len))
     noisy_state = jax.vmap(absorb, in_axes=(0, 0, 0, 0, None, None))(

time: 186 us -> 221 us (1.19)
  matrix products: 22.2 us -> 44.7 us
  other arithmetic: 11.9 us -> 28.4 us
  local copies, waits for them, and re-layouts: 25.7 us -> 16.5 us
  waiting for transfers between devices: 15.9 us -> 23.3 us
    reduce_sum x9, other arithmetic: 8.01 us -> 24.8 us  [absorb(): denominator = denominator * factor + jnp.sum(weights, axis=-1)]
    dot_general x9, matrix products: 5.97 us -> 20.3 us  [absorb(): jnp.einsum('tpd,ud->ptu', query_rows, key_part, preferred_element_type=jn...]
    unnamed x89 -> x23, local copies, waits for them, and re-layouts: 14.4 us -> 1.78 us
    dot_general x9, matrix products: 12.5 us -> 21.2 us  [absorb(): jnp.einsum('ptu,ud->ptd', weights.astype(jnp.bfloat16), value_part, prefe...]
    ppermute x8, waiting for transfers between devices: 4.32 us -> 11.1 us  [local(): going_up = lax.ppermute(going_up, ('zh', 'fsdp'), forward)]
    ppermute x7, starting transfers between devices: 44.2 us -> 48.4 us  [local(): going_down = lax.ppermute(going_down, ('zh', 'fsdp'), backward)]
    ppermute x4, waiting for transfers between devices: 8.04 us -> 12.2 us  [swap(): return lax.ppermute(value, axis, [(0, 1), (1, 0)])]
    while x0 -> x40, local copies, waits for them, and re-layouts: none -> 3.95 us
  transfers between devices with their start and end apart: 21 -> 21, of which waited for: 5 -> 4; matrix products, arithmetic and copies ran while one was open for 18% -> 22% of each run, Pallas kernels for 0% -> 0%
where the time goes in v4:
time: 221 us; the launch traced here: 220 us
  starting transfers between devices  106 us (48%)
  matrix products  44.7 us (20%)
  other arithmetic  28.4 us (13%)
  waiting for transfers between devices  23.3 us (11%)
  local copies, waits for them, and re-layouts  16.5 us (7%)
    ppermute x7, starting transfers between devices, local(): going_down = lax.ppermute(going_down, ('zh', 'fsdp'), backward)  48.4 us
    ppermute x4, starting transfers between devices, swap(): return lax.ppermute(value, axis, [(0, 1), (1, 0)])  28.9 us
    reduce_sum x9, other arithmetic, absorb(): denominator = denominator * factor + jnp.sum(weights, axis=-1)  24.8 us
    dot_general x9, matrix products, absorb(): jnp.einsum('ptu,ud->ptd', weights.astype(jnp.bfloat16), value_part, prefe...  21.2 us
    dot_general x9, matrix products, absorb(): jnp.einsum('tpd,ud->ptu', query_rows, key_part, preferred_element_type=jn...  20.3 us
    ppermute x8, starting transfers between devices, local(): going_up = lax.ppermute(going_up, ('zh', 'fsdp'), forward)  15.3 us
    all_to_all x2, starting transfers between devices, chain(): lax.all_to_all(spread, ('x', 'y'), 0, 0, tiled=True)  13.6 us
    ppermute x4, waiting for transfers between devices, swap(): return lax.ppermute(value, axis, [(0, 1), (1, 0)])  12.2 us
  transfers between devices with their start and end apart: 21, of which 4 were waited for; matrix products, arithmetic and copies ran while one was open for 22% of the time, Pallas kernels for 0%

profile of v4, /device:TPU:1, one launch (start us, length us, event | category | flops | bytes accessed | tf_op | source)
XLA Modules:
  0.0 220.2 jit_solution(6352913388643424662)
XLA Ops:
  0.9 19.2 %collective-permute-start.1 = (bf16[224,256]{1,0:T(8,128)(2,1)S(1)}, bf16[224,256]{1,0:T(8,128)(2,1)S(1)}, u32[]{:S(2)}, u32[]{:S(2)}) collective-permute-start(bf16[224,256]{1,0:T(8,128)(2,1)S(1)} %get-tuple-element.459), channel_id=1, source_target_pairs={{0,47},{1,0},{2,1},{3,2},{4,3},{5,4},{6,5},{7,6},{8,7},{9,8},{10,9... | collective-permute-start | bytes 344072 | tf_op jit(solution)/shard_map/ppermute | solution.py:135
  22.1 2.9 %collective-permute-start = (bf16[2,64,3584]{2,1,0:T(8,128)(2,1)}, bf16[2,64,3584]{2,1,0:T(8,128)(2,1)}, u32[]{:S(2)}, u32[]{:S(2)}) collective-permute-start(bf16[2,64,3584]{2,1,0:T(8,128)(2,1)} %bitcast.157), channel_id=1, source_target_pairs={{0,16},{16,0},{1,17},{17,1},{2,18},{18,2},{3,19},{19,3},{4,20},{20... | collective-permute-start | bytes 2752520 | tf_op jit(solution)/shard_map/ppermute | solution.py:102
  32.6 4.9 %collective-permute-start.2 = (bf16[224,256]{1,0:T(8,128)(2,1)S(1)}, bf16[224,256]{1,0:T(8,128)(2,1)S(1)}, u32[]{:S(2)}, u32[]{:S(2)}) collective-permute-start(bf16[224,256]{1,0:T(8,128)(2,1)S(1)} %collective-permute-done.1), channel_id=1, source_target_pairs={{0,47},{1,0},{2,1},{3,2},{4,3},{5,4},{6,5},{7,6},{8,7},{9,8},{10,9... | collective-permute-start | bytes 344072 | tf_op jit(solution)/shard_map/ppermute | solution.py:135
  39.5 5.3 %collective-permute-start.3 = (bf16[224,256]{1,0:T(8,128)(2,1)S(1)}, bf16[224,256]{1,0:T(8,128)(2,1)S(1)}, u32[]{:S(2)}, u32[]{:S(2)}) collective-permute-start(bf16[224,256]{1,0:T(8,128)(2,1)S(1)} %collective-permute-done.2), channel_id=1, source_target_pairs={{0,47},{1,0},{2,1},{3,2},{4,3},{5,4},{6,5},{7,6},{8,7},{9,8},{10,9... | collective-permute-start | bytes 344072 | tf_op jit(solution)/shard_map/ppermute | solution.py:135
  46.7 4.8 %collective-permute-start.4 = (bf16[224,256]{1,0:T(8,128)(2,1)S(1)}, bf16[224,256]{1,0:T(8,128)(2,1)S(1)}, u32[]{:S(2)}, u32[]{:S(2)}) collective-permute-start(bf16[224,256]{1,0:T(8,128)(2,1)S(1)} %collective-permute-done.3), channel_id=1, source_target_pairs={{0,47},{1,0},{2,1},{3,2},{4,3},{5,4},{6,5},{7,6},{8,7},{9,8},{10,9... | collective-permute-start | bytes 344072 | tf_op jit(solution)/shard_map/ppermute | solution.py:135
  53.5 4.8 %collective-permute-start.5 = (bf16[224,256]{1,0:T(8,128)(2,1)S(1)}, bf16[224,256]{1,0:T(8,128)(2,1)S(1)}, u32[]{:S(2)}, u32[]{:S(2)}) collective-permute-start(bf16[224,256]{1,0:T(8,128)(2,1)S(1)} %collective-permute-done.4), channel_id=1, source_target_pairs={{0,47},{1,0},{2,1},{3,2},{4,3},{5,4},{6,5},{7,6},{8,7},{9,8},{10,9... | collective-permute-start | bytes 344072 | tf_op jit(solution)/shard_map/ppermute | solution.py:135
  60.2 4.8 %collective-permute-start.6 = (bf16[224,256]{1,0:T(8,128)(2,1)S(1)}, bf16[224,256]{1,0:T(8,128)(2,1)S(1)}, u32[]{:S(2)}, u32[]{:S(2)}) collective-permute-start(bf16[224,256]{1,0:T(8,128)(2,1)S(1)} %collective-permute-done.5), channel_id=1, source_target_pairs={{0,47},{1,0},{2,1},{3,2},{4,3},{5,4},{6,5},{7,6},{8,7},{9,8},{10,9... | collective-permute-start | bytes 344072 | tf_op jit(solution)/shard_map/ppermute | solution.py:135
  66.9 4.8 %collective-permute-start.7 = (bf16[224,256]{1,0:T(8,128)(2,1)S(1)}, bf16[224,256]{1,0:T(8,128)(2,1)S(1)}, u32[]{:S(2)}, u32[]{:S(2)}) collective-permute-start(bf16[224,256]{1,0:T(8,128)(2,1)S(1)} %collective-permute-done.6), channel_id=1, source_target_pairs={{0,47},{1,0},{2,1},{3,2},{4,3},{5,4},{6,5},{7,6},{8,7},{9,8},{10,9... | collective-permute-start | bytes 344072 | tf_op jit(solution)/shard_map/ppermute | solution.py:135
  73.7 4.8 %collective-permute-done.14 = bf16[224,256]{1,0:T(8,128)(2,1)S(1)} collective-permute-done((bf16[224,256]{1,0:T(8,128)(2,1)S(1)}, bf16[224,256]{1,0:T(8,128)(2,1)S(1)}, u32[]{:S(2)}, u32[]{:S(2)}) %collective-permute-start.14) | collective-permute-done | bytes 114720 | tf_op jit(solution)/shard_map/ppermute | solution.py:132
  80.4 6.2 %collective-permute-done.15 = bf16[224,256]{1,0:T(8,128)(2,1)S(1)} collective-permute-done((bf16[224,256]{1,0:T(8,128)(2,1)S(1)}, bf16[224,256]{1,0:T(8,128)(2,1)S(1)}, u32[]{:S(2)}, u32[]{:S(2)}) %collective-permute-start.15) | collective-permute-done | bytes 114720 | tf_op jit(solution)/shard_map/ppermute | solution.py:132
  86.7 3.2 %fusion.72 = (bf16[2,2,64,256]{3,2,1,0:T(8,128)(2,1)S(1)}, f32[2,2,64,256]{3,2,1,0:T(8,128)S(1)}) fusion(bf16[3584,256]{1,0:T(8,128)(2,1)S(1)} %constant_dynamic-update-slice_fusion, s32[]{:T(128)S(6)} %select_n.127, bf16[1,2,64,3584]{3,2,1,0:T(8,128)(2,1)} %bitcast.158, bf16[1,2,64,3584]{3,2,1,0:T(8,128)(2,1)} %bitcast.2), kind=kOutput, calls=%fused_computation.152 | convolution fusion | flops 477167616 | bytes 4063236 | tf_op jit(solution)/shard_map/bctd,de->bcte/dot_general | solution.py:149
  92.0 6.9 %all-to-all-start = ((bf16[16,2,64,256]{3,2,1,0:T(8,128)(2,1)}), bf16[16,2,64,256]{3,2,1,0:T(8,128)(2,1)S(1)}, u32[]{:S(2)}, u32[]{:S(2)}) async-start(bf16[16,2,64,256]{3,2,1,0:T(8,128)(2,1)} %broadcast_in_dim.162), calls=%async_computation | async-start | bytes 2097152 | tf_op jit(solution)/shard_map/all_to_all | solution.py:177
  99.5 12.0 %collective-permute-start.17 = (bf16[2,64,256]{2,1,0:T(8,128)(2,1)S(1)}, bf16[2,64,256]{2,1,0:T(8,128)(2,1)S(1)}, u32[]{:S(2)}, u32[]{:S(2)}) collective-permute-start(bf16[2,64,256]{2,1,0:T(8,128)(2,1)S(1)} %pad_maximum_fusion), channel_id=1, source_target_pairs={{0,32},{32,0},{1,33},{33,1},{2,34},{34,2},{3,35},{35,3},{4,36},{36... | collective-permute-start | bytes 196616 | tf_op jit(solution)/shard_map/ppermute | solution.py:102
  112.0 11.5 %collective-permute-done.17 = bf16[2,64,256]{2,1,0:T(8,128)(2,1)S(1)} collective-permute-done((bf16[2,64,256]{2,1,0:T(8,128)(2,1)S(1)}, bf16[2,64,256]{2,1,0:T(8,128)(2,1)S(1)}, u32[]{:S(2)}, u32[]{:S(2)}) %collective-permute-start.17) | collective-permute-done | bytes 65568 | tf_op jit(solution)/shard_map/ppermute | solution.py:102
  124.6 6.7 %all-to-all-start.1 = ((bf16[16,2,64,256]{3,2,1,0:T(8,128)(2,1)}), bf16[16,2,64,256]{3,2,1,0:T(8,128)(2,1)S(1)}, u32[]{:S(2)}, u32[]{:S(2)}) async-start(bf16[16,2,64,256]{3,2,1,0:T(8,128)(2,1)} %broadcast_in_dim.163), calls=%async_computation.1 | async-start | bytes 2097152 | tf_op jit(solution)/shard_map/all_to_all | solution.py:177
  131.3 37.1 %while.36 = (s32[]{:T(128)}, f32[2,7,128]{2,1,0:T(8,128)S(1)}, f32[2,7,128]{2,1,0:T(8,128)S(1)}, f32[2,7,128,128]{3,2,1,0:T(8,128)}, s32[4,4,2]{2,0,1:T(4,128)S(...) while((s32[]{:T(128)}, f32[2,7,128]{2,1,0:T(8,128)S(1)}, ...), condition=%wide.region_4.5_spmd.clone, body=%wide.region_1.4_spmd.clone.sunk | while | flops 482518016 | bytes 29422412 | solution.py:188
  134.3 3.1 %fusion.92 = f32[2,7,128]{2,1,0:T(8,128)S(1)} fusion(f32[512,2,128,7]{2,0,3,1:T(8,128)} %get-tuple-element.597, f32[2,7,128]{2,1,0:T(8,128)S(1)} %select_maximum_fusion.4, pred[2,128,512]{1,2,0:T(8,128)(4,1)S(1)} %broadcast_compare_fusion.4), kind=kLoop, calls=%fused_computation.8.clone.1 | loop fusion | flops 4585728 | bytes 3815424 | tf_op jit(solution)/shard_map/while/body/eval_jaxpr/vmap()/reduce_sum | solution.py:41
  140.2 2.5 %fusion.91 = (f32[2,7,128]{2,1,0:T(8,128)S(1)}, f32[512,2,128,7]{2,0,3,1:T(8,128)}) fusion(pred[2,128,512]{1,2,0:T(8,128)(4,1)S(1)} %broadcast_compare_fusion.4, bf16[2,128,7,128]{3,1,2,0:T(8,128)(2,1)S(1)} %get-tuple-element.674, bf16[512,256]{1,0:T(8,128)(2,1)S(1)} %bitcast.146), kind=kOutput, calls=%fused_computation.6.clone.1 | convolution fusion | flops 237631744 | bytes 4398080 | tf_op jit(solution)/shard_map/while/body/eval_jaxpr/vmap(tpd,ud->ptu)/dot_general | solution.py:33
  142.7 3.1 %fusion.92 = f32[2,7,128]{2,1,0:T(8,128)S(1)} fusion(f32[512,2,128,7]{2,0,3,1:T(8,128)} %get-tuple-element.597, f32[2,7,128]{2,1,0:T(8,128)S(1)} %select_maximum_fusion.4, pred[2,128,512]{1,2,0:T(8,128)(4,1)S(1)} %broadcast_compare_fusion.4), kind=kLoop, calls=%fused_computation.8.clone.1 | loop fusion | flops 4585728 | bytes 3815424 | tf_op jit(solution)/shard_map/while/body/eval_jaxpr/vmap()/reduce_sum | solution.py:41
  145.8 3.4 %fusion.94 = f32[2,7,128,128]{3,2,1,0:T(8,128)} fusion(f32[512,2,128,7]{2,0,3,1:T(8,128)S(1)} %copy-done.1, f32[2,7,128]{2,1,0:T(8,128)S(1)} %select_maximum_fusion.4, pred[2,128,512]{1,2,0:T(8,128)(4,1)S(1)} %broadcast_compare_fusion.4, f32[2,7,128,128]{3,2,1,0:T(8,128)} %get-tuple-element.660, f32[2,7,128]{2,1,0:T(8,128)S(1)} %get-tuple-element.599, ...), kind=kOutput, calls=%fused_computation.11.clone.1 | convolution fusion | flops 240156672 | bytes 5783553 | tf_op jit(solution)/shard_map/while/body/eval_jaxpr/vmap(ptu,ud->ptd)/dot_general | solution.py:42
  149.8 2.5 %fusion.91 = (f32[2,7,128]{2,1,0:T(8,128)S(1)}, f32[512,2,128,7]{2,0,3,1:T(8,128)}) fusion(pred[2,128,512]{1,2,0:T(8,128)(4,1)S(1)} %broadcast_compare_fusion.4, bf16[2,128,7,128]{3,1,2,0:T(8,128)(2,1)S(1)} %get-tuple-element.674, bf16[512,256]{1,0:T(8,128)(2,1)S(1)} %bitcast.146), kind=kOutput, calls=%fused_computation.6.clone.1 | convolution fusion | flops 237631744 | bytes 4398080 | tf_op jit(solution)/shard_map/while/body/eval_jaxpr/vmap(tpd,ud->ptu)/dot_general | solution.py:33
  152.3 3.1 %fusion.92 = f32[2,7,128]{2,1,0:T(8,128)S(1)} fusion(f32[512,2,128,7]{2,0,3,1:T(8,128)} %get-tuple-element.597, f32[2,7,128]{2,1,0:T(8,128)S(1)} %select_maximum_fusion.4, pred[2,128,512]{1,2,0:T(8,128)(4,1)S(1)} %broadcast_compare_fusion.4), kind=kLoop, calls=%fused_computation.8.clone.1 | loop fusion | flops 4585728 | bytes 3815424 | tf_op jit(solution)/shard_map/while/body/eval_jaxpr/vmap()/reduce_sum | solution.py:41
  155.4 3.4 %fusion.94 = f32[2,7,128,128]{3,2,1,0:T(8,128)} fusion(f32[512,2,128,7]{2,0,3,1:T(8,128)S(1)} %copy-done.1, f32[2,7,128]{2,1,0:T(8,128)S(1)} %select_maximum_fusion.4, pred[2,128,512]{1,2,0:T(8,128)(4,1)S(1)} %broadcast_compare_fusion.4, f32[2,7,128,128]{3,2,1,0:T(8,128)} %get-tuple-element.660, f32[2,7,128]{2,1,0:T(8,128)S(1)} %get-tuple-element.599, ...), kind=kOutput, calls=%fused_computation.11.clone.1 | convolution fusion | flops 240156672 | bytes 5783553 | tf_op jit(solution)/shard_map/while/body/eval_jaxpr/vmap(ptu,ud->ptd)/dot_general | solution.py:42
  161.8 3.1 %fusion.92 = f32[2,7,128]{2,1,0:T(8,128)S(1)} fusion(f32[512,2,128,7]{2,0,3,1:T(8,128)} %get-tuple-element.597, f32[2,7,128]{2,1,0:T(8,128)S(1)} %select_maximum_fusion.4, pred[2,128,512]{1,2,0:T(8,128)(4,1)S(1)} %broadcast_compare_fusion.4), kind=kLoop, calls=%fused_computation.8.clone.1 | loop fusion | flops 4585728 | bytes 3815424 | tf_op jit(solution)/shard_map/while/body/eval_jaxpr/vmap()/reduce_sum | solution.py:41
  165.0 3.4 %fusion.94 = f32[2,7,128,128]{3,2,1,0:T(8,128)} fusion(f32[512,2,128,7]{2,0,3,1:T(8,128)S(1)} %copy-done.1, f32[2,7,128]{2,1,0:T(8,128)S(1)} %select_maximum_fusion.4, pred[2,128,512]{1,2,0:T(8,128)(4,1)S(1)} %broadcast_compare_fusion.4, f32[2,7,128,128]{3,2,1,0:T(8,128)} %get-tuple-element.660, f32[2,7,128]{2,1,0:T(8,128)S(1)} %get-tuple-element.599, ...), kind=kOutput, calls=%fused_computation.11.clone.1 | convolution fusion | flops 240156672 | bytes 5783553 | tf_op jit(solution)/shard_map/while/body/eval_jaxpr/vmap(ptu,ud->ptd)/dot_general | solution.py:42
  168.4 34.3 %while.37 = (s32[]{:T(128)}, f32[2,7,128]{2,1,0:T(8,128)S(1)}, f32[2,7,128]{2,1,0:T(8,128)S(1)}, f32[2,7,128,128]{3,2,1,0:T(8,128)}, s32[4,4,2]{2,0,1:T(4,128)S(...) while((s32[]{:T(128)}, f32[2,7,128]{2,1,0:T(8,128)S(1)}, ...), condition=%wide.region_8.9_spmd.clone, body=%wide.region_5.8_spmd.clone.sunk | while | flops 482518016 | bytes 36762500 | solution.py:188
  171.4 3.1 %fusion.98 = f32[2,7,128]{2,1,0:T(8,128)S(1)} fusion(f32[512,2,128,7]{2,0,3,1:T(8,128)} %get-tuple-element.610, f32[2,7,128]{2,1,0:T(8,128)S(1)} %select_maximum_fusion.5, pred[2,128,512]{1,2,0:T(8,128)(4,1)S(1)} %broadcast_compare_fusion.5), kind=kLoop, calls=%fused_computation.31.clone.1 | loop fusion | flops 4585728 | bytes 3815424 | tf_op jit(solution)/shard_map/while/body/eval_jaxpr/vmap()/reduce_sum | solution.py:41
  180.0 3.1 %fusion.98 = f32[2,7,128]{2,1,0:T(8,128)S(1)} fusion(f32[512,2,128,7]{2,0,3,1:T(8,128)} %get-tuple-element.610, f32[2,7,128]{2,1,0:T(8,128)S(1)} %select_maximum_fusion.5, pred[2,128,512]{1,2,0:T(8,128)(4,1)S(1)} %broadcast_compare_fusion.5), kind=kLoop, calls=%fused_computation.31.clone.1 | loop fusion | flops 4585728 | bytes 3815424 | tf_op jit(solution)/shard_map/while/body/eval_jaxpr/vmap()/reduce_sum | solution.py:41
  188.5 3.1 %fusion.98 = f32[2,7,128]{2,1,0:T(8,128)S(1)} fusion(f32[512,2,128,7]{2,0,3,1:T(8,128)} %get-tuple-element.610, f32[2,7,128]{2,1,0:T(8,128)S(1)} %select_maximum_fusion.5, pred[2,128,512]{1,2,0:T(8,128)(4,1)S(1)} %broadcast_compare_fusion.5), kind=kLoop, calls=%fused_computation.31.clone.1 | loop fusion | flops 4585728 | bytes 3815424 | tf_op jit(solution)/shard_map/while/body/eval_jaxpr/vmap()/reduce_sum | solution.py:41
  197.1 3.1 %fusion.98 = f32[2,7,128]{2,1,0:T(8,128)S(1)} fusion(f32[512,2,128,7]{2,0,3,1:T(8,128)} %get-tuple-element.610, f32[2,7,128]{2,1,0:T(8,128)S(1)} %select_maximum_fusion.5, pred[2,128,512]{1,2,0:T(8,128)(4,1)S(1)} %broadcast_compare_fusion.5), kind=kLoop, calls=%fused_computation.31.clone.1 | loop fusion | flops 4585728 | bytes 3815424 | tf_op jit(solution)/shard_map/while/body/eval_jaxpr/vmap()/reduce_sum | solution.py:41
  202.7 3.0 %fusion.44 = bf16[2,128,7,128]{3,1,2,0:T(8,128)(2,1)S(1)} fusion(f32[2,7,128,128]{3,2,1,0:T(8,128)} %get-tuple-element.290, f32[2,7,128,128]{3,2,1,0:T(8,128)} %get-tuple-element.288, f32[2,7,128]{2,1,0:T(8,128)S(1)} %get-tuple-element.455, f32[2,7,128]{2,1,0:T(8,128)S(1)} %get-tuple-element.457, f32[2,7,128]{2,1,0:T(8,128)S(1)} %get-tuple-element.456, ...), kind=kOutput, calls=%fused_computation.66 | convolution fusion | flops 31768576 | bytes 2835584 | tf_op jit(solution)/shard_map/vmap(ptu,ud->ptd)/dot_general | solution.py:42
  206.2 12.0 %collective-permute-start.18 = (bf16[2,64,896]{2,1,0:T(8,128)(2,1)S(1)}, bf16[2,64,896]{2,1,0:T(8,128)(2,1)S(1)}, u32[]{:S(2)}, u32[]{:S(2)}) collective-permute-start(bf16[2,64,896]{2,1,0:T(8,128)(2,1)S(1)} %squeeze.61), channel_id=1, source_target_pairs={{0,16},{16,0},{1,17},{17,1},{2,18},{18,2},{3,19},{19,3},{4,20},{20... | collective-permute-start | bytes 688136 | tf_op jit(solution)/shard_map/ppermute | solution.py:102
  (223 shorter events, 61.4 us)
Async XLA Ops:
  0.0 30.5 %copy-start = (s32[1,64]{1,0:T(1,128)S(1)}, s32[1,64]{1,0:T(1,128)}, u32[]{:S(2)}) copy-start(s32[1,64]{1,0:T(1,128)} %param.11) | copy-start | bytes 772
  0.9 31.7 %collective-permute-start.1 = (bf16[224,256]{1,0:T(8,128)(2,1)S(1)}, bf16[224,256]{1,0:T(8,128)(2,1)S(1)}, u32[]{:S(2)}, u32[]{:S(2)}) collective-permute-start(bf16[224,256]{1,0:T(8,128)(2,1)S(1)} %get-tuple-element.459), channel_id=1, source_target_pairs={{0,47},{1,0},{2,1},{3,2},{4,3},{5,4},{6,5},{7,6},{8,7},{9,8},{10,9... | collective-permute-start | bytes 344072 | tf_op jit(solution)/shard_map/ppermute | solution.py:135
  20.2 17.3 %collective-permute-start.8 = (bf16[224,256]{1,0:T(8,128)(2,1)S(1)}, bf16[224,256]{1,0:T(8,128)(2,1)S(1)}, u32[]{:S(2)}, u32[]{:S(2)}) collective-permute-start(bf16[224,256]{1,0:T(8,128)(2,1)S(1)} %get-tuple-element.459), channel_id=1, source_target_pairs={{0,1},{1,2},{2,3},{3,4},{4,5},{5,6},{6,7},{7,8},{8,9},{9,10},{10,1... | collective-permute-start | bytes 344072 | tf_op jit(solution)/shard_map/ppermute | solution.py:132
  22.1 64.6 %collective-permute-start = (bf16[2,64,3584]{2,1,0:T(8,128)(2,1)}, bf16[2,64,3584]{2,1,0:T(8,128)(2,1)}, u32[]{:S(2)}, u32[]{:S(2)}) collective-permute-start(bf16[2,64,3584]{2,1,0:T(8,128)(2,1)} %bitcast.157), channel_id=1, source_target_pairs={{0,16},{16,0},{1,17},{17,1},{2,18},{18,2},{3,19},{19,3},{4,20},{20... | collective-permute-start | bytes 2752520 | tf_op jit(solution)/shard_map/ppermute | solution.py:102
  28.0 71.1 %collective-permute-start.16 = (bf16[2,64,896]{2,1,0:T(8,128)(2,1)S(1)}, bf16[2,64,896]{2,1,0:T(8,128)(2,1)S(1)}, u32[]{:S(2)}, u32[]{:S(2)}) collective-permute-start(bf16[2,64,896]{2,1,0:T(8,128)(2,1)S(1)} %bitcast.152), channel_id=1, source_target_pairs={{0,16},{16,0},{1,17},{17,1},{2,18},{18,2},{3,19},{19,3},{4,20},{20... | collective-permute-start | bytes 688136 | tf_op jit(solution)/shard_map/ppermute | solution.py:102
  32.6 6.8 %collective-permute-start.2 = (bf16[224,256]{1,0:T(8,128)(2,1)S(1)}, bf16[224,256]{1,0:T(8,128)(2,1)S(1)}, u32[]{:S(2)}, u32[]{:S(2)}) collective-permute-start(bf16[224,256]{1,0:T(8,128)(2,1)S(1)} %collective-permute-done.1), channel_id=1, source_target_pairs={{0,47},{1,0},{2,1},{3,2},{4,3},{5,4},{6,5},{7,6},{8,7},{9,8},{10,9... | collective-permute-start | bytes 344072 | tf_op jit(solution)/shard_map/ppermute | solution.py:135
  37.5 7.3 %collective-permute-start.9 = (bf16[224,256]{1,0:T(8,128)(2,1)S(1)}, bf16[224,256]{1,0:T(8,128)(2,1)S(1)}, u32[]{:S(2)}, u32[]{:S(2)}) collective-permute-start(bf16[224,256]{1,0:T(8,128)(2,1)S(1)} %collective-permute-done.8), channel_id=1, source_target_pairs={{0,1},{1,2},{2,3},{3,4},{4,5},{5,6},{6,7},{7,8},{8,9},{9,10},{10,1... | collective-permute-start | bytes 344072 | tf_op jit(solution)/shard_map/ppermute | solution.py:132
  39.5 7.3 %collective-permute-start.3 = (bf16[224,256]{1,0:T(8,128)(2,1)S(1)}, bf16[224,256]{1,0:T(8,128)(2,1)S(1)}, u32[]{:S(2)}, u32[]{:S(2)}) collective-permute-start(bf16[224,256]{1,0:T(8,128)(2,1)S(1)} %collective-permute-done.2), channel_id=1, source_target_pairs={{0,47},{1,0},{2,1},{3,2},{4,3},{5,4},{6,5},{7,6},{8,7},{9,8},{10,9... | collective-permute-start | bytes 344072 | tf_op jit(solution)/shard_map/ppermute | solution.py:135
  44.8 6.7 %collective-permute-start.10 = (bf16[224,256]{1,0:T(8,128)(2,1)S(1)}, bf16[224,256]{1,0:T(8,128)(2,1)S(1)}, u32[]{:S(2)}, u32[]{:S(2)}) collective-permute-start(bf16[224,256]{1,0:T(8,128)(2,1)S(1)} %collective-permute-done.9), channel_id=1, source_target_pairs={{0,1},{1,2},{2,3},{3,4},{4,5},{5,6},{6,7},{7,8},{8,9},{9,10},{10,1... | collective-permute-start | bytes 344072 | tf_op jit(solution)/shard_map/ppermute | solution.py:132
  46.7 6.7 %collective-permute-start.4 = (bf16[224,256]{1,0:T(8,128)(2,1)S(1)}, bf16[224,256]{1,0:T(8,128)(2,1)S(1)}, u32[]{:S(2)}, u32[]{:S(2)}) collective-permute-start(bf16[224,256]{1,0:T(8,128)(2,1)S(1)} %collective-permute-done.3), channel_id=1, source_target_pairs={{0,47},{1,0},{2,1},{3,2},{4,3},{5,4},{6,5},{7,6},{8,7},{9,8},{10,9... | collective-permute-start | bytes 344072 | tf_op jit(solution)/shard_map/ppermute | solution.py:135
  51.5 6.7 %collective-permute-start.11 = (bf16[224,256]{1,0:T(8,128)(2,1)S(1)}, bf16[224,256]{1,0:T(8,128)(2,1)S(1)}, u32[]{:S(2)}, u32[]{:S(2)}) collective-permute-start(bf16[224,256]{1,0:T(8,128)(2,1)S(1)} %collective-permute-done.10), channel_id=1, source_target_pairs={{0,1},{1,2},{2,3},{3,4},{4,5},{5,6},{6,7},{7,8},{8,9},{9,10},{10,1... | collective-permute-start | bytes 344072 | tf_op jit(solution)/shard_map/ppermute | solution.py:132
  53.5 6.7 %collective-permute-start.5 = (bf16[224,256]{1,0:T(8,128)(2,1)S(1)}, bf16[224,256]{1,0:T(8,128)(2,1)S(1)}, u32[]{:S(2)}, u32[]{:S(2)}) collective-permute-start(bf16[224,256]{1,0:T(8,128)(2,1)S(1)} %collective-permute-done.4), channel_id=1, source_target_pairs={{0,47},{1,0},{2,1},{3,2},{4,3},{5,4},{6,5},{7,6},{8,7},{9,8},{10,9... | collective-permute-start | bytes 344072 | tf_op jit(solution)/shard_map/ppermute | solution.py:135
  58.3 6.7 %collective-permute-start.12 = (bf16[224,256]{1,0:T(8,128)(2,1)S(1)}, bf16[224,256]{1,0:T(8,128)(2,1)S(1)}, u32[]{:S(2)}, u32[]{:S(2)}) collective-permute-start(bf16[224,256]{1,0:T(8,128)(2,1)S(1)} %collective-permute-done.11), channel_id=1, source_target_pairs={{0,1},{1,2},{2,3},{3,4},{4,5},{5,6},{6,7},{7,8},{8,9},{9,10},{10,1... | collective-permute-start | bytes 344072 | tf_op jit(solution)/shard_map/ppermute | solution.py:132
  60.2 6.7 %collective-permute-start.6 = (bf16[224,256]{1,0:T(8,128)(2,1)S(1)}, bf16[224,256]{1,0:T(8,128)(2,1)S(1)}, u32[]{:S(2)}, u32[]{:S(2)}) collective-permute-start(bf16[224,256]{1,0:T(8,128)(2,1)S(1)} %collective-permute-done.5), channel_id=1, source_target_pairs={{0,47},{1,0},{2,1},{3,2},{4,3},{5,4},{6,5},{7,6},{8,7},{9,8},{10,9... | collective-permute-start | bytes 344072 | tf_op jit(solution)/shard_map/ppermute | solution.py:135
  65.0 6.7 %collective-permute-start.13 = (bf16[224,256]{1,0:T(8,128)(2,1)S(1)}, bf16[224,256]{1,0:T(8,128)(2,1)S(1)}, u32[]{:S(2)}, u32[]{:S(2)}) collective-permute-start(bf16[224,256]{1,0:T(8,128)(2,1)S(1)} %collective-permute-done.12), channel_id=1, source_target_pairs={{0,1},{1,2},{2,3},{3,4},{4,5},{5,6},{6,7},{7,8},{8,9},{9,10},{10,1... | collective-permute-start | bytes 344072 | tf_op jit(solution)/shard_map/ppermute | solution.py:132
  66.9 13.5 %collective-permute-start.7 = (bf16[224,256]{1,0:T(8,128)(2,1)S(1)}, bf16[224,256]{1,0:T(8,128)(2,1)S(1)}, u32[]{:S(2)}, u32[]{:S(2)}) collective-permute-start(bf16[224,256]{1,0:T(8,128)(2,1)S(1)} %collective-permute-done.6), channel_id=1, source_target_pairs={{0,47},{1,0},{2,1},{3,2},{4,3},{5,4},{6,5},{7,6},{8,7},{9,8},{10,9... | collective-permute-start | bytes 344072 | tf_op jit(solution)/shard_map/ppermute | solution.py:135
  71.7 6.8 %collective-permute-start.14 = (bf16[224,256]{1,0:T(8,128)(2,1)S(1)}, bf16[224,256]{1,0:T(8,128)(2,1)S(1)}, u32[]{:S(2)}, u32[]{:S(2)}) collective-permute-start(bf16[224,256]{1,0:T(8,128)(2,1)S(1)} %collective-permute-done.13), channel_id=1, source_target_pairs={{0,1},{1,2},{2,3},{3,4},{4,5},{5,6},{6,7},{7,8},{8,9},{9,10},{10,1... | collective-permute-start | bytes 344072 | tf_op jit(solution)/shard_map/ppermute | solution.py:132
  78.5 8.1 %collective-permute-start.15 = (bf16[224,256]{1,0:T(8,128)(2,1)S(1)}, bf16[224,256]{1,0:T(8,128)(2,1)S(1)}, u32[]{:S(2)}, u32[]{:S(2)}) collective-permute-start(bf16[224,256]{1,0:T(8,128)(2,1)S(1)} %collective-permute-done.14), channel_id=1, source_target_pairs={{0,1},{1,2},{2,3},{3,4},{4,5},{5,6},{6,7},{7,8},{8,9},{9,10},{10,1... | collective-permute-start | bytes 344072 | tf_op jit(solution)/shard_map/ppermute | solution.py:132
  92.0 39.3 %copy-start.3 = (s32[128]{0:T(128)S(1)}, s32[128]{0:T(128)}, u32[]{:S(2)}) copy-start(s32[128]{0:T(128)} %constant.209.clone.1) | copy-start | bytes 1540
  92.0 31.6 %all-to-all-start = ((bf16[16,2,64,256]{3,2,1,0:T(8,128)(2,1)}), bf16[16,2,64,256]{3,2,1,0:T(8,128)(2,1)S(1)}, u32[]{:S(2)}, u32[]{:S(2)}) async-start(bf16[16,2,64,256]{3,2,1,0:T(8,128)(2,1)} %broadcast_in_dim.162), calls=%async_computation | async-start | bytes 2097152 | tf_op jit(solution)/shard_map/all_to_all | solution.py:177
  99.5 24.0 %collective-permute-start.17 = (bf16[2,64,256]{2,1,0:T(8,128)(2,1)S(1)}, bf16[2,64,256]{2,1,0:T(8,128)(2,1)S(1)}, u32[]{:S(2)}, u32[]{:S(2)}) collective-permute-start(bf16[2,64,256]{2,1,0:T(8,128)(2,1)S(1)} %pad_maximum_fusion), channel_id=1, source_target_pairs={{0,32},{32,0},{1,33},{33,1},{2,34},{34,2},{3,35},{35,3},{4,36},{36... | collective-permute-start | bytes 196616 | tf_op jit(solution)/shard_map/ppermute | solution.py:102
  124.6 43.8 %all-to-all-start.1 = ((bf16[16,2,64,256]{3,2,1,0:T(8,128)(2,1)}), bf16[16,2,64,256]{3,2,1,0:T(8,128)(2,1)S(1)}, u32[]{:S(2)}, u32[]{:S(2)}) async-start(bf16[16,2,64,256]{3,2,1,0:T(8,128)(2,1)} %broadcast_in_dim.163), calls=%async_computation.1 | async-start | bytes 2097152 | tf_op jit(solution)/shard_map/all_to_all | solution.py:177
  134.3 3.1 %copy-start.1 = (f32[512,2,128,7]{2,0,3,1:T(8,128)S(1)}, f32[512,2,128,7]{2,0,3,1:T(8,128)}, u32[]{:S(2)}) copy-start(f32[512,2,128,7]{2,0,3,1:T(8,128)} %get-tuple-element.597) | copy-start | bytes 11010052 | tf_op jit(solution)/shard_map/while
  168.9 5.6 %copy-start.5 = (f32[2,7,128,128]{3,2,1,0:T(8,128)S(1)}, f32[2,7,128,128]{3,2,1,0:T(8,128)}, u32[]{:S(2)}) copy-start(f32[2,7,128,128]{3,2,1,0:T(8,128)} %get-tuple-element.627) | copy-start | bytes 2752516 | tf_op jit(solution)/shard_map/while
  171.4 3.1 %copy-start.2 = (f32[512,2,128,7]{2,0,3,1:T(8,128)S(1)}, f32[512,2,128,7]{2,0,3,1:T(8,128)}, u32[]{:S(2)}) copy-start(f32[512,2,128,7]{2,0,3,1:T(8,128)} %get-tuple-element.610) | copy-start | bytes 11010052 | tf_op jit(solution)/shard_map/while
  177.5 5.6 %copy-start.5 = (f32[2,7,128,128]{3,2,1,0:T(8,128)S(1)}, f32[2,7,128,128]{3,2,1,0:T(8,128)}, u32[]{:S(2)}) copy-start(f32[2,7,128,128]{3,2,1,0:T(8,128)} %get-tuple-element.627) | copy-start | bytes 2752516 | tf_op jit(solution)/shard_map/while
  180.0 3.1 %copy-start.2 = (f32[512,2,128,7]{2,0,3,1:T(8,128)S(1)}, f32[512,2,128,7]{2,0,3,1:T(8,128)}, u32[]{:S(2)}) copy-start(f32[512,2,128,7]{2,0,3,1:T(8,128)} %get-tuple-element.610) | copy-start | bytes 11010052 | tf_op jit(solution)/shard_map/while
  186.0 5.6 %copy-start.5 = (f32[2,7,128,128]{3,2,1,0:T(8,128)S(1)}, f32[2,7,128,128]{3,2,1,0:T(8,128)}, u32[]{:S(2)}) copy-start(f32[2,7,128,128]{3,2,1,0:T(8,128)} %get-tuple-element.627) | copy-start | bytes 2752516 | tf_op jit(solution)/shard_map/while
  188.5 3.1 %copy-start.2 = (f32[512,2,128,7]{2,0,3,1:T(8,128)S(1)}, f32[512,2,128,7]{2,0,3,1:T(8,128)}, u32[]{:S(2)}) copy-start(f32[512,2,128,7]{2,0,3,1:T(8,128)} %get-tuple-element.610) | copy-start | bytes 11010052 | tf_op jit(solution)/shard_map/while
  194.6 5.6 %copy-start.5 = (f32[2,7,128,128]{3,2,1,0:T(8,128)S(1)}, f32[2,7,128,128]{3,2,1,0:T(8,128)}, u32[]{:S(2)}) copy-start(f32[2,7,128,128]{3,2,1,0:T(8,128)} %get-tuple-element.627) | copy-start | bytes 2752516 | tf_op jit(solution)/shard_map/while
  197.1 3.1 %copy-start.2 = (f32[512,2,128,7]{2,0,3,1:T(8,128)S(1)}, f32[512,2,128,7]{2,0,3,1:T(8,128)}, u32[]{:S(2)}) copy-start(f32[512,2,128,7]{2,0,3,1:T(8,128)} %get-tuple-element.610) | copy-start | bytes 11010052 | tf_op jit(solution)/shard_map/while
  206.2 13.1 %collective-permute-start.18 = (bf16[2,64,896]{2,1,0:T(8,128)(2,1)S(1)}, bf16[2,64,896]{2,1,0:T(8,128)(2,1)S(1)}, u32[]{:S(2)}, u32[]{:S(2)}) collective-permute-start(bf16[2,64,896]{2,1,0:T(8,128)(2,1)S(1)} %squeeze.61), channel_id=1, source_target_pairs={{0,16},{16,0},{1,17},{17,1},{2,18},{18,2},{3,19},{19,3},{4,20},{20... | collective-permute-start | bytes 688136 | tf_op jit(solution)/shard_map/ppermute | solution.py:102
  (8 other events, 14.0 us)
